TPU v7x, 128 devices: a whole 4x4x4 slice. The times are simulated.
128 devices in a mesh: row: 8 (over x, core), col: 16 (over y, z).
Axes of the slice: x: 4, y: 4, z: 4, core: 2. Of those that a mesh axis runs over, the one named last changes fastest.
Arguments:
- kernel: float32 [16384, 16384], P('row', 'col'), as said below
Outputs:
- schur: float32 [16384, 16384], P('row', 'col')
- panels: float32 [16384, 768], P('row')
Inputs may be any that keep to these rules, and one draw needn't show every extreme that they name: kernel is symmetric and positive definite with smallest eigenvalue of order one.
All inputs are finite; a program needn't handle non-finite values.
Results may differ from a plain program's by a relative error of at most 0.00027.
Values sent between devices are 32-bit elements; how exact they have to be, the bound alone decides.
No kernel may reach another device: no remote copies, remote signals or barrier semaphores. Data moves between devices by JAX's collectives and lax.ppermute only.
A program may use at most 128 MiB of HBM per device.

v0:
```python
import jax
import jax.numpy as jnp
from jax import lax
from jax.sharding import PartitionSpec as P

BLOCK = 256
STEPS = 3


def gather_corner(kernel, row_index, col_index):
    row_count = lax.axis_size("row")
    col_count = lax.axis_size("col")
    piece = kernel[:BLOCK, :BLOCK]
    heard = [piece]
    for shift in range(1, col_count):
        pairs = [
            (a * col_count + b, a * col_count + (b + shift) % col_count)
            for a in range(STEPS)
            for b in range(STEPS)
        ]
        heard.append(lax.ppermute(piece, ("row", "col"), pairs))
    heard = jnp.stack(heard)
    band = jnp.concatenate(
        [heard[(col_index - b) % col_count] for b in range(STEPS)], axis=1
    )
    heard = [band]
    for shift in range(1, row_count):
        pairs = [
            (a * col_count + q, ((a + shift) % row_count) * col_count + q)
            for a in range(STEPS)
            for q in range(col_count)
        ]
        heard.append(lax.ppermute(band, ("row", "col"), pairs))
    heard = jnp.stack(heard)
    return jnp.concatenate(
        [heard[(row_index - a) % row_count] for a in range(STEPS)], axis=0
    )


def gather_columns(kernel, col_index):
    rows = kernel.shape[0]
    mine = col_index < STEPS
    piece = jnp.where(mine, kernel[:, :BLOCK], jnp.float32(0.0))
    band = jnp.zeros((rows, STEPS * BLOCK), jnp.float32)
    band = lax.dynamic_update_slice(band, piece, (0, jnp.minimum(col_index, STEPS - 1) * BLOCK))
    return lax.psum(band, "col")


def gather_rows(kernel, row_index):
    cols = kernel.shape[1]
    mine = row_index < STEPS
    piece = jnp.where(mine, kernel[:BLOCK, :], jnp.float32(0.0))
    band = jnp.zeros((STEPS * BLOCK, cols), jnp.float32)
    band = lax.dynamic_update_slice(band, piece, (jnp.minimum(row_index, STEPS - 1) * BLOCK, 0))
    return lax.psum(band, "row")


def shards(kernel):
    row_count = lax.axis_size("row")
    col_count = lax.axis_size("col")
    row_index = lax.axis_index("row")
    col_index = lax.axis_index("col")
    rows_local, cols_local = kernel.shape
    width = STEPS * BLOCK
    row_ids = jnp.arange(rows_local) // BLOCK * row_count + row_index
    col_ids = jnp.arange(cols_local) // BLOCK * col_count + col_index

    corner = gather_corner(kernel, row_index, col_index)
    band_cols = gather_columns(kernel, col_index)
    band_rows = gather_rows(kernel, row_index)

    factor = jnp.linalg.cholesky(corner)
    inverse = jax.scipy.linalg.solve_triangular(factor, jnp.eye(width, dtype=jnp.float32), lower=True)
    panels = lax.dot_general(
        band_cols, inverse, (((1,), (1,)), ((), ())),
        precision=lax.Precision.HIGHEST, preferred_element_type=jnp.float32,
    )
    across = lax.dot_general(
        band_rows, inverse, (((0,), (1,)), ((), ())),
        precision=lax.Precision.HIGHEST, preferred_element_type=jnp.float32,
    )
    own = lax.dynamic_slice_in_dim(factor, jnp.minimum(row_index, STEPS - 1) * BLOCK, BLOCK, 0)
    head = jnp.where(row_index < STEPS, own, panels[:BLOCK])
    panels = lax.dynamic_update_slice(panels, head, (0, 0))
    update = lax.dot_general(
        panels, across, (((1,), (1,)), ((), ())),
        precision=lax.Precision.HIGHEST, preferred_element_type=jnp.float32,
    )
    keep = (row_ids >= STEPS)[:, None] & (col_ids >= STEPS)[None, :]
    schur = jnp.where(keep, kernel - update, jnp.float32(0.0))
    return (schur, panels)


def solution(mesh):
    return jax.shard_map(
        shards,
        mesh=mesh,
        in_specs=(P("row", "col"),),
        out_specs=(P("row", "col"), P("row", None)),
        check_vma=False,
    )
```

profile of v0, /device:TPU:5, one launch (start us, length us, event | category | flops | bytes accessed | tf_op | source)
XLA Modules:
  0.0 466.4 jit_solution(11650589574560609366)
XLA Ops:
  8.2 1.4 collective-permute-start
  9.6 1.4 collective-permute-start.1
  10.9 1.3 collective-permute-start.2
  12.3 1.4 collective-permute-start.3
  13.6 1.4 collective-permute-start.4
  15.4 1.3 select_dynamic-update-slice_fusion.1
  16.7 1.7 copy-done
  18.4 1.7 bitcast_dynamic-update-slice_fusion.24
  20.8 1.7 bitcast_dynamic-update-slice_fusion.23
  23.1 1.7 bitcast_dynamic-update-slice_fusion.22
  25.5 1.7 bitcast_dynamic-update-slice_fusion.21
  27.8 1.7 bitcast_dynamic-update-slice_fusion.20
  30.2 1.8 bitcast_dynamic-update-slice_fusion.19
  44.5 3.1 broadcast_in_dim.22
  47.6 3.0 select_dynamic-update-slice_fusion
  51.5 1.5 fusion.22
  53.1 1.3 collective-permute-start.17
  55.4 1.3 collective-permute-start.18
  56.7 1.3 collective-permute-start.19
  59.6 41.0 %collective-permute-done.17 = f32[256,768]{1,0:T(8,128)S(1)} collective-permute-done((f32[256,768]{1,0:T(8,128)S(1)}, f32[256,768]{1,0:T(8,128)S(1)}, u32[]{:S(2)}, u32[]{:S(2)}) %collective-permute-start.17) | collective-permute-done | bytes 786464 | tf_op jit(solution)/shard_map/ppermute | solution.py:33
  100.7 46.0 %collective-permute-done.18 = f32[256,768]{1,0:T(8,128)S(1)} collective-permute-done((f32[256,768]{1,0:T(8,128)S(1)}, f32[256,768]{1,0:T(8,128)S(1)}, u32[]{:S(2)}, u32[]{:S(2)}) %collective-permute-start.18) | collective-permute-done | bytes 786464 | tf_op jit(solution)/shard_map/ppermute | solution.py:33
  146.8 5.1 %collective-permute-done.19 = f32[256,768]{1,0:T(8,128)S(1)} collective-permute-done((f32[256,768]{1,0:T(8,128)S(1)}, f32[256,768]{1,0:T(8,128)S(1)}, u32[]{:S(2)}, u32[]{:S(2)}) %collective-permute-start.19) | collective-permute-done | bytes 786464 | tf_op jit(solution)/shard_map/ppermute | solution.py:33
  154.0 1.6 pad_maximum_fusion
  155.6 2.6 copy.7
  158.2 1.7 fusion
  159.9 1.5 copy-done.5
  161.4 11.7 %cholesky.165 = f32[128,128]{1,0:T(8,128)S(1)} custom-call(f32[128,128]{1,0:T(8,128)S(1)} %cholesky.424), custom_call_target="Cholesky" | custom-call | tf_op jit(solution)/shard_map/jit(cholesky)/cholesky | solution.py:72
  173.3 9.8 %custom-call.47 = f32[1,128,128]{1,2,0:T(8,128)S(1)} custom-call(f32[1,128,128]{2,1,0:T(8,128)S(1)} %get-tuple-element.53), custom_call_target="InvertDiagBlocksLowerTriangular" | custom-call | tf_op jit(solution)/shard_map/jit(cholesky)/cholesky | solution.py:72
  183.1 1.4 constant_dynamic-update-slice_fusion.10
  184.5 1.4 convolution_subtract_fusion.4
  185.9 11.7 %cholesky.188 = f32[128,128]{1,0:T(8,128)S(1)} custom-call(f32[128,128]{1,0:T(8,128)S(1)} %cholesky.428), custom_call_target="Cholesky" | custom-call | tf_op jit(solution)/shard_map/jit(cholesky)/cholesky | solution.py:72
  197.7 10.0 %custom-call.48 = f32[1,128,128]{1,2,0:T(8,128)S(1)} custom-call(f32[1,128,128]{2,1,0:T(8,128)S(1)} %get-tuple-element.50), custom_call_target="InvertDiagBlocksLowerTriangular" | custom-call | tf_op jit(solution)/shard_map/jit(cholesky)/cholesky | solution.py:72
  208.0 1.5 convolution_subtract_fusion.5
  209.6 11.7 %cholesky.354 = f32[128,128]{1,0:T(8,128)S(1)} custom-call(f32[128,128]{1,0:T(8,128)S(1)} %cholesky.433), custom_call_target="Cholesky" | custom-call | tf_op jit(solution)/shard_map/jit(cholesky)/cholesky | solution.py:72
  222.0 9.8 %custom-call.49 = f32[1,128,128]{1,2,0:T(8,128)S(1)} custom-call(f32[1,128,128]{2,1,0:T(8,128)S(1)} %get-tuple-element.47), custom_call_target="InvertDiagBlocksLowerTriangular" | custom-call | tf_op jit(solution)/shard_map/jit(cholesky)/cholesky | solution.py:72
  232.2 1.6 convolution_subtract_fusion.6
  233.7 12.1 %cholesky.373 = f32[128,128]{1,0:T(8,128)S(1)} custom-call(f32[128,128]{1,0:T(8,128)S(1)} %cholesky.438), custom_call_target="Cholesky" | custom-call | tf_op jit(solution)/shard_map/jit(cholesky)/cholesky | solution.py:72
  245.9 9.8 %custom-call.50 = f32[1,128,128]{1,2,0:T(8,128)S(1)} custom-call(f32[1,128,128]{2,1,0:T(8,128)S(1)} %get-tuple-element.44), custom_call_target="InvertDiagBlocksLowerTriangular" | custom-call | tf_op jit(solution)/shard_map/jit(cholesky)/cholesky | solution.py:72
  256.0 1.5 convolution_subtract_fusion.7
  257.5 11.7 %cholesky.392 = f32[128,128]{1,0:T(8,128)S(1)} custom-call(f32[128,128]{1,0:T(8,128)S(1)} %cholesky.443), custom_call_target="Cholesky" | custom-call | tf_op jit(solution)/shard_map/jit(cholesky)/cholesky | solution.py:72
  269.2 9.8 %custom-call.51 = f32[1,128,128]{1,2,0:T(8,128)S(1)} custom-call(f32[1,128,128]{2,1,0:T(8,128)S(1)} %get-tuple-element.41), custom_call_target="InvertDiagBlocksLowerTriangular" | custom-call | tf_op jit(solution)/shard_map/jit(cholesky)/cholesky | solution.py:72
  279.2 1.3 convolution_subtract_fusion.8
  280.6 11.9 %cholesky.410 = f32[128,128]{1,0:T(8,128)S(1)} custom-call(f32[128,128]{1,0:T(8,128)S(1)} %convolution_subtract_fusion.8), custom_call_target="Cholesky" | custom-call | tf_op jit(solution)/shard_map/jit(cholesky)/cholesky | solution.py:72
  299.2 2.4 fusion.1
  301.6 18.1 %while.1 = (s32[]{:T(128)}, f32[768,768]{1,0:T(8,128)}, s32[6,2]{0,1:T(2,128)S(1)}, f32[6,128,128]{2,1,0:T(8,128)S(1)}, s32[]{:T(128)}) while((s32[]{:T(128)}, f32[768,768]{1,0:T(8,128)}, s32[6,2]{0,1:T(2,128)S(1)}, f32[6,128,128]{2,1,0:T(8,128)S(1)}, s32[]{:T(128)}) %tuple.49), condition=%wide.while_cond, body=%wide.while_body.sunk | while | flops 2 | bytes 131181 | solution.py:73
  302.3 2.4 bitcast_dynamic-update-slice_fusion.26
  305.4 2.3 bitcast_dynamic-update-slice_fusion.26
  308.4 2.3 bitcast_dynamic-update-slice_fusion.26
  311.4 2.3 bitcast_dynamic-update-slice_fusion.26
  314.4 2.3 bitcast_dynamic-update-slice_fusion.26
  317.4 2.3 bitcast_dynamic-update-slice_fusion.26
  319.7 59.0 %custom-call.52 = f32[6,128,128]{1,2,0:T(8,128)S(1)} custom-call(f32[6,128,128]{2,1,0:T(8,128)S(1)} %get-tuple-element.9), custom_call_target="InvertDiagBlocksLowerTriangular" | custom-call | tf_op jit(solution)/shard_map/jit(_solve_triangular)/triangular_solve | solution.py:73
  378.7 1.9 constant_dynamic-update-slice_fusion.4
  380.6 1.5 convolution_subtract_fusion.2
  382.1 1.3 constant_dynamic-update-slice_fusion.3
  383.4 1.5 convolution_subtract_fusion.3
  386.2 1.8 convolution_subtract_fusion.1
  388.0 1.3 constant_dynamic-update-slice_fusion.1
  389.3 2.0 fusion.10
  392.5 2.3 convolution_subtract_fusion
  396.1 17.6 %fusion.70 = f32[1024,768]{1,0:T(8,128)S(1)} fusion(f32[768,1024]{1,0:T(8,128)} %all-reduce.6.cloned.1.call-done, f32[768,768]{1,0:T(8,128)} %convolution_dynamic-update-slice_fusion), kind=kOutput, calls=%fused_computation.174 | convolution fusion | flops 7247757312 | bytes 8650752 | tf_op jit(solution)/shard_map/dot_general | solution.py:78
  413.7 19.0 %fusion.69 = f32[2048,768]{1,0:T(8,128)S(1)} fusion(f32[2048,768]{1,0:T(8,128)} %all-reduce.4.cloned.1.call-done, f32[768,768]{1,0:T(8,128)} %convolution_dynamic-update-slice_fusion), kind=kOutput, calls=%fused_computation.173 | convolution fusion | flops 14495514624 | bytes 14942208 | tf_op jit(solution)/shard_map/dot_general | solution.py:74
  432.7 1.3 fusion.18
  434.0 25.4 %subtract_select_fusion = f32[2048,1024]{1,0:T(8,128)} fusion(f32[2048,1024]{1,0:T(8,128)} %param.1, pred[1024]{0:T(1024)(128)(4,1)S(1)} %fusion.61, pred[2048]{0:T(1024)(128)(4,1)S(1)} %fusion.55, f32[2048,768]{1,0:T(8,128)S(1)} %fusion.18, f32[1024,768]{1,0:T(8,128)S(1)} %fusion.70), kind=kOutput, calls=%fused_computation.2 | convolution fusion | flops 19333644288 | bytes 26217472 | tf_op jit(solution)/shard_map/dot_general | solution.py:85
  (117 shorter events, 35.7 us)
Async XLA Ops:
  7.2 388.9 %all-reduce.6.cloned.1.call-start = ((), (), s32[]{:S(2)}) async-start(), calls=%async_computation.1 | async-start | bytes 6291456 | tf_op jit(solution)/shard_map/psum | solution.py:55
  8.2 11.9 %collective-permute-start = (f32[256,256]{1,0:T(8,128)S(1)}, f32[256,256]{1,0:T(8,128)}, u32[]{:S(2)}, u32[]{:S(2)}) collective-permute-start(f32[256,256]{1,0:T(8,128)S(1)} %slice.193), channel_id=1, source_target_pairs={{0,1},{1,2},{2,3},{16,17},{17,18},{18,19},{32,33},{33,34},{34,35}} | collective-permute-start | bytes 786440 | tf_op jit(solution)/shard_map/ppermute | solution.py:21
  9.6 12.9 %collective-permute-start.1 = (f32[256,256]{1,0:T(8,128)S(1)}, f32[256,256]{1,0:T(8,128)}, u32[]{:S(2)}, u32[]{:S(2)}) collective-permute-start(f32[256,256]{1,0:T(8,128)S(1)} %slice.193), channel_id=1, source_target_pairs={{0,2},{1,3},{2,4},{16,18},{17,19},{18,20},{32,34},{33,35},{34,36}} | collective-permute-start | bytes 786440 | tf_op jit(solution)/shard_map/ppermute | solution.py:21
  10.9 13.9 %collective-permute-start.2 = (f32[256,256]{1,0:T(8,128)S(1)}, f32[256,256]{1,0:T(8,128)}, u32[]{:S(2)}, u32[]{:S(2)}) collective-permute-start(f32[256,256]{1,0:T(8,128)S(1)} %slice.193), channel_id=1, source_target_pairs={{0,3},{1,4},{2,5},{16,19},{17,20},{18,21},{32,35},{33,36},{34,37}} | collective-permute-start | bytes 786440 | tf_op jit(solution)/shard_map/ppermute | solution.py:21
  12.3 14.9 %collective-permute-start.3 = (f32[256,256]{1,0:T(8,128)S(1)}, f32[256,256]{1,0:T(8,128)}, u32[]{:S(2)}, u32[]{:S(2)}) collective-permute-start(f32[256,256]{1,0:T(8,128)S(1)} %slice.193), channel_id=1, source_target_pairs={{0,4},{1,5},{2,6},{16,20},{17,21},{18,22},{32,36},{33,37},{34,38}} | collective-permute-start | bytes 786440 | tf_op jit(solution)/shard_map/ppermute | solution.py:21
  13.6 15.9 %collective-permute-start.4 = (f32[256,256]{1,0:T(8,128)S(1)}, f32[256,256]{1,0:T(8,128)}, u32[]{:S(2)}, u32[]{:S(2)}) collective-permute-start(f32[256,256]{1,0:T(8,128)S(1)} %slice.193), channel_id=1, source_target_pairs={{0,5},{1,6},{2,7},{16,21},{17,22},{18,23},{32,37},{33,38},{34,39}} | collective-permute-start | bytes 786440 | tf_op jit(solution)/shard_map/ppermute | solution.py:21
  16.7 1.7 copy-start
  18.4 395.3 %all-reduce.4.cloned.1.call-start = ((), (), s32[]{:S(2)}) async-start(), calls=%async_computation | async-start | bytes 12582912 | tf_op jit(solution)/shard_map/psum | solution.py:46
  20.1 11.8 %collective-permute-start.5 = (f32[256,256]{1,0:T(8,128)S(1)}, f32[256,256]{1,0:T(8,128)S(1)}, u32[]{:S(2)}, u32[]{:S(2)}) collective-permute-start(f32[256,256]{1,0:T(8,128)S(1)} %slice.193), channel_id=1, source_target_pairs={{0,6},{1,7},{2,8},{16,22},{17,23},{18,24},{32,38},{33,39},{34,40}} | collective-permute-start | bytes 786440 | tf_op jit(solution)/shard_map/ppermute | solution.py:21
  22.4 10.9 %collective-permute-start.6 = (f32[256,256]{1,0:T(8,128)S(1)}, f32[256,256]{1,0:T(8,128)S(1)}, u32[]{:S(2)}, u32[]{:S(2)}) collective-permute-start(f32[256,256]{1,0:T(8,128)S(1)} %slice.193), channel_id=1, source_target_pairs={{0,7},{1,8},{2,9},{16,23},{17,24},{18,25},{32,39},{33,40},{34,41}} | collective-permute-start | bytes 786440 | tf_op jit(solution)/shard_map/ppermute | solution.py:21
  24.8 9.9 %collective-permute-start.7 = (f32[256,256]{1,0:T(8,128)S(1)}, f32[256,256]{1,0:T(8,128)S(1)}, u32[]{:S(2)}, u32[]{:S(2)}) collective-permute-start(f32[256,256]{1,0:T(8,128)S(1)} %slice.193), channel_id=1, source_target_pairs={{0,8},{1,9},{2,10},{16,24},{17,25},{18,26},{32,40},{33,41},{34,42}} | collective-permute-start | bytes 786440 | tf_op jit(solution)/shard_map/ppermute | solution.py:21
  27.2 9.0 %collective-permute-start.8 = (f32[256,256]{1,0:T(8,128)S(1)}, f32[256,256]{1,0:T(8,128)S(1)}, u32[]{:S(2)}, u32[]{:S(2)}) collective-permute-start(f32[256,256]{1,0:T(8,128)S(1)} %slice.193), channel_id=1, source_target_pairs={{0,9},{1,10},{2,11},{16,25},{17,26},{18,27},{32,41},{33,42},{34,43}} | collective-permute-start | bytes 786440 | tf_op jit(solution)/shard_map/ppermute | solution.py:21
  29.5 8.0 %collective-permute-start.9 = (f32[256,256]{1,0:T(8,128)S(1)}, f32[256,256]{1,0:T(8,128)S(1)}, u32[]{:S(2)}, u32[]{:S(2)}) collective-permute-start(f32[256,256]{1,0:T(8,128)S(1)} %slice.193), channel_id=1, source_target_pairs={{0,10},{1,11},{2,12},{16,26},{17,27},{18,28},{32,42},{33,43},{34,44}} | collective-permute-start | bytes 786440 | tf_op jit(solution)/shard_map/ppermute | solution.py:21
  31.9 7.0 %collective-permute-start.10 = (f32[256,256]{1,0:T(8,128)S(1)}, f32[256,256]{1,0:T(8,128)S(1)}, u32[]{:S(2)}, u32[]{:S(2)}) collective-permute-start(f32[256,256]{1,0:T(8,128)S(1)} %slice.193), channel_id=1, source_target_pairs={{0,11},{1,12},{2,13},{16,27},{17,28},{18,29},{32,43},{33,44},{34,45}} | collective-permute-start | bytes 786440 | tf_op jit(solution)/shard_map/ppermute | solution.py:21
  33.3 6.3 %collective-permute-start.11 = (f32[256,256]{1,0:T(8,128)S(1)}, f32[256,256]{1,0:T(8,128)S(1)}, u32[]{:S(2)}, u32[]{:S(2)}) collective-permute-start(f32[256,256]{1,0:T(8,128)S(1)} %slice.193), channel_id=1, source_target_pairs={{0,12},{1,13},{2,14},{16,28},{17,29},{18,30},{32,44},{33,45},{34,46}} | collective-permute-start | bytes 786440 | tf_op jit(solution)/shard_map/ppermute | solution.py:21
  34.7 5.7 %collective-permute-start.12 = (f32[256,256]{1,0:T(8,128)S(1)}, f32[256,256]{1,0:T(8,128)S(1)}, u32[]{:S(2)}, u32[]{:S(2)}) collective-permute-start(f32[256,256]{1,0:T(8,128)S(1)} %slice.193), channel_id=1, source_target_pairs={{0,13},{1,14},{2,15},{16,29},{17,30},{18,31},{32,45},{33,46},{34,47}} | collective-permute-start | bytes 786440 | tf_op jit(solution)/shard_map/ppermute | solution.py:21
  36.1 5.0 %collective-permute-start.13 = (f32[256,256]{1,0:T(8,128)S(1)}, f32[256,256]{1,0:T(8,128)S(1)}, u32[]{:S(2)}, u32[]{:S(2)}) collective-permute-start(f32[256,256]{1,0:T(8,128)S(1)} %slice.193), channel_id=1, source_target_pairs={{0,14},{1,15},{2,0},{16,30},{17,31},{18,16},{32,46},{33,47},{34,32}} | collective-permute-start | bytes 786440 | tf_op jit(solution)/shard_map/ppermute | solution.py:21
  37.5 4.3 collective-permute-start.14
  43.8 14.2 %collective-permute-start.15 = (f32[256,768]{1,0:T(8,128)S(1)}, f32[256,768]{1,0:T(8,128)S(1)}, u32[]{:S(2)}, u32[]{:S(2)}) collective-permute-start(f32[256,768]{1,0:T(8,128)S(1)} %pad_maximum_fusion.1), channel_id=1, source_target_pairs={{0,16},{1,17},{2,18},{3,19},{4,20},{5,21},{6,22},{7,23},{8,24},{9,... | collective-permute-start | bytes 2359304 | tf_op jit(solution)/shard_map/ppermute | solution.py:33
  50.8 8.0 %collective-permute-start.16 = (f32[256,768]{1,0:T(8,128)S(1)}, f32[256,768]{1,0:T(8,128)S(1)}, u32[]{:S(2)}, u32[]{:S(2)}) collective-permute-start(f32[256,768]{1,0:T(8,128)S(1)} %pad_maximum_fusion.1), channel_id=1, source_target_pairs={{0,32},{1,33},{2,34},{3,35},{4,36},{5,37},{6,38},{7,39},{8,40},{9,... | collective-permute-start | bytes 2359304 | tf_op jit(solution)/shard_map/ppermute | solution.py:33
  53.1 47.6 %collective-permute-start.17 = (f32[256,768]{1,0:T(8,128)S(1)}, f32[256,768]{1,0:T(8,128)S(1)}, u32[]{:S(2)}, u32[]{:S(2)}) collective-permute-start(f32[256,768]{1,0:T(8,128)S(1)} %pad_maximum_fusion.1), channel_id=1, source_target_pairs={{0,48},{1,49},{2,50},{3,51},{4,52},{5,53},{6,54},{7,55},{8,56},{9,... | collective-permute-start | bytes 2359304 | tf_op jit(solution)/shard_map/ppermute | solution.py:33
  55.4 91.4 %collective-permute-start.18 = (f32[256,768]{1,0:T(8,128)S(1)}, f32[256,768]{1,0:T(8,128)S(1)}, u32[]{:S(2)}, u32[]{:S(2)}) collective-permute-start(f32[256,768]{1,0:T(8,128)S(1)} %pad_maximum_fusion.1), channel_id=1, source_target_pairs={{0,64},{1,65},{2,66},{3,67},{4,68},{5,69},{6,70},{7,71},{8,72},{9,... | collective-permute-start | bytes 2359304 | tf_op jit(solution)/shard_map/ppermute | solution.py:33
  56.7 95.3 %collective-permute-start.19 = (f32[256,768]{1,0:T(8,128)S(1)}, f32[256,768]{1,0:T(8,128)S(1)}, u32[]{:S(2)}, u32[]{:S(2)}) collective-permute-start(f32[256,768]{1,0:T(8,128)S(1)} %pad_maximum_fusion.1), channel_id=1, source_target_pairs={{0,80},{1,81},{2,82},{3,83},{4,84},{5,85},{6,86},{7,87},{8,88},{9,... | collective-permute-start | bytes 2359304 | tf_op jit(solution)/shard_map/ppermute | solution.py:33
  58.0 93.9 %collective-permute-start.20 = (f32[256,768]{1,0:T(8,128)S(1)}, f32[256,768]{1,0:T(8,128)S(1)}, u32[]{:S(2)}, u32[]{:S(2)}) collective-permute-start(f32[256,768]{1,0:T(8,128)S(1)} %pad_maximum_fusion.1), channel_id=1, source_target_pairs={{0,96},{1,97},{2,98},{3,99},{4,100},{5,101},{6,102},{7,103},{8,104... | collective-permute-start | bytes 2359304 | tf_op jit(solution)/shard_map/ppermute | solution.py:33
  58.8 93.2 %collective-permute-start.21 = (f32[256,768]{1,0:T(8,128)S(1)}, f32[256,768]{1,0:T(8,128)S(1)}, u32[]{:S(2)}, u32[]{:S(2)}) collective-permute-start(f32[256,768]{1,0:T(8,128)S(1)} %pad_maximum_fusion.1), channel_id=1, source_target_pairs={{0,112},{1,113},{2,114},{3,115},{4,116},{5,117},{6,118},{7,119},{8... | collective-permute-start | bytes 2359304 | tf_op jit(solution)/shard_map/ppermute | solution.py:33
  152.8 0.9 copy-start.2
  153.1 0.9 copy-start.3
  159.9 1.5 copy-start.5
  301.6 81.8 %copy-start.4 = (f32[768,768]{1,0:T(8,128)S(1)}, f32[768,768]{1,0:T(8,128)}, u32[]{:S(2)}) copy-start(f32[768,768]{1,0:T(8,128)} %fusion.22) | copy-start | bytes 7077892
  434.0 25.4 %copy-start.1 = (f32[2048,768]{1,0:T(8,128)}, f32[2048,768]{1,0:T(8,128)S(1)}, u32[]{:S(2)}) copy-start(f32[2048,768]{1,0:T(8,128)S(1)} %fusion.18) | copy-start | bytes 18874372
Sparse Core Ops, SparseCore 0:
  18.5 72.6 all-reduce.5
  95.2 156.6 all-reduce.3
where the time goes:
time: 473 us; the launch traced here: 466 us
  other arithmetic  197 us (42%)
  waiting for transfers between devices  92.3 us (20%)
  matrix products  89.1 us (19%)
  local copies, waits for them, and re-layouts  49 us (10%)
  starting transfers between devices  20.2 us (4%)
  between operations  18.8 us (4%)
    another operation x22, other arithmetic, shards(): factor = jnp.linalg.cholesky(corner)  124 us
    ppermute x7, waiting for transfers between devices, gather_corner(): heard.append(lax.ppermute(band, ('row', 'col'), pairs))  92.2 us
    another operation x3, other arithmetic, shards(): jax.scipy.linalg.solve_triangular(factor, jnp.eye(width, dtype=jnp.float3...  61.4 us
    dot_general x1, matrix products, shards(): lax.dot_general(panels, across, (((1,), (1,)), ((), ())), precision=lax.P...  25.4 us
    unnamed x33, local copies, waits for them, and re-layouts  21 us
    dot_general x1, matrix products, shards(): lax.dot_general(band_cols, inverse, (((1,), (1,)), ((), ())), precision=l...  19 us
    another operation x18, local copies, waits for them, and re-layouts  18 us
    dot_general x1, matrix products, shards(): lax.dot_general(band_rows, inverse, (((0,), (1,)), ((), ())), precision=l...  17.6 us
  transfers between devices with their start and end apart: 24, of which 3 were waited for; matrix products, arithmetic and copies ran while one was open for 61% of the time, Pallas kernels for 0%

commit v1 on v0

--- a/solution.py
+++ b/solution.py
@@ -55,6 +55,44 @@
     return lax.psum(band, "row")
 
 
+def mul(a, b, transpose_b=False):
+    dims = (((1,), (1 if transpose_b else 0,)), ((), ()))
+    return lax.dot_general(a, b, dims, precision=lax.Precision.HIGHEST, preferred_element_type=jnp.float32)
+
+
+def factor_corner(blocks):
+    eye = jnp.eye(BLOCK, dtype=jnp.float32)
+    zero = jnp.zeros((BLOCK, BLOCK), jnp.float32)
+    lower = [[None] * STEPS for _ in range(STEPS)]
+    diag_inv = []
+    for k in range(STEPS):
+        schur = blocks[k][k]
+        for j in range(k):
+            schur = schur - mul(lower[k][j], lower[k][j], True)
+        lower[k][k] = jnp.linalg.cholesky(schur)
+        diag_inv.append(jax.scipy.linalg.solve_triangular(lower[k][k], eye, lower=True))
+        for i in range(k + 1, STEPS):
+            below = blocks[i][k]
+            for j in range(k):
+                below = below - mul(lower[i][j], lower[k][j], True)
+            lower[i][k] = mul(below, diag_inv[k], True)
+    inv = [[None] * STEPS for _ in range(STEPS)]
+    for i in range(STEPS):
+        inv[i][i] = diag_inv[i]
+        for j in range(i - 1, -1, -1):
+            acc = mul(lower[i][j], inv[j][j])
+            for m in range(j + 1, i):
+                acc = acc + mul(lower[i][m], inv[m][j])
+            inv[i][j] = -mul(diag_inv[i], acc)
+    factor = jnp.concatenate(
+        [jnp.concatenate([lower[i][j] if j <= i else zero for j in range(STEPS)], axis=1) for i in range(STEPS)], axis=0
+    )
+    inverse = jnp.concatenate(
+        [jnp.concatenate([inv[i][j] if j <= i else zero for j in range(STEPS)], axis=1) for i in range(STEPS)], axis=0
+    )
+    return factor, inverse
+
+
 def shards(kernel):
     row_count = lax.axis_size("row")
     col_count = lax.axis_size("col")
@@ -69,22 +107,22 @@
     band_cols = gather_columns(kernel, col_index)
     band_rows = gather_rows(kernel, row_index)
 
-    factor = jnp.linalg.cholesky(corner)
-    inverse = jax.scipy.linalg.solve_triangular(factor, jnp.eye(width, dtype=jnp.float32), lower=True)
+    blocks = [[corner[a * BLOCK:(a + 1) * BLOCK, b * BLOCK:(b + 1) * BLOCK] for b in range(STEPS)] for a in range(STEPS)]
+    factor, inverse = factor_corner(blocks)
     panels = lax.dot_general(
         band_cols, inverse, (((1,), (1,)), ((), ())),
-        precision=lax.Precision.HIGHEST, preferred_element_type=jnp.float32,
+        precision=lax.Precision.HIGH, preferred_element_type=jnp.float32,
     )
     across = lax.dot_general(
         band_rows, inverse, (((0,), (1,)), ((), ())),
-        precision=lax.Precision.HIGHEST, preferred_element_type=jnp.float32,
+        precision=lax.Precision.HIGH, preferred_element_type=jnp.float32,
     )
     own = lax.dynamic_slice_in_dim(factor, jnp.minimum(row_index, STEPS - 1) * BLOCK, BLOCK, 0)
     head = jnp.where(row_index < STEPS, own, panels[:BLOCK])
     panels = lax.dynamic_update_slice(panels, head, (0, 0))
     update = lax.dot_general(
         panels, across, (((1,), (1,)), ((), ())),
-        precision=lax.Precision.HIGHEST, preferred_element_type=jnp.float32,
+        precision=lax.Precision.HIGH, preferred_element_type=jnp.float32,
     )
     keep = (row_ids >= STEPS)[:, None] & (col_ids >= STEPS)[None, :]
     schur = jnp.where(keep, kernel - update, jnp.float32(0.0))

time: 473 us -> 402 us (0.85)
  matrix products: 89.1 us -> 49.2 us
  other arithmetic: 197 us -> 172 us
  local copies, waits for them, and re-layouts: 49 us -> 42.8 us
    another operation x21 -> x15, matrix products: 27.2 us -> 4.27 us  [the longest x9 2.65 us: factor_corner(): jax.scipy.linalg.solve_triangular(lower[k][k], eye, lower=True)]
    another operation x25 -> x28, other arithmetic: 185 us -> 166 us  [the longest x20 104 us: factor_corner(): lower[k][k] = jnp.linalg.cholesky(schur)]
    dot_general x1, matrix products: 25.4 us -> 16.5 us  [shards(): lax.dot_general(panels, across, (((1,), (1,)), ((), ())), precision=lax.P...]
    dot_general x1, matrix products: 19 us -> 10.2 us  [shards(): lax.dot_general(band_cols, inverse, (((1,), (1,)), ((), ())), precision=l...]
    dot_general x0 -> x14, matrix products: none -> 7.12 us  [mul(): lax.dot_general(a, b, dims, precision=lax.Precision.HIGHEST, preferred_el...]
    dot_general x1, matrix products: 17.6 us -> 11.1 us  [shards(): lax.dot_general(band_rows, inverse, (((0,), (1,)), ((), ())), precision=l...]
    another operation x25 -> x33, local copies, waits for them, and re-layouts: 18.1 us -> 12.1 us  [the longest x22 11.8 us: factor_corner(): jax.scipy.linalg.solve_triangular(lower[k][k], eye, lower=True)]
  transfers between devices with their start and end apart: 24 -> 24, of which waited for: 3 -> 3; matrix products, arithmetic and copies ran while one was open for 61% -> 59% of each run, Pallas kernels for 0% -> 0%
where the time goes in v1:
time: 402 us; the launch traced here: 397 us
  other arithmetic  172 us (43%)
  waiting for transfers between devices  93.5 us (23%)
  matrix products  49.2 us (12%)
  local copies, waits for them, and re-layouts  42.8 us (11%)
  starting transfers between devices  20.4 us (5%)
  between operations  19 us (5%)
    another operation x20, other arithmetic, factor_corner(): lower[k][k] = jnp.linalg.cholesky(schur)  104 us
    ppermute x7, waiting for transfers between devices, gather_corner(): heard.append(lax.ppermute(band, ('row', 'col'), pairs))  93.4 us
    another operation x8, other arithmetic, factor_corner(): jax.scipy.linalg.solve_triangular(lower[k][k], eye, lower=True)  61.7 us
    unnamed x33, local copies, waits for them, and re-layouts  20.7 us
    dot_general x1, matrix products, shards(): lax.dot_general(panels, across, (((1,), (1,)), ((), ())), precision=lax.P...  16.5 us
    ppermute x15, starting transfers between devices, gather_corner(): heard.append(lax.ppermute(piece, ('row', 'col'), pairs))  13.5 us
    another operation x22, local copies, waits for them, and re-layouts, factor_corner(): jax.scipy.linalg.solve_triangular(lower[k][k], eye, lower=True)  11.8 us
    dot_general x1, matrix products, shards(): lax.dot_general(band_rows, inverse, (((0,), (1,)), ((), ())), precision=l...  11.1 us
  transfers between devices with their start and end apart: 24, of which 3 were waited for; matrix products, arithmetic and copies ran while one was open for 59% of the time, Pallas kernels for 0%

profile of v1, /device:TPU:5, one launch (start us, length us, event | category | flops | bytes accessed | tf_op | source)
XLA Modules:
  0.0 397.1 jit_solution(16110203762971616950)
XLA Ops:
  7.2 1.0 slice.64
  8.2 1.4 collective-permute-start
  9.6 1.4 collective-permute-start.1
  10.9 1.4 collective-permute-start.2
  12.3 1.4 collective-permute-start.3
  13.6 1.4 collective-permute-start.4
  15.4 1.3 select_dynamic-update-slice_fusion.1
  16.7 1.7 copy-done.1
  18.4 1.7 bitcast_dynamic-update-slice_fusion.26
  20.8 1.7 bitcast_dynamic-update-slice_fusion.25
  23.1 1.7 bitcast_dynamic-update-slice_fusion.24
  25.5 1.7 bitcast_dynamic-update-slice_fusion.23
  27.8 1.7 bitcast_dynamic-update-slice_fusion.22
  30.2 1.7 bitcast_dynamic-update-slice_fusion.21
  32.6 0.7 bitcast_dynamic-update-slice_fusion.20
  34.0 0.7 bitcast_dynamic-update-slice_fusion.19
  35.4 0.7 bitcast_dynamic-update-slice_fusion.18
  36.8 0.7 bitcast_dynamic-update-slice_fusion.17
  38.2 0.7 bitcast_dynamic-update-slice_fusion.16
  39.7 0.7 bitcast_dynamic-update-slice_fusion.14
  41.1 0.7 bitcast_dynamic-update-slice_fusion.12
  42.6 1.2 dynamic-slice_bitcast_fusion.2
  44.5 3.1 broadcast_in_dim.24
  47.6 3.1 select_dynamic-update-slice_fusion
  51.4 1.3 collective-permute-start.17
  52.8 1.3 collective-permute-start.18
  54.1 1.3 collective-permute-start.19
  56.3 0.9 collective-permute-start.21
  57.3 43.4 %collective-permute-done.17 = f32[256,768]{1,0:T(8,128)} collective-permute-done((f32[256,768]{1,0:T(8,128)S(1)}, f32[256,768]{1,0:T(8,128)}, u32[]{:S(2)}, u32[]{:S(2)}) %collective-permute-start.17) | collective-permute-done | bytes 786464 | tf_op jit(solution)/shard_map/ppermute | solution.py:33
  100.7 1.2 bitcast_dynamic-update-slice_fusion.7
  101.8 44.9 %collective-permute-done.18 = f32[256,768]{1,0:T(8,128)S(1)} collective-permute-done((f32[256,768]{1,0:T(8,128)S(1)}, f32[256,768]{1,0:T(8,128)S(1)}, u32[]{:S(2)}, u32[]{:S(2)}) %collective-permute-start.18) | collective-permute-done | bytes 786464 | tf_op jit(solution)/shard_map/ppermute | solution.py:33
  146.8 5.1 %collective-permute-done.19 = f32[256,768]{1,0:T(8,128)S(1)} collective-permute-done((f32[256,768]{1,0:T(8,128)S(1)}, f32[256,768]{1,0:T(8,128)S(1)}, u32[]{:S(2)}, u32[]{:S(2)}) %collective-permute-start.19) | collective-permute-done | bytes 786464 | tf_op jit(solution)/shard_map/ppermute | solution.py:33
  152.3 1.2 copy.17
  153.4 1.0 slice.88
  154.5 1.0 fusion.17
  155.6 11.7 %cholesky.172 = f32[128,128]{1,0:T(8,128)S(1)} custom-call(f32[128,128]{1,0:T(8,128)S(1)} %cholesky.270), custom_call_target="Cholesky" | custom-call | tf_op jit(solution)/shard_map/jit(cholesky)/cholesky | solution.py:72
  167.3 9.8 %custom-call.15 = f32[1,128,128]{1,2,0:T(8,128)S(1)} custom-call(f32[1,128,128]{2,1,0:T(8,128)S(1)} %get-tuple-element.80), custom_call_target="InvertDiagBlocksLowerTriangular" | custom-call | tf_op jit(solution)/shard_map/jit(cholesky)/cholesky | solution.py:72
  177.6 11.7 %cholesky.189 = f32[128,128]{1,0:T(8,128)S(1)} custom-call(f32[128,128]{1,0:T(8,128)S(1)} %convolution_subtract_fusion.9), custom_call_target="Cholesky" | custom-call | tf_op jit(solution)/shard_map/jit(cholesky)/cholesky | solution.py:72
  191.4 0.7 fusion.21
  192.2 4.0 while.6
  192.8 1.4 bitcast_dynamic-update-slice_fusion.30
  194.8 1.4 bitcast_dynamic-update-slice_fusion.30
  196.2 20.1 %custom-call.16 = f32[2,128,128]{1,2,0:T(8,128)S(1)} custom-call(f32[2,128,128]{2,1,0:T(8,128)S(1)} %get-tuple-element.24), custom_call_target="InvertDiagBlocksLowerTriangular" | custom-call | tf_op jit(solution)/shard_map/jit(_solve_triangular)/triangular_solve | solution.py:73
  218.7 11.7 %cholesky.206 = f32[128,128]{1,0:T(8,128)S(1)} custom-call(f32[128,128]{1,0:T(8,128)S(1)} %cholesky.273), custom_call_target="Cholesky" | custom-call | tf_op jit(solution)/shard_map/jit(cholesky)/cholesky | solution.py:72
  230.4 9.8 %custom-call.17 = f32[1,128,128]{1,2,0:T(8,128)S(1)} custom-call(f32[1,128,128]{2,1,0:T(8,128)S(1)} %get-tuple-element.76), custom_call_target="InvertDiagBlocksLowerTriangular" | custom-call | tf_op jit(solution)/shard_map/jit(cholesky)/cholesky | solution.py:72
  242.5 11.9 %cholesky.223 = f32[128,128]{1,0:T(8,128)S(1)} custom-call(f32[128,128]{1,0:T(8,128)S(1)} %convolution_subtract_fusion.8), custom_call_target="Cholesky" | custom-call | tf_op jit(solution)/shard_map/jit(cholesky)/cholesky | solution.py:72
  257.0 0.7 fusion.19
  257.8 4.0 %while.7 = (s32[]{:T(128)}, f32[256,256]{1,0:T(8,128)S(1)}, s32[2,2]{1,0:T(2,128)S(1)}, f32[2,128,128]{2,1,0:T(8,128)S(1)}, s32[]{:T(128)}) while((s32[]{:T(128)}, f32[256,256]{1,0:T(8,128)S(1)}, s32[2,2]{1,0:T(2,128)S(1)}, f32[2,128,128]{2,1,0:T(8,128)S(1)}, s32[]{:T(128)}) %tuple.82), condition=%wide.while_cond.clone, body=%wide.while_body.clone.sunk | while | flops 2 | bytes 131181 | solution.py:73
  258.4 1.4 bitcast_dynamic-update-slice_fusion.31
  260.5 1.4 bitcast_dynamic-update-slice_fusion.31
  261.8 19.7 %custom-call.18 = f32[2,128,128]{1,2,0:T(8,128)S(1)} custom-call(f32[2,128,128]{2,1,0:T(8,128)S(1)} %get-tuple-element.25), custom_call_target="InvertDiagBlocksLowerTriangular" | custom-call | tf_op jit(solution)/shard_map/jit(_solve_triangular)/triangular_solve | solution.py:73
  284.4 11.7 %cholesky.240 = f32[128,128]{1,0:T(8,128)S(1)} custom-call(f32[128,128]{1,0:T(8,128)S(1)} %cholesky.276), custom_call_target="Cholesky" | custom-call | tf_op jit(solution)/shard_map/jit(cholesky)/cholesky | solution.py:72
  296.1 9.8 %custom-call.19 = f32[1,128,128]{1,2,0:T(8,128)S(1)} custom-call(f32[1,128,128]{2,1,0:T(8,128)S(1)} %get-tuple-element.72), custom_call_target="InvertDiagBlocksLowerTriangular" | custom-call | tf_op jit(solution)/shard_map/jit(cholesky)/cholesky | solution.py:72
  306.7 12.1 %cholesky.257 = f32[128,128]{1,0:T(8,128)S(1)} custom-call(f32[128,128]{1,0:T(8,128)S(1)} %convolution_subtract_fusion.7), custom_call_target="Cholesky" | custom-call | tf_op jit(solution)/shard_map/jit(cholesky)/cholesky | solution.py:72
  321.4 0.7 fusion.18
  322.2 3.9 while.8
  322.8 1.3 bitcast_dynamic-update-slice_fusion.32
  324.8 1.3 bitcast_dynamic-update-slice_fusion.32
  326.1 19.7 %custom-call.20 = f32[2,128,128]{1,2,0:T(8,128)S(1)} custom-call(f32[2,128,128]{2,1,0:T(8,128)S(1)} %get-tuple-element.26), custom_call_target="InvertDiagBlocksLowerTriangular" | custom-call | tf_op jit(solution)/shard_map/jit(_solve_triangular)/triangular_solve | solution.py:73
  350.4 11.1 %fusion.31 = f32[1024,768]{1,0:T(8,128)} fusion(f32[768,1024]{1,0:T(8,128)} %all-reduce.8.cloned.1.call-done, f32[256,256]{1,0:T(8,128)S(1)} %cholesky.201, f32[256,256]{1,0:T(8,128)S(1)} %pad_maximum_fusion.2, f32[128,256]{1,0:T(8,128)S(1)} %fusion.36, f32[128,256]{1,0:T(8,128)S(1)} %fusion.25, f32[256,256]{1,0:T(8,128)S(1)} %convolution_negate_fusion, ...), kind=kOutput, calls=%fused_computation.102 | convolution fusion | flops 3629776896 | bytes 8126464 | tf_op jit(solution)/shard_map/dot_general | solution.py:116
  361.5 10.2 %fusion.33 = f32[2048,768]{1,0:T(8,128)S(1)} fusion(f32[2048,768]{1,0:T(8,128)} %all-reduce.6.cloned.1.call-done, f32[256,256]{1,0:T(8,128)S(1)} %cholesky.201, f32[256,256]{1,0:T(8,128)S(1)} %pad_maximum_fusion.2, f32[128,256]{1,0:T(8,128)S(1)} %fusion.36, f32[128,256]{1,0:T(8,128)S(1)} %fusion.25, f32[256,256]{1,0:T(8,128)S(1)} %convolution_negate_fusion, ...), kind=kOutput, calls=%fused_computation.103 | convolution fusion | flops 7253655552 | bytes 14417920 | tf_op jit(solution)/shard_map/dot_general | solution.py:112
  371.7 0.9 fusion.7
  372.6 1.0 copy-done.2
  373.6 16.5 %subtract_select_fusion = f32[2048,1024]{1,0:T(8,128)} fusion(f32[2048,1024]{1,0:T(8,128)} %param.4, pred[1024]{0:T(1024)(128)(4,1)S(1)} %fusion.58, pred[2048]{0:T(1024)(128)(4,1)S(1)} %fusion.52, f32[2048,768]{1,0:T(8,128)S(1)} %fusion.7, f32[1024,768]{1,0:T(8,128)S(1)} %copy-done.2), kind=kOutput, calls=%fused_computation.6 | convolution fusion | flops 9669967872 | bytes 26217472 | tf_op jit(solution)/shard_map/dot_general | solution.py:123
  (143 shorter events, 32.6 us)
Async XLA Ops:
  7.2 343.2 %all-reduce.8.cloned.1.call-start = ((), (), s32[]{:S(2)}) async-start(), calls=%async_computation.1 | async-start | bytes 6291456 | tf_op jit(solution)/shard_map/psum | solution.py:55
  8.2 11.9 %collective-permute-start = (f32[256,256]{1,0:T(8,128)S(1)}, f32[256,256]{1,0:T(8,128)}, u32[]{:S(2)}, u32[]{:S(2)}) collective-permute-start(f32[256,256]{1,0:T(8,128)S(1)} %slice.64), channel_id=1, source_target_pairs={{0,1},{1,2},{2,3},{16,17},{17,18},{18,19},{32,33},{33,34},{34,35}} | collective-permute-start | bytes 786440 | tf_op jit(solution)/shard_map/ppermute | solution.py:21
  9.6 12.9 %collective-permute-start.1 = (f32[256,256]{1,0:T(8,128)S(1)}, f32[256,256]{1,0:T(8,128)}, u32[]{:S(2)}, u32[]{:S(2)}) collective-permute-start(f32[256,256]{1,0:T(8,128)S(1)} %slice.64), channel_id=1, source_target_pairs={{0,2},{1,3},{2,4},{16,18},{17,19},{18,20},{32,34},{33,35},{34,36}} | collective-permute-start | bytes 786440 | tf_op jit(solution)/shard_map/ppermute | solution.py:21
  10.9 13.9 %collective-permute-start.2 = (f32[256,256]{1,0:T(8,128)S(1)}, f32[256,256]{1,0:T(8,128)}, u32[]{:S(2)}, u32[]{:S(2)}) collective-permute-start(f32[256,256]{1,0:T(8,128)S(1)} %slice.64), channel_id=1, source_target_pairs={{0,3},{1,4},{2,5},{16,19},{17,20},{18,21},{32,35},{33,36},{34,37}} | collective-permute-start | bytes 786440 | tf_op jit(solution)/shard_map/ppermute | solution.py:21
  12.3 14.9 %collective-permute-start.3 = (f32[256,256]{1,0:T(8,128)S(1)}, f32[256,256]{1,0:T(8,128)}, u32[]{:S(2)}, u32[]{:S(2)}) collective-permute-start(f32[256,256]{1,0:T(8,128)S(1)} %slice.64), channel_id=1, source_target_pairs={{0,4},{1,5},{2,6},{16,20},{17,21},{18,22},{32,36},{33,37},{34,38}} | collective-permute-start | bytes 786440 | tf_op jit(solution)/shard_map/ppermute | solution.py:21
  13.6 15.9 %collective-permute-start.4 = (f32[256,256]{1,0:T(8,128)S(1)}, f32[256,256]{1,0:T(8,128)}, u32[]{:S(2)}, u32[]{:S(2)}) collective-permute-start(f32[256,256]{1,0:T(8,128)S(1)} %slice.64), channel_id=1, source_target_pairs={{0,5},{1,6},{2,7},{16,21},{17,22},{18,23},{32,37},{33,38},{34,39}} | collective-permute-start | bytes 786440 | tf_op jit(solution)/shard_map/ppermute | solution.py:21
  16.7 1.7 copy-start.1
  18.4 343.1 %all-reduce.6.cloned.1.call-start = ((), (), s32[]{:S(2)}) async-start(), calls=%async_computation | async-start | bytes 12582912 | tf_op jit(solution)/shard_map/psum | solution.py:46
  20.1 11.8 %collective-permute-start.5 = (f32[256,256]{1,0:T(8,128)S(1)}, f32[256,256]{1,0:T(8,128)S(1)}, u32[]{:S(2)}, u32[]{:S(2)}) collective-permute-start(f32[256,256]{1,0:T(8,128)S(1)} %slice.64), channel_id=1, source_target_pairs={{0,6},{1,7},{2,8},{16,22},{17,23},{18,24},{32,38},{33,39},{34,40}} | collective-permute-start | bytes 786440 | tf_op jit(solution)/shard_map/ppermute | solution.py:21
  22.4 10.9 %collective-permute-start.6 = (f32[256,256]{1,0:T(8,128)S(1)}, f32[256,256]{1,0:T(8,128)S(1)}, u32[]{:S(2)}, u32[]{:S(2)}) collective-permute-start(f32[256,256]{1,0:T(8,128)S(1)} %slice.64), channel_id=1, source_target_pairs={{0,7},{1,8},{2,9},{16,23},{17,24},{18,25},{32,39},{33,40},{34,41}} | collective-permute-start | bytes 786440 | tf_op jit(solution)/shard_map/ppermute | solution.py:21
  24.8 9.9 %collective-permute-start.7 = (f32[256,256]{1,0:T(8,128)S(1)}, f32[256,256]{1,0:T(8,128)S(1)}, u32[]{:S(2)}, u32[]{:S(2)}) collective-permute-start(f32[256,256]{1,0:T(8,128)S(1)} %slice.64), channel_id=1, source_target_pairs={{0,8},{1,9},{2,10},{16,24},{17,25},{18,26},{32,40},{33,41},{34,42}} | collective-permute-start | bytes 786440 | tf_op jit(solution)/shard_map/ppermute | solution.py:21
  27.2 9.0 %collective-permute-start.8 = (f32[256,256]{1,0:T(8,128)S(1)}, f32[256,256]{1,0:T(8,128)S(1)}, u32[]{:S(2)}, u32[]{:S(2)}) collective-permute-start(f32[256,256]{1,0:T(8,128)S(1)} %slice.64), channel_id=1, source_target_pairs={{0,9},{1,10},{2,11},{16,25},{17,26},{18,27},{32,41},{33,42},{34,43}} | collective-permute-start | bytes 786440 | tf_op jit(solution)/shard_map/ppermute | solution.py:21
  29.5 8.0 %collective-permute-start.9 = (f32[256,256]{1,0:T(8,128)S(1)}, f32[256,256]{1,0:T(8,128)S(1)}, u32[]{:S(2)}, u32[]{:S(2)}) collective-permute-start(f32[256,256]{1,0:T(8,128)S(1)} %slice.64), channel_id=1, source_target_pairs={{0,10},{1,11},{2,12},{16,26},{17,27},{18,28},{32,42},{33,43},{34,44}} | collective-permute-start | bytes 786440 | tf_op jit(solution)/shard_map/ppermute | solution.py:21
  31.9 7.0 %collective-permute-start.10 = (f32[256,256]{1,0:T(8,128)S(1)}, f32[256,256]{1,0:T(8,128)S(1)}, u32[]{:S(2)}, u32[]{:S(2)}) collective-permute-start(f32[256,256]{1,0:T(8,128)S(1)} %slice.64), channel_id=1, source_target_pairs={{0,11},{1,12},{2,13},{16,27},{17,28},{18,29},{32,43},{33,44},{34,45}} | collective-permute-start | bytes 786440 | tf_op jit(solution)/shard_map/ppermute | solution.py:21
  33.3 6.3 %collective-permute-start.11 = (f32[256,256]{1,0:T(8,128)S(1)}, f32[256,256]{1,0:T(8,128)S(1)}, u32[]{:S(2)}, u32[]{:S(2)}) collective-permute-start(f32[256,256]{1,0:T(8,128)S(1)} %slice.64), channel_id=1, source_target_pairs={{0,12},{1,13},{2,14},{16,28},{17,29},{18,30},{32,44},{33,45},{34,46}} | collective-permute-start | bytes 786440 | tf_op jit(solution)/shard_map/ppermute | solution.py:21
  34.7 5.7 %collective-permute-start.12 = (f32[256,256]{1,0:T(8,128)S(1)}, f32[256,256]{1,0:T(8,128)S(1)}, u32[]{:S(2)}, u32[]{:S(2)}) collective-permute-start(f32[256,256]{1,0:T(8,128)S(1)} %slice.64), channel_id=1, source_target_pairs={{0,13},{1,14},{2,15},{16,29},{17,30},{18,31},{32,45},{33,46},{34,47}} | collective-permute-start | bytes 786440 | tf_op jit(solution)/shard_map/ppermute | solution.py:21
  36.1 5.0 %collective-permute-start.13 = (f32[256,256]{1,0:T(8,128)S(1)}, f32[256,256]{1,0:T(8,128)S(1)}, u32[]{:S(2)}, u32[]{:S(2)}) collective-permute-start(f32[256,256]{1,0:T(8,128)S(1)} %slice.64), channel_id=1, source_target_pairs={{0,14},{1,15},{2,0},{16,30},{17,31},{18,16},{32,46},{33,47},{34,32}} | collective-permute-start | bytes 786440 | tf_op jit(solution)/shard_map/ppermute | solution.py:21
  37.5 4.3 %collective-permute-start.14 = (f32[256,256]{1,0:T(8,128)S(1)}, f32[256,256]{1,0:T(8,128)S(1)}, u32[]{:S(2)}, u32[]{:S(2)}) collective-permute-start(f32[256,256]{1,0:T(8,128)S(1)} %slice.64), channel_id=1, source_target_pairs={{0,15},{1,0},{2,1},{16,31},{17,16},{18,17},{32,47},{33,32},{34,33}} | collective-permute-start | bytes 786440 | tf_op jit(solution)/shard_map/ppermute | solution.py:21
  43.8 11.7 %collective-permute-start.15 = (f32[256,768]{1,0:T(8,128)S(1)}, f32[256,768]{1,0:T(8,128)S(1)}, u32[]{:S(2)}, u32[]{:S(2)}) collective-permute-start(f32[256,768]{1,0:T(8,128)S(1)} %pad_maximum_fusion.1), channel_id=1, source_target_pairs={{0,16},{1,17},{2,18},{3,19},{4,20},{5,21},{6,22},{7,23},{8,24},{9,... | collective-permute-start | bytes 2359304 | tf_op jit(solution)/shard_map/ppermute | solution.py:33
  50.7 5.6 %collective-permute-start.16 = (f32[256,768]{1,0:T(8,128)S(1)}, f32[256,768]{1,0:T(8,128)S(1)}, u32[]{:S(2)}, u32[]{:S(2)}) collective-permute-start(f32[256,768]{1,0:T(8,128)S(1)} %pad_maximum_fusion.1), channel_id=1, source_target_pairs={{0,32},{1,33},{2,34},{3,35},{4,36},{5,37},{6,38},{7,39},{8,40},{9,... | collective-permute-start | bytes 2359304 | tf_op jit(solution)/shard_map/ppermute | solution.py:33
  51.4 49.2 %collective-permute-start.17 = (f32[256,768]{1,0:T(8,128)S(1)}, f32[256,768]{1,0:T(8,128)}, u32[]{:S(2)}, u32[]{:S(2)}) collective-permute-start(f32[256,768]{1,0:T(8,128)S(1)} %pad_maximum_fusion.1), channel_id=1, source_target_pairs={{0,48},{1,49},{2,50},{3,51},{4,52},{5,53},{6,54},{7,55},{8,56},{9,... | collective-permute-start | bytes 2359304 | tf_op jit(solution)/shard_map/ppermute | solution.py:33
  52.8 93.9 %collective-permute-start.18 = (f32[256,768]{1,0:T(8,128)S(1)}, f32[256,768]{1,0:T(8,128)S(1)}, u32[]{:S(2)}, u32[]{:S(2)}) collective-permute-start(f32[256,768]{1,0:T(8,128)S(1)} %pad_maximum_fusion.1), channel_id=1, source_target_pairs={{0,64},{1,65},{2,66},{3,67},{4,68},{5,69},{6,70},{7,71},{8,72},{9,... | collective-permute-start | bytes 2359304 | tf_op jit(solution)/shard_map/ppermute | solution.py:33
  54.1 97.8 %collective-permute-start.19 = (f32[256,768]{1,0:T(8,128)S(1)}, f32[256,768]{1,0:T(8,128)S(1)}, u32[]{:S(2)}, u32[]{:S(2)}) collective-permute-start(f32[256,768]{1,0:T(8,128)S(1)} %pad_maximum_fusion.1), channel_id=1, source_target_pairs={{0,80},{1,81},{2,82},{3,83},{4,84},{5,85},{6,86},{7,87},{8,88},{9,... | collective-permute-start | bytes 2359304 | tf_op jit(solution)/shard_map/ppermute | solution.py:33
  55.5 96.4 %collective-permute-start.20 = (f32[256,768]{1,0:T(8,128)S(1)}, f32[256,768]{1,0:T(8,128)S(1)}, u32[]{:S(2)}, u32[]{:S(2)}) collective-permute-start(f32[256,768]{1,0:T(8,128)S(1)} %pad_maximum_fusion.1), channel_id=1, source_target_pairs={{0,96},{1,97},{2,98},{3,99},{4,100},{5,101},{6,102},{7,103},{8,104... | collective-permute-start | bytes 2359304 | tf_op jit(solution)/shard_map/ppermute | solution.py:33
  56.3 95.7 %collective-permute-start.21 = (f32[256,768]{1,0:T(8,128)S(1)}, f32[256,768]{1,0:T(8,128)S(1)}, u32[]{:S(2)}, u32[]{:S(2)}) collective-permute-start(f32[256,768]{1,0:T(8,128)S(1)} %pad_maximum_fusion.1), channel_id=1, source_target_pairs={{0,112},{1,113},{2,114},{3,115},{4,116},{5,117},{6,118},{7,119},{8... | collective-permute-start | bytes 2359304 | tf_op jit(solution)/shard_map/ppermute | solution.py:33
  361.5 10.2 %copy-start.3 = (f32[256,256]{1,0:T(8,128)S(1)}, f32[256,256]{1,0:T(8,128)}, u32[]{:S(2)}) copy-start(f32[256,256]{1,0:T(8,128)} %get-tuple-element.56) | copy-start | bytes 786436
  361.5 10.2 %copy-start.4 = (f32[256,256]{1,0:T(8,128)S(1)}, f32[256,256]{1,0:T(8,128)}, u32[]{:S(2)}) copy-start(f32[256,256]{1,0:T(8,128)} %get-tuple-element.54) | copy-start | bytes 786436
  361.5 10.2 %copy-start.5 = (f32[256,256]{1,0:T(8,128)S(1)}, f32[256,256]{1,0:T(8,128)}, u32[]{:S(2)}) copy-start(f32[256,256]{1,0:T(8,128)} %get-tuple-element.52) | copy-start | bytes 786436
  371.7 1.9 copy-start.2
  373.6 16.5 %copy-start = (f32[2048,768]{1,0:T(8,128)}, f32[2048,768]{1,0:T(8,128)S(1)}, u32[]{:S(2)}) copy-start(f32[2048,768]{1,0:T(8,128)S(1)} %fusion.7) | copy-start | bytes 18874372
Sparse Core Ops, SparseCore 0:
  18.5 72.9 all-reduce.7
  95.5 155.0 all-reduce.5

commit v2 on v1

--- a/solution.py
+++ b/solution.py
@@ -16,25 +16,20 @@
         pairs = [
             (a * col_count + b, a * col_count + (b + shift) % col_count)
             for a in range(STEPS)
-            for b in range(STEPS)
+            for b in range(a + 1)
         ]
         heard.append(lax.ppermute(piece, ("row", "col"), pairs))
     heard = jnp.stack(heard)
-    band = jnp.concatenate(
-        [heard[(col_index - b) % col_count] for b in range(STEPS)], axis=1
-    )
-    heard = [band]
-    for shift in range(1, row_count):
-        pairs = [
-            (a * col_count + q, ((a + shift) % row_count) * col_count + q)
-            for a in range(STEPS)
-            for q in range(col_count)
-        ]
-        heard.append(lax.ppermute(band, ("row", "col"), pairs))
-    heard = jnp.stack(heard)
-    return jnp.concatenate(
-        [heard[(row_index - a) % row_count] for a in range(STEPS)], axis=0
-    )
+    blocks = []
+    for a in range(STEPS):
+        band = jnp.concatenate([heard[(col_index - b) % col_count] for b in range(a + 1)], axis=1)
+        down = [band]
+        for shift in range(1, row_count):
+            pairs = [(a * col_count + q, ((a + shift) % row_count) * col_count + q) for q in range(col_count)]
+            down.append(lax.ppermute(band, ("row", "col"), pairs))
+        band = jnp.stack(down)[(row_index - a) % row_count]
+        blocks.append([band[:, b * BLOCK:(b + 1) * BLOCK] for b in range(a + 1)])
+    return blocks
 
 
 def gather_columns(kernel, col_index):
@@ -103,26 +98,25 @@
     row_ids = jnp.arange(rows_local) // BLOCK * row_count + row_index
     col_ids = jnp.arange(cols_local) // BLOCK * col_count + col_index
 
-    corner = gather_corner(kernel, row_index, col_index)
+    blocks = gather_corner(kernel, row_index, col_index)
     band_cols = gather_columns(kernel, col_index)
     band_rows = gather_rows(kernel, row_index)
 
-    blocks = [[corner[a * BLOCK:(a + 1) * BLOCK, b * BLOCK:(b + 1) * BLOCK] for b in range(STEPS)] for a in range(STEPS)]
     factor, inverse = factor_corner(blocks)
     panels = lax.dot_general(
         band_cols, inverse, (((1,), (1,)), ((), ())),
-        precision=lax.Precision.HIGH, preferred_element_type=jnp.float32,
+        precision=lax.Precision.HIGHEST, preferred_element_type=jnp.float32,
     )
     across = lax.dot_general(
         band_rows, inverse, (((0,), (1,)), ((), ())),
-        precision=lax.Precision.HIGH, preferred_element_type=jnp.float32,
+        precision=lax.Precision.HIGHEST, preferred_element_type=jnp.float32,
     )
     own = lax.dynamic_slice_in_dim(factor, jnp.minimum(row_index, STEPS - 1) * BLOCK, BLOCK, 0)
     head = jnp.where(row_index < STEPS, own, panels[:BLOCK])
     panels = lax.dynamic_update_slice(panels, head, (0, 0))
     update = lax.dot_general(
         panels, across, (((1,), (1,)), ((), ())),
-        precision=lax.Precision.HIGH, preferred_element_type=jnp.float32,
+        precision=lax.Precision.HIGHEST, preferred_element_type=jnp.float32,
     )
     keep = (row_ids >= STEPS)[:, None] & (col_ids >= STEPS)[None, :]
     schur = jnp.where(keep, kernel - update, jnp.float32(0.0))

time: 402 us -> 431 us (1.072)
  the two profiles are of different devices: /device:TPU:5 before, /device:TPU:1 now
where the time goes in v2:
time: 431 us; the launch traced here: 426 us
  other arithmetic  172 us (40%)
  starting transfers between devices  77.3 us (18%)
  matrix products  73 us (17%)
  local copies, waits for them, and re-layouts  61.5 us (14%)
  waiting for transfers between devices  21.8 us (5%)
  between operations  19.1 us (4%)
    another operation x20, other arithmetic, factor_corner(): lower[k][k] = jnp.linalg.cholesky(schur)  103 us
    another operation x8, other arithmetic, factor_corner(): jax.scipy.linalg.solve_triangular(lower[k][k], eye, lower=True)  60.6 us
    ppermute x21, starting transfers between devices, gather_corner(): down.append(lax.ppermute(band, ('row', 'col'), pairs))  52.1 us
    unnamed x49, local copies, waits for them, and re-layouts  36.4 us
    dot_general x1, matrix products, shards(): lax.dot_general(panels, across, (((1,), (1,)), ((), ())), precision=lax.P...  25.4 us
    ppermute x15, starting transfers between devices, gather_corner(): heard.append(lax.ppermute(piece, ('row', 'col'), pairs))  25.1 us
    dot_general x1, matrix products, shards(): lax.dot_general(band_cols, inverse, (((1,), (1,)), ((), ())), precision=l...  18.4 us
    dot_general x1, matrix products, shards(): lax.dot_general(band_rows, inverse, (((0,), (1,)), ((), ())), precision=l...  17.9 us
  transfers between devices with their start and end apart: 38, of which 6 were waited for; matrix products, arithmetic and copies ran while one was open for 60% of the time, Pallas kernels for 0%

profile of v2, /device:TPU:1, one launch (start us, length us, event | category | flops | bytes accessed | tf_op | source)
XLA Modules:
  0.0 425.6 jit_solution(11552758089186619202)
XLA Ops:
  7.6 1.3 select_dynamic-update-slice_fusion.1
  8.9 1.6 copy-done
  11.6 4.4 %collective-permute-start = (f32[256,256]{1,0:T(8,128)S(1)}, f32[256,256]{1,0:T(8,128)S(1)}, u32[]{:S(2)}, u32[]{:S(2)}) collective-permute-start(f32[256,256]{1,0:T(8,128)S(1)} %slice.61), channel_id=1, source_target_pairs={{0,1},{16,17},{17,18},{32,33},{33,34},{34,35}} | collective-permute-start | bytes 786440 | tf_op jit(solution)/shard_map/ppermute | solution.py:21
  16.0 3.3 collective-permute-start.1
  19.2 1.3 collective-permute-start.2
  20.5 1.3 collective-permute-start.3
  21.9 1.3 collective-permute-start.4
  23.2 3.1 broadcast_in_dim.24
  26.3 3.1 select_dynamic-update-slice_fusion
  29.4 1.7 bitcast_dynamic-update-slice_fusion.41
  31.3 1.3 collective-permute-start.5
  33.3 1.3 collective-permute-start.6
  46.4 3.6 collective-permute-done.7
  52.0 3.6 collective-permute-done.8
  57.6 3.6 collective-permute-done.9
  61.2 1.9 collective-permute-start.14
  63.9 3.0 collective-permute-done.10
  71.7 2.1 collective-permute-start.22
  73.8 1.3 collective-permute-start.23
  79.0 2.1 collective-permute-start.24
  84.7 25.6 %collective-permute-start.25 = (f32[256,512]{1,0:T(8,128)S(1)}, f32[256,512]{1,0:T(8,128)}, u32[]{:S(2)}, u32[]{:S(2)}) collective-permute-start(f32[256,512]{1,0:T(8,128)S(1)} %pad_maximum_fusion.2), channel_id=1, source_target_pairs={{16,80},{17,81},{18,82},{19,83},{20,84},{21,85},{22,86},{23,87},{2... | collective-permute-start | bytes 1572872 | tf_op jit(solution)/shard_map/ppermute | solution.py:29
  110.3 2.3 collective-permute-start.26
  112.6 1.3 copy-done.7
  115.1 11.7 %cholesky.172 = f32[128,128]{1,0:T(8,128)S(1)} custom-call(f32[128,128]{1,0:T(8,128)S(1)} %cholesky.270), custom_call_target="Cholesky" | custom-call | tf_op jit(solution)/shard_map/jit(cholesky)/cholesky | solution.py:67
  126.9 9.8 %custom-call.15 = f32[1,128,128]{1,2,0:T(8,128)S(1)} custom-call(f32[1,128,128]{2,1,0:T(8,128)S(1)} %get-tuple-element.78), custom_call_target="InvertDiagBlocksLowerTriangular" | custom-call | tf_op jit(solution)/shard_map/jit(cholesky)/cholesky | solution.py:67
  137.1 11.7 %cholesky.189 = f32[128,128]{1,0:T(8,128)S(1)} custom-call(f32[128,128]{1,0:T(8,128)S(1)} %convolution_subtract_fusion.9), custom_call_target="Cholesky" | custom-call | tf_op jit(solution)/shard_map/jit(cholesky)/cholesky | solution.py:67
  151.6 4.3 %while.6 = (s32[]{:T(128)}, f32[256,256]{1,0:T(8,128)S(1)}, s32[2,2]{1,0:T(2,128)S(1)}, f32[2,128,128]{2,1,0:T(8,128)S(1)}, s32[]{:T(128)}) while((s32[]{:T(128)}, f32[256,256]{1,0:T(8,128)S(1)}, s32[2,2]{1,0:T(2,128)S(1)}, f32[2,128,128]{2,1,0:T(8,128)S(1)}, s32[]{:T(128)}) %tuple.68), condition=%wide.while_cond, body=%wide.while_body.sunk | while | flops 2 | bytes 131181 | solution.py:68
  152.7 1.3 bitcast_dynamic-update-slice_fusion.45
  154.6 1.3 bitcast_dynamic-update-slice_fusion.45
  155.9 19.7 %custom-call.16 = f32[2,128,128]{1,2,0:T(8,128)S(1)} custom-call(f32[2,128,128]{2,1,0:T(8,128)S(1)} %get-tuple-element.24), custom_call_target="InvertDiagBlocksLowerTriangular" | custom-call | tf_op jit(solution)/shard_map/jit(_solve_triangular)/triangular_solve | solution.py:68
  176.5 2.3 collective-permute-start.27
  178.9 1.9 bitcast_dynamic-update-slice_fusion.17
  180.7 1.3 collective-permute-start.28
  182.9 1.5 collective-permute-start.29
  184.4 1.9 bitcast_dynamic-update-slice_fusion.15
  186.4 1.6 collective-permute-start.30
  188.0 1.9 bitcast_dynamic-update-slice_fusion.14
  189.9 1.5 collective-permute-start.31
  191.5 1.9 bitcast_dynamic-update-slice_fusion.13
  193.3 1.5 collective-permute-start.32
  195.7 1.6 collective-permute-start.33
  201.3 11.7 %cholesky.206 = f32[128,128]{1,0:T(8,128)S(1)} custom-call(f32[128,128]{1,0:T(8,128)S(1)} %cholesky.273), custom_call_target="Cholesky" | custom-call | tf_op jit(solution)/shard_map/jit(cholesky)/cholesky | solution.py:67
  213.0 9.8 %custom-call.17 = f32[1,128,128]{1,2,0:T(8,128)S(1)} custom-call(f32[1,128,128]{2,1,0:T(8,128)S(1)} %get-tuple-element.74), custom_call_target="InvertDiagBlocksLowerTriangular" | custom-call | tf_op jit(solution)/shard_map/jit(cholesky)/cholesky | solution.py:67
  223.5 11.8 %cholesky.223 = f32[128,128]{1,0:T(8,128)S(1)} custom-call(f32[128,128]{1,0:T(8,128)S(1)} %convolution_subtract_fusion.8), custom_call_target="Cholesky" | custom-call | tf_op jit(solution)/shard_map/jit(cholesky)/cholesky | solution.py:67
  238.7 3.9 while.7
  239.4 1.3 bitcast_dynamic-update-slice_fusion.46
  241.3 1.3 bitcast_dynamic-update-slice_fusion.46
  242.7 19.7 %custom-call.18 = f32[2,128,128]{1,2,0:T(8,128)S(1)} custom-call(f32[2,128,128]{2,1,0:T(8,128)S(1)} %get-tuple-element.25), custom_call_target="InvertDiagBlocksLowerTriangular" | custom-call | tf_op jit(solution)/shard_map/jit(_solve_triangular)/triangular_solve | solution.py:68
  264.5 2.1 bitcast_dynamic-update-slice_fusion.9
  267.9 2.1 bitcast_dynamic-update-slice_fusion.8
  269.9 2.1 bitcast_dynamic-update-slice_fusion.7
  272.0 2.1 bitcast_dynamic-update-slice_fusion.6
  274.1 2.1 bitcast_dynamic-update-slice_fusion.5
  277.1 7.0 %collective-permute-done.35 = f32[256,768]{1,0:T(8,128)S(1)} collective-permute-done((f32[256,768]{1,0:T(8,128)S(1)}, f32[256,768]{1,0:T(8,128)S(1)}, u32[]{:S(2)}, u32[]{:S(2)}) %collective-permute-start.35) | collective-permute-done | bytes 786464 | tf_op jit(solution)/shard_map/ppermute | solution.py:29
  290.9 11.7 %cholesky.240 = f32[128,128]{1,0:T(8,128)S(1)} custom-call(f32[128,128]{1,0:T(8,128)S(1)} %cholesky.276), custom_call_target="Cholesky" | custom-call | tf_op jit(solution)/shard_map/jit(cholesky)/cholesky | solution.py:67
  302.7 9.8 %custom-call.19 = f32[1,128,128]{1,2,0:T(8,128)S(1)} custom-call(f32[1,128,128]{2,1,0:T(8,128)S(1)} %get-tuple-element.70), custom_call_target="InvertDiagBlocksLowerTriangular" | custom-call | tf_op jit(solution)/shard_map/jit(cholesky)/cholesky | solution.py:67
  313.2 11.9 %cholesky.257 = f32[128,128]{1,0:T(8,128)S(1)} custom-call(f32[128,128]{1,0:T(8,128)S(1)} %convolution_subtract_fusion.7), custom_call_target="Cholesky" | custom-call | tf_op jit(solution)/shard_map/jit(cholesky)/cholesky | solution.py:67
  327.8 3.9 while.8
  328.4 1.3 bitcast_dynamic-update-slice_fusion.47
  330.3 1.3 bitcast_dynamic-update-slice_fusion.47
  331.7 19.7 %custom-call.20 = f32[2,128,128]{1,2,0:T(8,128)S(1)} custom-call(f32[2,128,128]{2,1,0:T(8,128)S(1)} %get-tuple-element.26), custom_call_target="InvertDiagBlocksLowerTriangular" | custom-call | tf_op jit(solution)/shard_map/jit(_solve_triangular)/triangular_solve | solution.py:68
  354.9 17.9 %fusion.31 = f32[1024,768]{1,0:T(8,128)} fusion(f32[768,1024]{1,0:T(8,128)} %all-reduce.8.cloned.1.call-done, f32[256,256]{1,0:T(8,128)S(1)} %cholesky.201, f32[256,256]{1,0:T(8,128)S(1)} %pad_maximum_fusion.3, f32[128,256]{1,0:T(8,128)S(1)} %fusion.36, f32[128,256]{1,0:T(8,128)S(1)} %fusion.25, f32[256,256]{1,0:T(8,128)S(1)} %convolution_negate_fusion, ...), kind=kOutput, calls=%fused_computation.119 | convolution fusion | flops 7253655552 | bytes 8126464 | tf_op jit(solution)/shard_map/dot_general | solution.py:110
  372.9 18.4 %fusion.33 = f32[2048,768]{1,0:T(8,128)S(1)} fusion(f32[2048,768]{1,0:T(8,128)} %all-reduce.6.cloned.1.call-done, f32[256,256]{1,0:T(8,128)S(1)} %cholesky.201, f32[256,256]{1,0:T(8,128)S(1)} %pad_maximum_fusion.3, f32[128,256]{1,0:T(8,128)S(1)} %fusion.36, f32[128,256]{1,0:T(8,128)S(1)} %fusion.25, f32[256,256]{1,0:T(8,128)S(1)} %convolution_negate_fusion, ...), kind=kOutput, calls=%fused_computation.120 | convolution fusion | flops 14501412864 | bytes 14417920 | tf_op jit(solution)/shard_map/dot_general | solution.py:106
  393.2 25.4 %subtract_select_fusion = f32[2048,1024]{1,0:T(8,128)} fusion(f32[2048,1024]{1,0:T(8,128)} %param.4, pred[1024]{0:T(1024)(128)(4,1)S(1)} %fusion.58, pred[2048]{0:T(1024)(128)(4,1)S(1)} %fusion.52, f32[2048,768]{1,0:T(8,128)S(1)} %fusion.7, f32[1024,768]{1,0:T(8,128)S(1)} %copy-done.2), kind=kOutput, calls=%fused_computation.6 | convolution fusion | flops 19333644288 | bytes 26217472 | tf_op jit(solution)/shard_map/dot_general | solution.py:117
  (191 shorter events, 65.7 us)
Async XLA Ops:
  7.2 347.7 %all-reduce.8.cloned.1.call-start = ((), (), s32[]{:S(2)}) async-start(), calls=%async_computation.1 | async-start | bytes 6291456 | tf_op jit(solution)/shard_map/psum | solution.py:50
  8.9 1.6 copy-start
  10.6 362.3 %all-reduce.6.cloned.1.call-start = ((), (), s32[]{:S(2)}) async-start(), calls=%async_computation | async-start | bytes 12582912 | tf_op jit(solution)/shard_map/psum | solution.py:41
  11.6 19.7 %collective-permute-start = (f32[256,256]{1,0:T(8,128)S(1)}, f32[256,256]{1,0:T(8,128)S(1)}, u32[]{:S(2)}, u32[]{:S(2)}) collective-permute-start(f32[256,256]{1,0:T(8,128)S(1)} %slice.61), channel_id=1, source_target_pairs={{0,1},{16,17},{17,18},{32,33},{33,34},{34,35}} | collective-permute-start | bytes 786440 | tf_op jit(solution)/shard_map/ppermute | solution.py:21
  16.0 17.3 %collective-permute-start.1 = (f32[256,256]{1,0:T(8,128)S(1)}, f32[256,256]{1,0:T(8,128)S(1)}, u32[]{:S(2)}, u32[]{:S(2)}) collective-permute-start(f32[256,256]{1,0:T(8,128)S(1)} %slice.61), channel_id=1, source_target_pairs={{0,2},{16,18},{17,19},{32,34},{33,35},{34,36}} | collective-permute-start | bytes 786440 | tf_op jit(solution)/shard_map/ppermute | solution.py:21
  19.2 16.1 %collective-permute-start.2 = (f32[256,256]{1,0:T(8,128)S(1)}, f32[256,256]{1,0:T(8,128)S(1)}, u32[]{:S(2)}, u32[]{:S(2)}) collective-permute-start(f32[256,256]{1,0:T(8,128)S(1)} %slice.61), channel_id=1, source_target_pairs={{0,3},{16,19},{17,20},{32,35},{33,36},{34,37}} | collective-permute-start | bytes 786440 | tf_op jit(solution)/shard_map/ppermute | solution.py:21
  20.5 16.8 %collective-permute-start.3 = (f32[256,256]{1,0:T(8,128)S(1)}, f32[256,256]{1,0:T(8,128)S(1)}, u32[]{:S(2)}, u32[]{:S(2)}) collective-permute-start(f32[256,256]{1,0:T(8,128)S(1)} %slice.61), channel_id=1, source_target_pairs={{0,4},{16,20},{17,21},{32,36},{33,37},{34,38}} | collective-permute-start | bytes 786440 | tf_op jit(solution)/shard_map/ppermute | solution.py:21
  21.9 17.5 %collective-permute-start.4 = (f32[256,256]{1,0:T(8,128)S(1)}, f32[256,256]{1,0:T(8,128)S(1)}, u32[]{:S(2)}, u32[]{:S(2)}) collective-permute-start(f32[256,256]{1,0:T(8,128)S(1)} %slice.61), channel_id=1, source_target_pairs={{0,5},{16,21},{17,22},{32,37},{33,38},{34,39}} | collective-permute-start | bytes 786440 | tf_op jit(solution)/shard_map/ppermute | solution.py:21
  31.3 10.2 %collective-permute-start.5 = (f32[256,256]{1,0:T(8,128)S(1)}, f32[256,256]{1,0:T(8,128)S(1)}, u32[]{:S(2)}, u32[]{:S(2)}) collective-permute-start(f32[256,256]{1,0:T(8,128)S(1)} %slice.61), channel_id=1, source_target_pairs={{0,6},{16,22},{17,23},{32,38},{33,39},{34,40}} | collective-permute-start | bytes 786440 | tf_op jit(solution)/shard_map/ppermute | solution.py:21
  33.3 11.1 %collective-permute-start.6 = (f32[256,256]{1,0:T(8,128)S(1)}, f32[256,256]{1,0:T(8,128)S(1)}, u32[]{:S(2)}, u32[]{:S(2)}) collective-permute-start(f32[256,256]{1,0:T(8,128)S(1)} %slice.61), channel_id=1, source_target_pairs={{0,7},{16,23},{17,24},{32,39},{33,40},{34,41}} | collective-permute-start | bytes 786440 | tf_op jit(solution)/shard_map/ppermute | solution.py:21
  35.3 14.6 %collective-permute-start.7 = (f32[256,256]{1,0:T(8,128)S(1)}, f32[256,256]{1,0:T(8,128)S(1)}, u32[]{:S(2)}, u32[]{:S(2)}) collective-permute-start(f32[256,256]{1,0:T(8,128)S(1)} %slice.61), channel_id=1, source_target_pairs={{0,8},{16,24},{17,25},{32,40},{33,41},{34,42}} | collective-permute-start | bytes 786440 | tf_op jit(solution)/shard_map/ppermute | solution.py:21
  37.4 18.2 %collective-permute-start.8 = (f32[256,256]{1,0:T(8,128)S(1)}, f32[256,256]{1,0:T(8,128)S(1)}, u32[]{:S(2)}, u32[]{:S(2)}) collective-permute-start(f32[256,256]{1,0:T(8,128)S(1)} %slice.61), channel_id=1, source_target_pairs={{0,9},{16,25},{17,26},{32,41},{33,42},{34,43}} | collective-permute-start | bytes 786440 | tf_op jit(solution)/shard_map/ppermute | solution.py:21
  39.4 21.8 %collective-permute-start.9 = (f32[256,256]{1,0:T(8,128)S(1)}, f32[256,256]{1,0:T(8,128)S(1)}, u32[]{:S(2)}, u32[]{:S(2)}) collective-permute-start(f32[256,256]{1,0:T(8,128)S(1)} %slice.61), channel_id=1, source_target_pairs={{0,10},{16,26},{17,27},{32,42},{33,43},{34,44}} | collective-permute-start | bytes 786440 | tf_op jit(solution)/shard_map/ppermute | solution.py:21
  41.4 25.4 %collective-permute-start.10 = (f32[256,256]{1,0:T(8,128)S(1)}, f32[256,256]{1,0:T(8,128)S(1)}, u32[]{:S(2)}, u32[]{:S(2)}) collective-permute-start(f32[256,256]{1,0:T(8,128)S(1)} %slice.61), channel_id=1, source_target_pairs={{0,11},{16,27},{17,28},{32,43},{33,44},{34,45}} | collective-permute-start | bytes 786440 | tf_op jit(solution)/shard_map/ppermute | solution.py:21
  44.4 23.2 %collective-permute-start.11 = (f32[256,256]{1,0:T(8,128)S(1)}, f32[256,256]{1,0:T(8,128)S(1)}, u32[]{:S(2)}, u32[]{:S(2)}) collective-permute-start(f32[256,256]{1,0:T(8,128)S(1)} %slice.61), channel_id=1, source_target_pairs={{0,12},{16,28},{17,29},{32,44},{33,45},{34,46}} | collective-permute-start | bytes 786440 | tf_op jit(solution)/shard_map/ppermute | solution.py:21
  50.0 18.3 %collective-permute-start.12 = (f32[256,256]{1,0:T(8,128)S(1)}, f32[256,256]{1,0:T(8,128)S(1)}, u32[]{:S(2)}, u32[]{:S(2)}) collective-permute-start(f32[256,256]{1,0:T(8,128)S(1)} %slice.61), channel_id=1, source_target_pairs={{0,13},{16,29},{17,30},{32,45},{33,46},{34,47}} | collective-permute-start | bytes 786440 | tf_op jit(solution)/shard_map/ppermute | solution.py:21
  55.6 13.4 %collective-permute-start.13 = (f32[256,256]{1,0:T(8,128)S(1)}, f32[256,256]{1,0:T(8,128)S(1)}, u32[]{:S(2)}, u32[]{:S(2)}) collective-permute-start(f32[256,256]{1,0:T(8,128)S(1)} %slice.61), channel_id=1, source_target_pairs={{0,14},{16,30},{17,31},{32,46},{33,47},{34,32}} | collective-permute-start | bytes 786440 | tf_op jit(solution)/shard_map/ppermute | solution.py:21
  61.2 8.5 %collective-permute-start.14 = (f32[256,256]{1,0:T(8,128)S(1)}, f32[256,256]{1,0:T(8,128)S(1)}, u32[]{:S(2)}, u32[]{:S(2)}) collective-permute-start(f32[256,256]{1,0:T(8,128)S(1)} %slice.61), channel_id=1, source_target_pairs={{0,15},{16,31},{17,16},{32,47},{33,32},{34,33}} | collective-permute-start | bytes 786440 | tf_op jit(solution)/shard_map/ppermute | solution.py:21
  71.7 104.8 %collective-permute-start.22 = (f32[256,512]{1,0:T(8,128)S(1)}, f32[256,512]{1,0:T(8,128)}, u32[]{:S(2)}, u32[]{:S(2)}) collective-permute-start(f32[256,512]{1,0:T(8,128)S(1)} %pad_maximum_fusion.2), channel_id=1, source_target_pairs={{16,32},{17,33},{18,34},{19,35},{20,36},{21,37},{22,38},{23,39},{2... | collective-permute-start | bytes 1572872 | tf_op jit(solution)/shard_map/ppermute | solution.py:29
  73.8 106.9 %collective-permute-start.23 = (f32[256,512]{1,0:T(8,128)S(1)}, f32[256,512]{1,0:T(8,128)S(1)}, u32[]{:S(2)}, u32[]{:S(2)}) collective-permute-start(f32[256,512]{1,0:T(8,128)S(1)} %pad_maximum_fusion.2), channel_id=1, source_target_pairs={{16,48},{17,49},{18,50},{19,51},{20,52},{21,53},{22,54},{23,55},{2... | collective-permute-start | bytes 1572872 | tf_op jit(solution)/shard_map/ppermute | solution.py:29
  75.1 5.9 %collective-permute-start.15 = (f32[256,256]{1,0:T(8,128)S(1)}, f32[256,256]{1,0:T(8,128)S(1)}, u32[]{:S(2)}, u32[]{:S(2)}) collective-permute-start(f32[256,256]{1,0:T(8,128)S(1)} %get-tuple-element.66), channel_id=1, source_target_pairs={{0,16},{1,17},{2,18},{3,19},{4,20},{5,21},{6,22},{7,23},{8,24},{9,... | collective-permute-start | bytes 786440 | tf_op jit(solution)/shard_map/ppermute | solution.py:29
  76.4 5.3 %collective-permute-start.16 = (f32[256,256]{1,0:T(8,128)S(1)}, f32[256,256]{1,0:T(8,128)S(1)}, u32[]{:S(2)}, u32[]{:S(2)}) collective-permute-start(f32[256,256]{1,0:T(8,128)S(1)} %get-tuple-element.66), channel_id=1, source_target_pairs={{0,32},{1,33},{2,34},{3,35},{4,36},{5,37},{6,38},{7,39},{8,40},{9,... | collective-permute-start | bytes 786440 | tf_op jit(solution)/shard_map/ppermute | solution.py:29
  79.0 103.9 %collective-permute-start.24 = (f32[256,512]{1,0:T(8,128)S(1)}, f32[256,512]{1,0:T(8,128)}, u32[]{:S(2)}, u32[]{:S(2)}) collective-permute-start(f32[256,512]{1,0:T(8,128)S(1)} %pad_maximum_fusion.2), channel_id=1, source_target_pairs={{16,64},{17,65},{18,66},{19,67},{20,68},{21,69},{22,70},{23,71},{2... | collective-permute-start | bytes 1572872 | tf_op jit(solution)/shard_map/ppermute | solution.py:29
  81.1 1.4 collective-permute-start.17
  81.8 1.4 collective-permute-start.18
  82.5 1.4 collective-permute-start.19
  83.2 1.4 collective-permute-start.20
  84.0 26.3 %collective-permute-start.21 = (f32[256,256]{1,0:T(8,128)S(1)}, f32[256,256]{1,0:T(8,128)S(1)}, u32[]{:S(2)}, u32[]{:S(2)}) collective-permute-start(f32[256,256]{1,0:T(8,128)S(1)} %get-tuple-element.66), channel_id=1, source_target_pairs={{0,112},{1,113},{2,114},{3,115},{4,116},{5,117},{6,118},{7,119},{8... | collective-permute-start | bytes 786440 | tf_op jit(solution)/shard_map/ppermute | solution.py:29
  84.7 101.7 %collective-permute-start.25 = (f32[256,512]{1,0:T(8,128)S(1)}, f32[256,512]{1,0:T(8,128)}, u32[]{:S(2)}, u32[]{:S(2)}) collective-permute-start(f32[256,512]{1,0:T(8,128)S(1)} %pad_maximum_fusion.2), channel_id=1, source_target_pairs={{16,80},{17,81},{18,82},{19,83},{20,84},{21,85},{22,86},{23,87},{2... | collective-permute-start | bytes 1572872 | tf_op jit(solution)/shard_map/ppermute | solution.py:29
  110.3 79.6 %collective-permute-start.26 = (f32[256,512]{1,0:T(8,128)S(1)}, f32[256,512]{1,0:T(8,128)}, u32[]{:S(2)}, u32[]{:S(2)}) collective-permute-start(f32[256,512]{1,0:T(8,128)S(1)} %pad_maximum_fusion.2), channel_id=1, source_target_pairs={{16,96},{17,97},{18,98},{19,99},{20,100},{21,101},{22,102},{23,103... | collective-permute-start | bytes 1572872 | tf_op jit(solution)/shard_map/ppermute | solution.py:29
  112.6 1.3 copy-start.7
  176.5 16.8 %collective-permute-start.27 = (f32[256,512]{1,0:T(8,128)S(1)}, f32[256,512]{1,0:T(8,128)S(1)}, u32[]{:S(2)}, u32[]{:S(2)}) collective-permute-start(f32[256,512]{1,0:T(8,128)S(1)} %pad_maximum_fusion.2), channel_id=1, source_target_pairs={{16,112},{17,113},{18,114},{19,115},{20,116},{21,117},{22,118},{23... | collective-permute-start | bytes 1572872 | tf_op jit(solution)/shard_map/ppermute | solution.py:29
  180.7 15.0 %collective-permute-start.28 = (f32[256,512]{1,0:T(8,128)S(1)}, f32[256,512]{1,0:T(8,128)S(1)}, u32[]{:S(2)}, u32[]{:S(2)}) collective-permute-start(f32[256,512]{1,0:T(8,128)S(1)} %pad_maximum_fusion.2), channel_id=1, source_target_pairs={{16,0},{17,1},{18,2},{19,3},{20,4},{21,5},{22,6},{23,7},{24,8},{25... | collective-permute-start | bytes 1572872 | tf_op jit(solution)/shard_map/ppermute | solution.py:29
  182.9 80.9 %collective-permute-start.29 = (f32[256,768]{1,0:T(8,128)S(1)}, f32[256,768]{1,0:T(8,128)}, u32[]{:S(2)}, u32[]{:S(2)}) collective-permute-start(f32[256,768]{1,0:T(8,128)S(1)} %pad_maximum_fusion.1), channel_id=1, source_target_pairs={{32,48},{33,49},{34,50},{35,51},{36,52},{37,53},{38,54},{39,55},{4... | collective-permute-start | bytes 2359304 | tf_op jit(solution)/shard_map/ppermute | solution.py:29
  186.4 80.2 %collective-permute-start.30 = (f32[256,768]{1,0:T(8,128)S(1)}, f32[256,768]{1,0:T(8,128)}, u32[]{:S(2)}, u32[]{:S(2)}) collective-permute-start(f32[256,768]{1,0:T(8,128)S(1)} %pad_maximum_fusion.1), channel_id=1, source_target_pairs={{32,64},{33,65},{34,66},{35,67},{36,68},{37,69},{38,70},{39,71},{4... | collective-permute-start | bytes 2359304 | tf_op jit(solution)/shard_map/ppermute | solution.py:29
  189.9 80.0 %collective-permute-start.31 = (f32[256,768]{1,0:T(8,128)S(1)}, f32[256,768]{1,0:T(8,128)}, u32[]{:S(2)}, u32[]{:S(2)}) collective-permute-start(f32[256,768]{1,0:T(8,128)S(1)} %pad_maximum_fusion.1), channel_id=1, source_target_pairs={{32,80},{33,81},{34,82},{35,83},{36,84},{37,85},{38,86},{39,87},{4... | collective-permute-start | bytes 2359304 | tf_op jit(solution)/shard_map/ppermute | solution.py:29
  193.3 78.7 %collective-permute-start.32 = (f32[256,768]{1,0:T(8,128)S(1)}, f32[256,768]{1,0:T(8,128)}, u32[]{:S(2)}, u32[]{:S(2)}) collective-permute-start(f32[256,768]{1,0:T(8,128)S(1)} %pad_maximum_fusion.1), channel_id=1, source_target_pairs={{32,96},{33,97},{34,98},{35,99},{36,100},{37,101},{38,102},{39,103... | collective-permute-start | bytes 2359304 | tf_op jit(solution)/shard_map/ppermute | solution.py:29
  195.7 78.3 %collective-permute-start.33 = (f32[256,768]{1,0:T(8,128)S(1)}, f32[256,768]{1,0:T(8,128)}, u32[]{:S(2)}, u32[]{:S(2)}) collective-permute-start(f32[256,768]{1,0:T(8,128)S(1)} %pad_maximum_fusion.1), channel_id=1, source_target_pairs={{32,112},{33,113},{34,114},{35,115},{36,116},{37,117},{38,118},{39... | collective-permute-start | bytes 2359304 | tf_op jit(solution)/shard_map/ppermute | solution.py:29
  263.8 12.3 %collective-permute-start.34 = (f32[256,768]{1,0:T(8,128)S(1)}, f32[256,768]{1,0:T(8,128)S(1)}, u32[]{:S(2)}, u32[]{:S(2)}) collective-permute-start(f32[256,768]{1,0:T(8,128)S(1)} %pad_maximum_fusion.1), channel_id=1, source_target_pairs={{32,0},{33,1},{34,2},{35,3},{36,4},{37,5},{38,6},{39,7},{40,8},{41... | collective-permute-start | bytes 2359304 | tf_op jit(solution)/shard_map/ppermute | solution.py:29
  266.6 17.4 %collective-permute-start.35 = (f32[256,768]{1,0:T(8,128)S(1)}, f32[256,768]{1,0:T(8,128)S(1)}, u32[]{:S(2)}, u32[]{:S(2)}) collective-permute-start(f32[256,768]{1,0:T(8,128)S(1)} %pad_maximum_fusion.1), channel_id=1, source_target_pairs={{32,16},{33,17},{34,18},{35,19},{36,20},{37,21},{38,22},{39,23},{4... | collective-permute-start | bytes 2359304 | tf_op jit(solution)/shard_map/ppermute | solution.py:29
  372.9 18.4 %copy-start.3 = (f32[256,256]{1,0:T(8,128)S(1)}, f32[256,256]{1,0:T(8,128)}, u32[]{:S(2)}) copy-start(f32[256,256]{1,0:T(8,128)} %copy.18) | copy-start | bytes 786436
  372.9 18.4 %copy-start.4 = (f32[256,256]{1,0:T(8,128)S(1)}, f32[256,256]{1,0:T(8,128)}, u32[]{:S(2)}) copy-start(f32[256,256]{1,0:T(8,128)} %copy.19) | copy-start | bytes 786436
  372.9 18.5 %copy-start.5 = (f32[256,256]{1,0:T(8,128)S(1)}, f32[256,256]{1,0:T(8,128)}, u32[]{:S(2)}) copy-start(f32[256,256]{1,0:T(8,128)} %get-tuple-element.56) | copy-start | bytes 786436
  372.9 18.5 %copy-start.6 = (f32[256,256]{1,0:T(8,128)S(1)}, f32[256,256]{1,0:T(8,128)}, u32[]{:S(2)}) copy-start(f32[256,256]{1,0:T(8,128)} %get-tuple-element.54) | copy-start | bytes 786436
  391.3 1.9 copy-start.2
  393.2 25.4 %copy-start.1 = (f32[2048,768]{1,0:T(8,128)}, f32[2048,768]{1,0:T(8,128)S(1)}, u32[]{:S(2)}) copy-start(f32[2048,768]{1,0:T(8,128)S(1)} %fusion.7) | copy-start | bytes 18874372
Sparse Core Ops, SparseCore 0:
  10.7 72.0 all-reduce.7
  86.7 137.6 all-reduce.5

commit v3 on v2

--- a/solution.py
+++ b/solution.py
@@ -5,6 +5,14 @@
 
 BLOCK = 256
 STEPS = 3
+
+
+def pick(received, index, count, want):
+    total = None
+    for shift, part in enumerate(received):
+        term = jnp.where((index - shift) % count == want, part, jnp.float32(0.0))
+        total = term if total is None else total + term
+    return total
 
 
 def gather_corner(kernel, row_index, col_index):
@@ -19,16 +27,29 @@
             for b in range(a + 1)
         ]
         heard.append(lax.ppermute(piece, ("row", "col"), pairs))
-    heard = jnp.stack(heard)
-    blocks = []
+    bands = []
     for a in range(STEPS):
-        band = jnp.concatenate([heard[(col_index - b) % col_count] for b in range(a + 1)], axis=1)
-        down = [band]
+        band = jnp.concatenate([pick(heard, col_index, col_count, b) for b in range(a + 1)], axis=1)
+        bands.append(jnp.pad(band, ((0, 0), (0, (STEPS - 1 - a) * BLOCK))))
+    groups = [[0], list(range(1, STEPS))]
+    blocks = [None] * STEPS
+    for group in groups:
+        width = (max(group) + 1) * BLOCK
+        mine = None
+        for a in group:
+            term = jnp.where(row_index == a, bands[a][:, :width], jnp.float32(0.0))
+            mine = term if mine is None else mine + term
+        down = [mine]
         for shift in range(1, row_count):
-            pairs = [(a * col_count + q, ((a + shift) % row_count) * col_count + q) for q in range(col_count)]
-            down.append(lax.ppermute(band, ("row", "col"), pairs))
-        band = jnp.stack(down)[(row_index - a) % row_count]
-        blocks.append([band[:, b * BLOCK:(b + 1) * BLOCK] for b in range(a + 1)])
+            pairs = [
+                (a * col_count + q, ((a + shift) % row_count) * col_count + q)
+                for a in group
+                for q in range(col_count)
+            ]
+            down.append(lax.ppermute(mine, ("row", "col"), pairs))
+        for a in group:
+            band = pick(down, row_index, row_count, a)
+            blocks[a] = [band[:, b * BLOCK:(b + 1) * BLOCK] for b in range(a + 1)]
     return blocks
 
 

time: 431 us -> 401 us (0.930)
  the two profiles are of different devices: /device:TPU:1 before, /device:TPU:10 now
where the time goes in v3:
time: 401 us; the launch traced here: 396 us
  other arithmetic  180 us (45%)
  matrix products  70.1 us (17%)
  starting transfers between devices  53.4 us (13%)
  waiting for transfers between devices  41.9 us (10%)
  local copies, waits for them, and re-layouts  31.2 us (8%)
  between operations  19.1 us (5%)
    another operation x20, other arithmetic, factor_corner(): lower[k][k] = jnp.linalg.cholesky(schur)  104 us
    another operation x8, other arithmetic, factor_corner(): jax.scipy.linalg.solve_triangular(lower[k][k], eye, lower=True)  63.8 us
    ppermute x14, starting transfers between devices, gather_corner(): down.append(lax.ppermute(mine, ('row', 'col'), pairs))  40.6 us
    ppermute x15, waiting for transfers between devices, gather_corner(): heard.append(lax.ppermute(piece, ('row', 'col'), pairs))  27.1 us
    dot_general x1, matrix products, shards(): lax.dot_general(panels, across, (((1,), (1,)), ((), ())), precision=lax.P...  25.6 us
    dot_general x1, matrix products, shards(): lax.dot_general(band_cols, inverse, (((1,), (1,)), ((), ())), precision=l...  18.4 us
    another operation x37, local copies, waits for them, and re-layouts, factor_corner(): jax.scipy.linalg.solve_triangular(lower[k][k], eye, lower=True)  15.8 us
    ppermute x14, waiting for transfers between devices, gather_corner(): down.append(lax.ppermute(mine, ('row', 'col'), pairs))  14.7 us
  transfers between devices with their start and end apart: 31, of which 5 were waited for; matrix products, arithmetic and copies ran while one was open for 57% of the time, Pallas kernels for 0%

profile of v3, /device:TPU:10, one launch (start us, length us, event | category | flops | bytes accessed | tf_op | source)
XLA Modules:
  0.0 395.8 jit_solution(16086340478500500671)
XLA Ops:
  7.6 1.3 select_dynamic-update-slice_fusion.1
  9.0 1.7 copy-done
  10.7 1.0 slice.62
  18.7 3.1 broadcast_in_dim.151
  21.8 3.1 select_dynamic-update-slice_fusion
  25.6 1.3 collective-permute-start.3
  26.9 1.3 collective-permute-start.2
  28.3 1.3 collective-permute-start.1
  29.6 1.4 collective-permute-start
  31.0 23.9 %collective-permute-done.3 = f32[256,256]{0,1:T(8,128)} collective-permute-done((f32[256,256]{0,1:T(8,128)S(1)}, f32[256,256]{0,1:T(8,128)}, u32[]{:S(2)}, u32[]{:S(2)}) %collective-permute-start.3) | collective-permute-done | bytes 262176 | tf_op jit(solution)/shard_map/ppermute | solution.py:29
  54.9 2.1 collective-permute-done.2
  57.0 1.1 collective-permute-done.1
  58.0 1.3 broadcast_select_fusion
  62.8 1.3 select_add_fusion.3
  64.0 1.3 collective-permute-start.16
  66.0 1.3 select_add_fusion.2
  67.4 16.3 %collective-permute-start.28 = (f32[256,768]{0,1:T(8,128)S(1)}, f32[256,768]{0,1:T(8,128)S(1)}, u32[]{:S(2)}, u32[]{:S(2)}) collective-permute-start(f32[256,768]{0,1:T(8,128)S(1)} %fusion.4), channel_id=1, source_target_pairs={{16,0},{17,1},{18,2},{19,3},{20,4},{21,5},{22,6},{23,7},{24,8},{25... | collective-permute-start | bytes 2359304 | tf_op jit(solution)/shard_map/ppermute | solution.py:49
  83.7 7.8 %collective-permute-start.27 = (f32[256,768]{0,1:T(8,128)S(1)}, f32[256,768]{0,1:T(8,128)S(1)}, u32[]{:S(2)}, u32[]{:S(2)}) collective-permute-start(f32[256,768]{0,1:T(8,128)S(1)} %fusion.4), channel_id=1, source_target_pairs={{16,112},{17,113},{18,114},{19,115},{20,116},{21,117},{22,118},{23... | collective-permute-start | bytes 2359304 | tf_op jit(solution)/shard_map/ppermute | solution.py:49
  91.6 2.2 collective-permute-start.26
  93.7 2.2 collective-permute-start.25
  95.9 2.3 collective-permute-start.24
  98.6 11.7 %cholesky.172 = f32[128,128]{1,0:T(8,128)S(1)} custom-call(f32[128,128]{1,0:T(8,128)S(1)} %cholesky.270), custom_call_target="Cholesky" | custom-call | tf_op jit(solution)/shard_map/jit(cholesky)/cholesky | solution.py:88
  110.4 9.8 %custom-call.15 = f32[1,128,128]{1,2,0:T(8,128)S(1)} custom-call(f32[1,128,128]{2,1,0:T(8,128)S(1)} %get-tuple-element.82), custom_call_target="InvertDiagBlocksLowerTriangular" | custom-call | tf_op jit(solution)/shard_map/jit(cholesky)/cholesky | solution.py:88
  120.8 11.7 %cholesky.189 = f32[128,128]{1,0:T(8,128)S(1)} custom-call(f32[128,128]{1,0:T(8,128)S(1)} %convolution_subtract_fusion.5), custom_call_target="Cholesky" | custom-call | tf_op jit(solution)/shard_map/jit(cholesky)/cholesky | solution.py:88
  132.7 0.7 compare_reduce_fusion.4
  134.8 0.7 fusion.27
  135.6 4.3 %while.6 = (s32[]{:T(128)}, f32[256,256]{0,1:T(8,128)S(1)}, s32[2,2]{1,0:T(2,128)S(1)}, f32[2,128,128]{2,1,0:T(8,128)S(1)}, s32[]{:T(128)}) while((s32[]{:T(128)}, f32[256,256]{0,1:T(8,128)S(1)}, s32[2,2]{1,0:T(2,128)S(1)}, f32[2,128,128]{2,1,0:T(8,128)S(1)}, s32[]{:T(128)}) %tuple.67), condition=%wide.while_cond, body=%wide.while_body.sunk | while | flops 2 | bytes 393329 | solution.py:89
  136.2 1.4 dynamic-slice.17
  138.4 1.4 dynamic-slice.17
  139.9 19.7 %custom-call.16 = f32[2,128,128]{1,2,0:T(8,128)S(1)} custom-call(f32[2,128,128]{2,1,0:T(8,128)S(1)} %get-tuple-element.24), custom_call_target="InvertDiagBlocksLowerTriangular" | custom-call | tf_op jit(solution)/shard_map/jit(_solve_triangular)/triangular_solve | solution.py:89
  159.6 2.2 collective-permute-start.23
  161.8 2.3 collective-permute-start.22
  165.2 0.7 pad_maximum_fusion.2
  165.9 4.4 %collective-permute-done.23 = f32[256,768]{0,1:T(8,128)} collective-permute-done((f32[256,768]{0,1:T(8,128)S(1)}, f32[256,768]{0,1:T(8,128)}, u32[]{:S(2)}, u32[]{:S(2)}) %collective-permute-start.23) | collective-permute-done | bytes 786464 | tf_op jit(solution)/shard_map/ppermute | solution.py:49
  170.4 10.3 %collective-permute-done.22 = f32[256,768]{0,1:T(8,128)} collective-permute-done((f32[256,768]{0,1:T(8,128)S(1)}, f32[256,768]{0,1:T(8,128)}, u32[]{:S(2)}, u32[]{:S(2)}) %collective-permute-start.22) | collective-permute-done | bytes 786464 | tf_op jit(solution)/shard_map/ppermute | solution.py:49
  180.6 1.6 select_add_fusion.1
  183.4 0.8 copy.12
  184.2 1.0 fusion.22
  185.9 11.7 %cholesky.206 = f32[128,128]{1,0:T(8,128)S(1)} custom-call(f32[128,128]{1,0:T(8,128)S(1)} %cholesky.273), custom_call_target="Cholesky" | custom-call | tf_op jit(solution)/shard_map/jit(cholesky)/cholesky | solution.py:88
  197.8 9.8 %custom-call.17 = f32[1,128,128]{1,2,0:T(8,128)S(1)} custom-call(f32[1,128,128]{2,1,0:T(8,128)S(1)} %get-tuple-element.80), custom_call_target="InvertDiagBlocksLowerTriangular" | custom-call | tf_op jit(solution)/shard_map/jit(cholesky)/cholesky | solution.py:88
  207.6 1.1 constant_dynamic-update-slice_fusion.1
  208.8 1.1 convolution_subtract_fusion.4
  209.9 11.9 %cholesky.223 = f32[128,128]{1,0:T(8,128)S(1)} custom-call(f32[128,128]{1,0:T(8,128)S(1)} %convolution_subtract_fusion.4), custom_call_target="Cholesky" | custom-call | tf_op jit(solution)/shard_map/jit(cholesky)/cholesky | solution.py:88
  225.2 1.7 fusion.25
  227.5 5.4 %while.7 = (s32[]{:T(128)}, f32[256,256]{0,1:T(8,128)S(1)}, s32[2,2]{1,0:T(2,128)S(1)}, f32[2,128,128]{2,1,0:T(8,128)}, s32[]{:T(128)}) while((s32[]{:T(128)}, f32[256,256]{0,1:T(8,128)S(1)}, s32[2,2]{1,0:T(2,128)S(1)}, f32[2,128,128]{2,1,0:T(8,128)}, s32[]{:T(128)}) %tuple.80), condition=%wide.while_cond.clone, body=%wide.while_body.clone.sunk | while | flops 2 | bytes 393329 | solution.py:89
  228.2 1.3 dynamic-slice.19
  230.9 1.3 dynamic-slice.19
  232.9 20.5 %custom-call.18 = f32[2,128,128]{1,2,0:T(8,128)S(1)} custom-call(f32[2,128,128]{2,1,0:T(8,128)} %get-tuple-element.25), custom_call_target="InvertDiagBlocksLowerTriangular" | custom-call | tf_op jit(solution)/shard_map/jit(_solve_triangular)/triangular_solve | solution.py:89
  254.7 1.0 convolution_subtract_fusion.1
  255.7 1.0 copy.16
  260.8 11.7 %cholesky.240 = f32[128,128]{1,0:T(8,128)S(1)} custom-call(f32[128,128]{1,0:T(8,128)S(1)} %cholesky.276), custom_call_target="Cholesky" | custom-call | tf_op jit(solution)/shard_map/jit(cholesky)/cholesky | solution.py:88
  272.6 9.8 %custom-call.19 = f32[1,128,128]{1,2,0:T(8,128)S(1)} custom-call(f32[1,128,128]{2,1,0:T(8,128)S(1)} %get-tuple-element.78), custom_call_target="InvertDiagBlocksLowerTriangular" | custom-call | tf_op jit(solution)/shard_map/jit(cholesky)/cholesky | solution.py:88
  283.1 12.1 %cholesky.257 = f32[128,128]{1,0:T(8,128)S(1)} custom-call(f32[128,128]{1,0:T(8,128)S(1)} %convolution_subtract_fusion.3), custom_call_target="Cholesky" | custom-call | tf_op jit(solution)/shard_map/jit(cholesky)/cholesky | solution.py:88
  296.0 0.7 compare_reduce_fusion
  298.1 0.8 fusion.24
  298.8 4.4 %while.8 = (s32[]{:T(128)}, f32[256,256]{0,1:T(8,128)S(1)}, s32[2,2]{1,0:T(2,128)S(1)}, f32[2,128,128]{2,1,0:T(8,128)S(1)}, s32[]{:T(128)}) while((s32[]{:T(128)}, f32[256,256]{0,1:T(8,128)S(1)}, s32[2,2]{1,0:T(2,128)S(1)}, f32[2,128,128]{2,1,0:T(8,128)S(1)}, s32[]{:T(128)}) %tuple.81), condition=%wide.while_cond.clone.1, body=%wide.while_body.clone.1.sunk | while | flops 2 | bytes 393329 | solution.py:89
  299.5 1.4 dynamic-slice.21
  301.7 1.4 dynamic-slice.21
  303.2 19.7 %custom-call.20 = f32[2,128,128]{1,2,0:T(8,128)S(1)} custom-call(f32[2,128,128]{2,1,0:T(8,128)S(1)} %get-tuple-element.26), custom_call_target="InvertDiagBlocksLowerTriangular" | custom-call | tf_op jit(solution)/shard_map/jit(_solve_triangular)/triangular_solve | solution.py:89
  328.3 10.8 %fusion.36 = f32[1024,768]{1,0:T(8,128)} fusion(f32[768,1024]{1,0:T(8,128)} %all-reduce.9.cloned.1.call-done, f32[256,256]{0,1:T(8,128)S(1)} %broadcast_in_dim.153, f32[256,256]{0,1:T(8,128)S(1)} %copy-done.9, f32[128,256]{0,1:T(8,128)S(1)} %fusion.41, f32[128,256]{0,1:T(8,128)S(1)} %copy.24, f32[256,256]{0,1:T(8,128)S(1)} %convolution_negate_fusion, ...), kind=kOutput, calls=%fused_computation.89 | convolution fusion | flops 7253655552 | bytes 8126464 | tf_op jit(solution)/shard_map/dot_general | solution.py:131
  339.1 18.4 %fusion.38 = f32[2048,768]{1,0:T(8,128)S(1)} fusion(f32[2048,768]{1,0:T(8,128)} %all-reduce.7.cloned.1.call-done, f32[256,256]{0,1:T(8,128)S(1)} %broadcast_in_dim.153, f32[256,256]{0,1:T(8,128)S(1)} %copy-done.9, f32[128,256]{0,1:T(8,128)S(1)} %fusion.41, f32[128,256]{0,1:T(8,128)S(1)} %copy.24, f32[256,256]{0,1:T(8,128)S(1)} %convolution_negate_fusion, ...), kind=kOutput, calls=%fused_computation.90 | convolution fusion | flops 14501412864 | bytes 14417920 | tf_op jit(solution)/shard_map/dot_general | solution.py:127
  357.6 2.7 copy-done.1
  362.2 0.9 constant_dynamic-update-slice_fusion.3
  363.1 25.6 %subtract_select_fusion = f32[2048,1024]{1,0:T(8,128)} fusion(f32[2048,1024]{1,0:T(8,128)} %param.4, pred[1024]{0:T(1024)(128)(4,1)S(1)} %fusion.63, pred[2048]{0:T(1024)(128)(4,1)S(1)} %fusion.57, f32[2048,768]{1,0:T(8,128)} %constant_dynamic-update-slice_fusion.3, f32[1024,768]{1,0:T(8,128)} %fusion.36), kind=kOutput, calls=%fused_computation.6 | convolution fusion | flops 19333644288 | bytes 26217472 | tf_op jit(solution)/shard_map/dot_general | solution.py:138
  (169 shorter events, 39.3 us)
Async XLA Ops:
  7.2 321.1 %all-reduce.9.cloned.1.call-start = ((), (), s32[]{:S(2)}) async-start(), calls=%async_computation.1 | async-start | bytes 6291456 | tf_op jit(solution)/shard_map/psum | solution.py:71
  8.9 1.7 copy-start
  10.6 328.5 %all-reduce.7.cloned.1.call-start = ((), (), s32[]{:S(2)}) async-start(), calls=%async_computation | async-start | bytes 12582912 | tf_op jit(solution)/shard_map/psum | solution.py:62
  11.8 3.4 collective-permute-start.14
  12.5 3.4 collective-permute-start.13
  13.2 3.5 collective-permute-start.12
  13.9 3.5 collective-permute-start.11
  14.5 3.5 collective-permute-start.10
  15.2 9.7 %collective-permute-start.9 = (f32[256,256]{0,1:T(8,128)S(1)}, f32[256,256]{0,1:T(8,128)S(1)}, u32[]{:S(2)}, u32[]{:S(2)}) collective-permute-start(f32[256,256]{0,1:T(8,128)S(1)} %copy.37), channel_id=1, source_target_pairs={{0,10},{16,26},{17,27},{32,42},{33,43},{34,44}} | collective-permute-start | bytes 786440 | tf_op jit(solution)/shard_map/ppermute | solution.py:29
  15.9 9.7 %collective-permute-start.8 = (f32[256,256]{0,1:T(8,128)S(1)}, f32[256,256]{0,1:T(8,128)S(1)}, u32[]{:S(2)}, u32[]{:S(2)}) collective-permute-start(f32[256,256]{0,1:T(8,128)S(1)} %copy.37), channel_id=1, source_target_pairs={{0,9},{16,25},{17,26},{32,41},{33,42},{34,43}} | collective-permute-start | bytes 786440 | tf_op jit(solution)/shard_map/ppermute | solution.py:29
  16.6 10.3 %collective-permute-start.7 = (f32[256,256]{0,1:T(8,128)S(1)}, f32[256,256]{0,1:T(8,128)S(1)}, u32[]{:S(2)}, u32[]{:S(2)}) collective-permute-start(f32[256,256]{0,1:T(8,128)S(1)} %copy.37), channel_id=1, source_target_pairs={{0,8},{16,24},{17,25},{32,40},{33,41},{34,42}} | collective-permute-start | bytes 786440 | tf_op jit(solution)/shard_map/ppermute | solution.py:29
  17.3 10.9 %collective-permute-start.6 = (f32[256,256]{0,1:T(8,128)S(1)}, f32[256,256]{0,1:T(8,128)S(1)}, u32[]{:S(2)}, u32[]{:S(2)}) collective-permute-start(f32[256,256]{0,1:T(8,128)S(1)} %copy.37), channel_id=1, source_target_pairs={{0,7},{16,23},{17,24},{32,39},{33,40},{34,41}} | collective-permute-start | bytes 786440 | tf_op jit(solution)/shard_map/ppermute | solution.py:29
  18.0 11.5 %collective-permute-start.5 = (f32[256,256]{0,1:T(8,128)S(1)}, f32[256,256]{0,1:T(8,128)S(1)}, u32[]{:S(2)}, u32[]{:S(2)}) collective-permute-start(f32[256,256]{0,1:T(8,128)S(1)} %copy.37), channel_id=1, source_target_pairs={{0,6},{16,22},{17,23},{32,38},{33,39},{34,40}} | collective-permute-start | bytes 786440 | tf_op jit(solution)/shard_map/ppermute | solution.py:29
  24.9 6.0 %collective-permute-start.4 = (f32[256,256]{0,1:T(8,128)S(1)}, f32[256,256]{0,1:T(8,128)S(1)}, u32[]{:S(2)}, u32[]{:S(2)}) collective-permute-start(f32[256,256]{0,1:T(8,128)S(1)} %copy.37), channel_id=1, source_target_pairs={{0,5},{16,21},{17,22},{32,37},{33,38},{34,39}} | collective-permute-start | bytes 786440 | tf_op jit(solution)/shard_map/ppermute | solution.py:29
  25.6 29.3 %collective-permute-start.3 = (f32[256,256]{0,1:T(8,128)S(1)}, f32[256,256]{0,1:T(8,128)}, u32[]{:S(2)}, u32[]{:S(2)}) collective-permute-start(f32[256,256]{0,1:T(8,128)S(1)} %copy.37), channel_id=1, source_target_pairs={{0,4},{16,20},{17,21},{32,36},{33,37},{34,38}} | collective-permute-start | bytes 786440 | tf_op jit(solution)/shard_map/ppermute | solution.py:29
  26.9 30.0 %collective-permute-start.2 = (f32[256,256]{0,1:T(8,128)S(1)}, f32[256,256]{0,1:T(8,128)}, u32[]{:S(2)}, u32[]{:S(2)}) collective-permute-start(f32[256,256]{0,1:T(8,128)S(1)} %copy.37), channel_id=1, source_target_pairs={{0,3},{16,19},{17,20},{32,35},{33,36},{34,37}} | collective-permute-start | bytes 786440 | tf_op jit(solution)/shard_map/ppermute | solution.py:29
  28.3 29.8 %collective-permute-start.1 = (f32[256,256]{0,1:T(8,128)S(1)}, f32[256,256]{0,1:T(8,128)}, u32[]{:S(2)}, u32[]{:S(2)}) collective-permute-start(f32[256,256]{0,1:T(8,128)S(1)} %copy.37), channel_id=1, source_target_pairs={{0,2},{16,18},{17,19},{32,34},{33,35},{34,36}} | collective-permute-start | bytes 786440 | tf_op jit(solution)/shard_map/ppermute | solution.py:29
  29.6 28.5 %collective-permute-start = (f32[256,256]{0,1:T(8,128)S(1)}, f32[256,256]{0,1:T(8,128)}, u32[]{:S(2)}, u32[]{:S(2)}) collective-permute-start(f32[256,256]{0,1:T(8,128)S(1)} %copy.37), channel_id=1, source_target_pairs={{0,1},{16,17},{17,18},{32,33},{33,34},{34,35}} | collective-permute-start | bytes 786440 | tf_op jit(solution)/shard_map/ppermute | solution.py:29
  59.3 4.7 %collective-permute-start.21 = (f32[256,256]{0,1:T(8,128)S(1)}, f32[256,256]{0,1:T(8,128)S(1)}, u32[]{:S(2)}, u32[]{:S(2)}) collective-permute-start(f32[256,256]{0,1:T(8,128)S(1)} %get-tuple-element.69), channel_id=1, source_target_pairs={{0,112},{1,113},{2,114},{3,115},{4,116},{5,117},{6,118},{7,119},{8... | collective-permute-start | bytes 786440 | tf_op jit(solution)/shard_map/ppermute | solution.py:49
  60.0 5.3 %collective-permute-start.20 = (f32[256,256]{0,1:T(8,128)S(1)}, f32[256,256]{0,1:T(8,128)S(1)}, u32[]{:S(2)}, u32[]{:S(2)}) collective-permute-start(f32[256,256]{0,1:T(8,128)S(1)} %get-tuple-element.69), channel_id=1, source_target_pairs={{0,96},{1,97},{2,98},{3,99},{4,100},{5,101},{6,102},{7,103},{8,104... | collective-permute-start | bytes 786440 | tf_op jit(solution)/shard_map/ppermute | solution.py:49
  60.7 6.7 %collective-permute-start.19 = (f32[256,256]{0,1:T(8,128)S(1)}, f32[256,256]{0,1:T(8,128)S(1)}, u32[]{:S(2)}, u32[]{:S(2)}) collective-permute-start(f32[256,256]{0,1:T(8,128)S(1)} %get-tuple-element.69), channel_id=1, source_target_pairs={{0,80},{1,81},{2,82},{3,83},{4,84},{5,85},{6,86},{7,87},{8,88},{9,... | collective-permute-start | bytes 786440 | tf_op jit(solution)/shard_map/ppermute | solution.py:49
  61.4 22.4 %collective-permute-start.18 = (f32[256,256]{0,1:T(8,128)S(1)}, f32[256,256]{0,1:T(8,128)S(1)}, u32[]{:S(2)}, u32[]{:S(2)}) collective-permute-start(f32[256,256]{0,1:T(8,128)S(1)} %get-tuple-element.69), channel_id=1, source_target_pairs={{0,64},{1,65},{2,66},{3,67},{4,68},{5,69},{6,70},{7,71},{8,72},{9,... | collective-permute-start | bytes 786440 | tf_op jit(solution)/shard_map/ppermute | solution.py:49
  62.1 29.5 %collective-permute-start.17 = (f32[256,256]{0,1:T(8,128)S(1)}, f32[256,256]{0,1:T(8,128)S(1)}, u32[]{:S(2)}, u32[]{:S(2)}) collective-permute-start(f32[256,256]{0,1:T(8,128)S(1)} %get-tuple-element.69), channel_id=1, source_target_pairs={{0,48},{1,49},{2,50},{3,51},{4,52},{5,53},{6,54},{7,55},{8,56},{9,... | collective-permute-start | bytes 786440 | tf_op jit(solution)/shard_map/ppermute | solution.py:49
  64.0 29.7 %collective-permute-start.16 = (f32[256,256]{0,1:T(8,128)S(1)}, f32[256,256]{0,1:T(8,128)S(1)}, u32[]{:S(2)}, u32[]{:S(2)}) collective-permute-start(f32[256,256]{0,1:T(8,128)S(1)} %get-tuple-element.69), channel_id=1, source_target_pairs={{0,32},{1,33},{2,34},{3,35},{4,36},{5,37},{6,38},{7,39},{8,40},{9,... | collective-permute-start | bytes 786440 | tf_op jit(solution)/shard_map/ppermute | solution.py:49
  65.4 30.6 %collective-permute-start.15 = (f32[256,256]{0,1:T(8,128)S(1)}, f32[256,256]{0,1:T(8,128)S(1)}, u32[]{:S(2)}, u32[]{:S(2)}) collective-permute-start(f32[256,256]{0,1:T(8,128)S(1)} %get-tuple-element.69), channel_id=1, source_target_pairs={{0,16},{1,17},{2,18},{3,19},{4,20},{5,21},{6,22},{7,23},{8,24},{9,... | collective-permute-start | bytes 786440 | tf_op jit(solution)/shard_map/ppermute | solution.py:49
  67.4 92.1 %collective-permute-start.28 = (f32[256,768]{0,1:T(8,128)S(1)}, f32[256,768]{0,1:T(8,128)S(1)}, u32[]{:S(2)}, u32[]{:S(2)}) collective-permute-start(f32[256,768]{0,1:T(8,128)S(1)} %fusion.4), channel_id=1, source_target_pairs={{16,0},{17,1},{18,2},{19,3},{20,4},{21,5},{22,6},{23,7},{24,8},{25... | collective-permute-start | bytes 2359304 | tf_op jit(solution)/shard_map/ppermute | solution.py:49
  83.7 78.0 %collective-permute-start.27 = (f32[256,768]{0,1:T(8,128)S(1)}, f32[256,768]{0,1:T(8,128)S(1)}, u32[]{:S(2)}, u32[]{:S(2)}) collective-permute-start(f32[256,768]{0,1:T(8,128)S(1)} %fusion.4), channel_id=1, source_target_pairs={{16,112},{17,113},{18,114},{19,115},{20,116},{21,117},{22,118},{23... | collective-permute-start | bytes 2359304 | tf_op jit(solution)/shard_map/ppermute | solution.py:49
  91.6 74.4 %collective-permute-start.26 = (f32[256,768]{0,1:T(8,128)S(1)}, f32[256,768]{0,1:T(8,128)}, u32[]{:S(2)}, u32[]{:S(2)}) collective-permute-start(f32[256,768]{0,1:T(8,128)S(1)} %fusion.4), channel_id=1, source_target_pairs={{16,96},{17,97},{18,98},{19,99},{20,100},{21,101},{22,102},{23,103... | collective-permute-start | bytes 2359304 | tf_op jit(solution)/shard_map/ppermute | solution.py:49
  93.7 72.2 %collective-permute-start.25 = (f32[256,768]{0,1:T(8,128)S(1)}, f32[256,768]{0,1:T(8,128)}, u32[]{:S(2)}, u32[]{:S(2)}) collective-permute-start(f32[256,768]{0,1:T(8,128)S(1)} %fusion.4), channel_id=1, source_target_pairs={{16,80},{17,81},{18,82},{19,83},{20,84},{21,85},{22,86},{23,87},{2... | collective-permute-start | bytes 2359304 | tf_op jit(solution)/shard_map/ppermute | solution.py:49
  95.9 70.0 %collective-permute-start.24 = (f32[256,768]{0,1:T(8,128)S(1)}, f32[256,768]{0,1:T(8,128)}, u32[]{:S(2)}, u32[]{:S(2)}) collective-permute-start(f32[256,768]{0,1:T(8,128)S(1)} %fusion.4), channel_id=1, source_target_pairs={{16,64},{17,65},{18,66},{19,67},{20,68},{21,69},{22,70},{23,71},{2... | collective-permute-start | bytes 2359304 | tf_op jit(solution)/shard_map/ppermute | solution.py:49
  159.6 10.8 %collective-permute-start.23 = (f32[256,768]{0,1:T(8,128)S(1)}, f32[256,768]{0,1:T(8,128)}, u32[]{:S(2)}, u32[]{:S(2)}) collective-permute-start(f32[256,768]{0,1:T(8,128)S(1)} %fusion.4), channel_id=1, source_target_pairs={{16,48},{17,49},{18,50},{19,51},{20,52},{21,53},{22,54},{23,55},{2... | collective-permute-start | bytes 2359304 | tf_op jit(solution)/shard_map/ppermute | solution.py:49
  161.8 18.9 %collective-permute-start.22 = (f32[256,768]{0,1:T(8,128)S(1)}, f32[256,768]{0,1:T(8,128)}, u32[]{:S(2)}, u32[]{:S(2)}) collective-permute-start(f32[256,768]{0,1:T(8,128)S(1)} %fusion.4), channel_id=1, source_target_pairs={{16,32},{17,33},{18,34},{19,35},{20,36},{21,37},{22,38},{23,39},{2... | collective-permute-start | bytes 2359304 | tf_op jit(solution)/shard_map/ppermute | solution.py:49
  185.2 0.7 copy-start.7
  223.3 0.7 copy-start.3
  253.4 0.7 copy-start.10
  254.0 0.7 copy-start.2
  256.7 1.7 copy-start.8
  256.7 1.7 copy-start.11
  325.3 3.1 copy-start.9
  357.6 2.7 copy-start.1
  360.3 0.9 copy-start.4
  360.3 1.0 copy-start.5
  360.3 1.1 copy-start.6
Sparse Core Ops, SparseCore 0:
  10.9 68.7 all-reduce.8
  83.7 149.2 all-reduce.6

commit v4 on v3

--- a/solution.py
+++ b/solution.py
@@ -76,8 +76,26 @@
     return lax.dot_general(a, b, dims, precision=lax.Precision.HIGHEST, preferred_element_type=jnp.float32)
 
 
+def factor_block(schur):
+    half = schur.shape[0] // 2
+    eye = jnp.eye(half, dtype=jnp.float32)
+    top = jnp.linalg.cholesky(schur[:half, :half])
+    top_inv = jax.scipy.linalg.solve_triangular(top, eye, lower=True)
+    side = mul(schur[half:, :half], top_inv, True)
+    bottom = jnp.linalg.cholesky(schur[half:, half:] - mul(side, side, True))
+    bottom_inv = jax.scipy.linalg.solve_triangular(bottom, eye, lower=True)
+    corner = -mul(bottom_inv, mul(side, top_inv))
+    zero = jnp.zeros((half, half), jnp.float32)
+    factor = jnp.concatenate(
+        [jnp.concatenate([top, zero], axis=1), jnp.concatenate([side, bottom], axis=1)], axis=0
+    )
+    inverse = jnp.concatenate(
+        [jnp.concatenate([top_inv, zero], axis=1), jnp.concatenate([corner, bottom_inv], axis=1)], axis=0
+    )
+    return factor, inverse
+
+
 def factor_corner(blocks):
-    eye = jnp.eye(BLOCK, dtype=jnp.float32)
     zero = jnp.zeros((BLOCK, BLOCK), jnp.float32)
     lower = [[None] * STEPS for _ in range(STEPS)]
     diag_inv = []
@@ -85,8 +103,8 @@
         schur = blocks[k][k]
         for j in range(k):
             schur = schur - mul(lower[k][j], lower[k][j], True)
-        lower[k][k] = jnp.linalg.cholesky(schur)
-        diag_inv.append(jax.scipy.linalg.solve_triangular(lower[k][k], eye, lower=True))
+        lower[k][k], inverse = factor_block(schur)
+        diag_inv.append(inverse)
         for i in range(k + 1, STEPS):
             below = blocks[i][k]
             for j in range(k):

time: 401 us -> 365 us (0.910)
  other arithmetic: 180 us -> 158 us
  local copies, waits for them, and re-layouts: 31.2 us -> 14.6 us
  matrix products: 70.1 us -> 76 us
    another operation x28 -> x30, other arithmetic: 168 us -> 140 us  [the longest x9 37.4 us: factor_block(): bottom = jnp.linalg.cholesky(schur[half:, half:] - mul(side, side, True))]
    another operation x54 -> x3, local copies, waits for them, and re-layouts: 16.6 us -> 0.91 us  [factor_block(): bottom_inv = jax.scipy.linalg.solve_triangular(bottom, eye, lower=True)]
    dot_general x1, matrix products: 10.8 us -> 18.1 us  [shards(): lax.dot_general(band_rows, inverse, (((0,), (1,)), ((), ())), precision=l...]
    another operation x15 -> x6, matrix products: 6.98 us -> 1.65 us  [the longest x3 0.86 us: factor_block(): top_inv = jax.scipy.linalg.solve_triangular(top, eye, lower=True)]
    unnamed x26 -> x58, local copies, waits for them, and re-layouts: 7.89 us -> 2.64 us
    concatenate x0 -> x5, other arithmetic: none -> 4.82 us  [the longest x4 4.08 us: factor_block(): jnp.concatenate([jnp.concatenate([top, zero], axis=1), jnp.concatenate([s...]
    dot_general x0 -> x6, local copies, waits for them, and re-layouts: none -> 4.07 us  [mul(): lax.dot_general(a, b, dims, precision=lax.Precision.HIGHEST, preferred_el...]
    dot_general x14 -> x26, matrix products: 8.35 us -> 12.1 us  [mul(): lax.dot_general(a, b, dims, precision=lax.Precision.HIGHEST, preferred_el...]
  transfers between devices with their start and end apart: 31 -> 31, of which waited for: 5 -> 5; matrix products, arithmetic and copies ran while one was open for 57% -> 55% of each run, Pallas kernels for 0% -> 0%
where the time goes in v4:
time: 365 us; the launch traced here: 359 us
  other arithmetic  158 us (43%)
  matrix products  76 us (21%)
  starting transfers between devices  49.7 us (14%)
  waiting for transfers between devices  44.4 us (12%)
  between operations  16.1 us (4%)
  local copies, waits for them, and re-layouts  14.6 us (4%)
    ppermute x14, starting transfers between devices, gather_corner(): down.append(lax.ppermute(mine, ('row', 'col'), pairs))  37.6 us
    another operation x9, other arithmetic, factor_block(): bottom = jnp.linalg.cholesky(schur[half:, half:] - mul(side, side, True))  37.4 us
    another operation x9, other arithmetic, factor_block(): top = jnp.linalg.cholesky(schur[:half, :half])  37.3 us
    another operation x6, other arithmetic, factor_block(): bottom_inv = jax.scipy.linalg.solve_triangular(bottom, eye, lower=True)  33 us
    another operation x6, other arithmetic, factor_block(): top_inv = jax.scipy.linalg.solve_triangular(top, eye, lower=True)  32.8 us
    ppermute x15, waiting for transfers between devices, gather_corner(): heard.append(lax.ppermute(piece, ('row', 'col'), pairs))  29.8 us
    dot_general x1, matrix products, shards(): lax.dot_general(panels, across, (((1,), (1,)), ((), ())), precision=lax.P...  25.4 us
    dot_general x1, matrix products, shards(): lax.dot_general(band_cols, inverse, (((1,), (1,)), ((), ())), precision=l...  18.8 us
  transfers between devices with their start and end apart: 31, of which 5 were waited for; matrix products, arithmetic and copies ran while one was open for 55% of the time, Pallas kernels for 0%

profile of v4, /device:TPU:10, one launch (start us, length us, event | category | flops | bytes accessed | tf_op | source)
XLA Modules:
  0.0 359.1 jit_solution(7230190084783252554)
XLA Ops:
  7.6 1.3 select_dynamic-update-slice_fusion.1
  8.9 1.7 copy-done
  10.7 1.0 slice.64
  12.3 0.7 collective-permute-start.13
  13.0 0.7 collective-permute-start.12
  13.7 0.7 collective-permute-start.11
  15.1 3.1 broadcast_in_dim.151
  18.2 3.0 select_dynamic-update-slice_fusion
  25.3 1.0 fusion.4
  27.0 1.3 collective-permute-start.3
  28.3 1.3 collective-permute-start.2
  29.6 1.3 collective-permute-start.1
  31.6 1.3 iota_compare_fusion
  33.0 22.8 %collective-permute-done.3 = f32[256,256]{1,0:T(8,128)S(1)} collective-permute-done((f32[256,256]{1,0:T(8,128)S(1)}, f32[256,256]{1,0:T(8,128)S(1)}, u32[]{:S(2)}, u32[]{:S(2)}) %collective-permute-start.3) | collective-permute-done | bytes 262176 | tf_op jit(solution)/shard_map/ppermute | solution.py:29
  55.8 3.7 %collective-permute-done.2 = f32[256,256]{1,0:T(8,128)S(1)} collective-permute-done((f32[256,256]{1,0:T(8,128)S(1)}, f32[256,256]{1,0:T(8,128)S(1)}, u32[]{:S(2)}, u32[]{:S(2)}) %collective-permute-start.2) | collective-permute-done | bytes 262176 | tf_op jit(solution)/shard_map/ppermute | solution.py:29
  59.4 3.3 collective-permute-done.1
  62.8 1.3 broadcast_select_fusion
  67.5 1.3 select_add_fusion.3
  68.8 1.3 collective-permute-start.16
  70.8 1.3 select_add_fusion.2
  72.1 13.1 %collective-permute-start.28 = (f32[256,768]{1,0:T(8,128)S(1)}, f32[256,768]{1,0:T(8,128)S(1)}, u32[]{:S(2)}, u32[]{:S(2)}) collective-permute-start(f32[256,768]{1,0:T(8,128)S(1)} %fusion.7), channel_id=1, source_target_pairs={{16,0},{17,1},{18,2},{19,3},{20,4},{21,5},{22,6},{23,7},{24,8},{25... | collective-permute-start | bytes 2359304 | tf_op jit(solution)/shard_map/ppermute | solution.py:49
  85.3 8.3 %collective-permute-start.27 = (f32[256,768]{1,0:T(8,128)S(1)}, f32[256,768]{1,0:T(8,128)S(1)}, u32[]{:S(2)}, u32[]{:S(2)}) collective-permute-start(f32[256,768]{1,0:T(8,128)S(1)} %fusion.7), channel_id=1, source_target_pairs={{16,112},{17,113},{18,114},{19,115},{20,116},{21,117},{22,118},{23... | collective-permute-start | bytes 2359304 | tf_op jit(solution)/shard_map/ppermute | solution.py:49
  93.6 2.2 collective-permute-start.26
  95.8 2.2 collective-permute-start.25
  98.0 2.4 collective-permute-start.24
  100.7 11.7 %cholesky.104 = f32[128,128]{1,0:T(8,128)S(1)} custom-call(f32[128,128]{1,0:T(8,128)S(1)} %copy.4), custom_call_target="Cholesky" | custom-call | tf_op jit(solution)/shard_map/jit(cholesky)/cholesky | solution.py:82
  113.8 9.8 %custom-call.10 = f32[1,128,128]{1,2,0:T(8,128)S(1)} custom-call(f32[1,128,128]{2,1,0:T(8,128)S(1)} %get-tuple-element.14), custom_call_target="InvertDiagBlocksLowerTriangular" | custom-call | tf_op jit(solution)/shard_map/jit(_solve_triangular)/triangular_solve | solution.py:83
  124.7 11.7 %cholesky.115 = f32[128,128]{1,0:T(8,128)S(1)} custom-call(f32[128,128]{1,0:T(8,128)S(1)} %copy.6), custom_call_target="Cholesky" | custom-call | tf_op jit(solution)/shard_map/jit(cholesky)/cholesky | solution.py:85
  137.8 10.2 %custom-call.11 = f32[1,128,128]{1,2,0:T(8,128)S(1)} custom-call(f32[1,128,128]{2,1,0:T(8,128)S(1)} %get-tuple-element.12), custom_call_target="InvertDiagBlocksLowerTriangular" | custom-call | tf_op jit(solution)/shard_map/jit(_solve_triangular)/triangular_solve | solution.py:86
  148.0 2.2 collective-permute-start.23
  150.2 1.9 collective-permute-start.22
  153.2 0.7 select_maximum_fusion.1
  154.0 0.7 select_maximum_fusion
  154.7 4.1 %collective-permute-done.23 = f32[256,768]{1,0:T(8,128)} collective-permute-done((f32[256,768]{1,0:T(8,128)S(1)}, f32[256,768]{1,0:T(8,128)}, u32[]{:S(2)}, u32[]{:S(2)}) %collective-permute-start.23) | collective-permute-done | bytes 786464 | tf_op jit(solution)/shard_map/ppermute | solution.py:49
  158.8 10.3 %collective-permute-done.22 = f32[256,768]{1,0:T(8,128)} collective-permute-done((f32[256,768]{1,0:T(8,128)S(1)}, f32[256,768]{1,0:T(8,128)}, u32[]{:S(2)}, u32[]{:S(2)}) %collective-permute-start.22) | collective-permute-done | bytes 786464 | tf_op jit(solution)/shard_map/ppermute | solution.py:49
  169.1 1.5 select_add_fusion.1
  171.9 11.7 %cholesky.126 = f32[128,128]{1,0:T(8,128)S(1)} custom-call(f32[128,128]{1,0:T(8,128)S(1)} %copy.10), custom_call_target="Cholesky" | custom-call | tf_op jit(solution)/shard_map/jit(cholesky)/cholesky | solution.py:82
  184.3 1.2 select_bitcast_fusion.3
  185.5 9.8 %custom-call.12 = f32[1,128,128]{1,2,0:T(8,128)S(1)} custom-call(f32[1,128,128]{2,1,0:T(8,128)S(1)} %get-tuple-element.10), custom_call_target="InvertDiagBlocksLowerTriangular" | custom-call | tf_op jit(solution)/shard_map/jit(_solve_triangular)/triangular_solve | solution.py:83
  196.9 0.9 copy-done.2
  198.4 11.9 %cholesky.137 = f32[128,128]{1,0:T(8,128)S(1)} custom-call(f32[128,128]{1,0:T(8,128)S(1)} %copy.12), custom_call_target="Cholesky" | custom-call | tf_op jit(solution)/shard_map/jit(cholesky)/cholesky | solution.py:85
  211.0 1.3 select_bitcast_fusion.2
  212.2 9.8 %custom-call.13 = f32[1,128,128]{1,2,0:T(8,128)S(1)} custom-call(f32[1,128,128]{2,1,0:T(8,128)S(1)} %get-tuple-element.8), custom_call_target="InvertDiagBlocksLowerTriangular" | custom-call | tf_op jit(solution)/shard_map/jit(_solve_triangular)/triangular_solve | solution.py:86
  222.7 0.9 copy.26
  223.6 0.7 copy.25
  224.3 0.9 copy.28
  226.2 0.8 copy.29
  228.5 11.7 %cholesky.148 = f32[128,128]{1,0:T(8,128)S(1)} custom-call(f32[128,128]{1,0:T(8,128)S(1)} %copy.17), custom_call_target="Cholesky" | custom-call | tf_op jit(solution)/shard_map/jit(cholesky)/cholesky | solution.py:82
  240.2 0.7 compare_reduce_fusion.1
  241.0 1.3 select_bitcast_fusion.1
  242.3 10.0 %custom-call.14 = f32[1,128,128]{1,2,0:T(8,128)S(1)} custom-call(f32[1,128,128]{2,1,0:T(8,128)S(1)} %get-tuple-element.6), custom_call_target="InvertDiagBlocksLowerTriangular" | custom-call | tf_op jit(solution)/shard_map/jit(_solve_triangular)/triangular_solve | solution.py:83
  253.5 0.7 copy.27
  254.7 11.7 %cholesky.159 = f32[128,128]{1,0:T(8,128)S(1)} custom-call(f32[128,128]{1,0:T(8,128)S(1)} %copy.19), custom_call_target="Cholesky" | custom-call | tf_op jit(solution)/shard_map/jit(cholesky)/cholesky | solution.py:85
  267.1 1.2 select_bitcast_fusion
  268.3 9.8 %custom-call.15 = f32[1,128,128]{1,2,0:T(8,128)S(1)} custom-call(f32[1,128,128]{2,1,0:T(8,128)S(1)} %get-tuple-element.4), custom_call_target="InvertDiagBlocksLowerTriangular" | custom-call | tf_op jit(solution)/shard_map/jit(_solve_triangular)/triangular_solve | solution.py:86
  278.4 0.7 copy.21
  279.2 1.1 pad_select_fusion
  280.9 1.4 fusion.44
  284.0 1.1 convolution_negate_fusion
  286.1 0.8 broadcast_in_dim.153
  286.9 18.1 %fusion.83 = f32[1024,768]{1,0:T(8,128)} fusion(f32[768,1024]{1,0:T(8,128)} %all-reduce.14.cloned.1.call-done, f32[256,256]{1,0:T(8,128)} %broadcast_in_dim.153, f32[256,256]{1,0:T(8,128)} %select_maximum_fusion.1, f32[128,128]{1,0:T(8,128)S(1)} %copy-done.20, f32[128,128]{1,0:T(8,128)S(1)} %convolution_negate_fusion.3, f32[128,256]{1,0:T(8,128)S(1)} %copy-done.6, ...), kind=kOutput, calls=%fused_computation.177 | convolution fusion | flops 7254835200 | bytes 8126464 | tf_op jit(solution)/shard_map/dot_general | solution.py:149
  305.2 18.8 %fusion.85 = f32[2048,768]{1,0:T(8,128)S(1)} fusion(f32[2048,768]{1,0:T(8,128)} %all-reduce.12.cloned.1.call-done, f32[256,256]{1,0:T(8,128)} %broadcast_in_dim.153, f32[256,256]{1,0:T(8,128)} %select_maximum_fusion.1, f32[128,128]{1,0:T(8,128)S(1)} %copy-done.20, f32[128,128]{1,0:T(8,128)S(1)} %convolution_negate_fusion.3, f32[128,256]{1,0:T(8,128)S(1)} %copy-done.6, ...), kind=kOutput, calls=%fused_computation.178 | convolution fusion | flops 14502592512 | bytes 14417920 | tf_op jit(solution)/shard_map/dot_general | solution.py:145
  324.0 2.5 fusion.15
  326.6 25.4 %subtract_select_fusion = f32[2048,1024]{1,0:T(8,128)} fusion(f32[2048,1024]{1,0:T(8,128)} %param.4, pred[1024]{0:T(1024)(128)(4,1)S(1)} %fusion.72, pred[2048]{0:T(1024)(128)(4,1)S(1)} %fusion.66, f32[2048,768]{1,0:T(8,128)S(1)} %fusion.15, f32[1024,768]{1,0:T(8,128)S(1)} %copy-done.4), kind=kOutput, calls=%fused_computation | convolution fusion | flops 19333644288 | bytes 26217472 | tf_op jit(solution)/shard_map/dot_general | solution.py:156
  (176 shorter events, 29.6 us)
Async XLA Ops:
  7.2 279.0 %all-reduce.14.cloned.1.call-start = ((), (), s32[]{:S(2)}) async-start(), calls=%async_computation.1 | async-start | bytes 6291456 | tf_op jit(solution)/shard_map/psum | solution.py:71
  8.9 1.7 copy-start
  10.6 294.5 %all-reduce.12.cloned.1.call-start = ((), (), s32[]{:S(2)}) async-start(), calls=%async_computation | async-start | bytes 12582912 | tf_op jit(solution)/shard_map/psum | solution.py:62
  11.6 10.2 %collective-permute-start.14 = (f32[256,256]{1,0:T(8,128)S(1)}, f32[256,256]{1,0:T(8,128)S(1)}, u32[]{:S(2)}, u32[]{:S(2)}) collective-permute-start(f32[256,256]{1,0:T(8,128)S(1)} %slice.64), channel_id=1, source_target_pairs={{0,15},{16,31},{17,16},{32,47},{33,32},{34,33}} | collective-permute-start | bytes 786440 | tf_op jit(solution)/shard_map/ppermute | solution.py:29
  12.3 10.2 %collective-permute-start.13 = (f32[256,256]{1,0:T(8,128)S(1)}, f32[256,256]{1,0:T(8,128)S(1)}, u32[]{:S(2)}, u32[]{:S(2)}) collective-permute-start(f32[256,256]{1,0:T(8,128)S(1)} %slice.64), channel_id=1, source_target_pairs={{0,14},{16,30},{17,31},{32,46},{33,47},{34,32}} | collective-permute-start | bytes 786440 | tf_op jit(solution)/shard_map/ppermute | solution.py:29
  13.0 10.3 %collective-permute-start.12 = (f32[256,256]{1,0:T(8,128)S(1)}, f32[256,256]{1,0:T(8,128)S(1)}, u32[]{:S(2)}, u32[]{:S(2)}) collective-permute-start(f32[256,256]{1,0:T(8,128)S(1)} %slice.64), channel_id=1, source_target_pairs={{0,13},{16,29},{17,30},{32,45},{33,46},{34,47}} | collective-permute-start | bytes 786440 | tf_op jit(solution)/shard_map/ppermute | solution.py:29
  13.7 10.3 %collective-permute-start.11 = (f32[256,256]{1,0:T(8,128)S(1)}, f32[256,256]{1,0:T(8,128)S(1)}, u32[]{:S(2)}, u32[]{:S(2)}) collective-permute-start(f32[256,256]{1,0:T(8,128)S(1)} %slice.64), channel_id=1, source_target_pairs={{0,12},{16,28},{17,29},{32,44},{33,45},{34,46}} | collective-permute-start | bytes 786440 | tf_op jit(solution)/shard_map/ppermute | solution.py:29
  14.4 10.3 %collective-permute-start.10 = (f32[256,256]{1,0:T(8,128)S(1)}, f32[256,256]{1,0:T(8,128)S(1)}, u32[]{:S(2)}, u32[]{:S(2)}) collective-permute-start(f32[256,256]{1,0:T(8,128)S(1)} %slice.64), channel_id=1, source_target_pairs={{0,11},{16,27},{17,28},{32,43},{33,44},{34,45}} | collective-permute-start | bytes 786440 | tf_op jit(solution)/shard_map/ppermute | solution.py:29
  21.9 4.5 %collective-permute-start.9 = (f32[256,256]{1,0:T(8,128)S(1)}, f32[256,256]{1,0:T(8,128)S(1)}, u32[]{:S(2)}, u32[]{:S(2)}) collective-permute-start(f32[256,256]{1,0:T(8,128)S(1)} %slice.64), channel_id=1, source_target_pairs={{0,10},{16,26},{17,27},{32,42},{33,43},{34,44}} | collective-permute-start | bytes 786440 | tf_op jit(solution)/shard_map/ppermute | solution.py:29
  22.6 4.4 %collective-permute-start.8 = (f32[256,256]{1,0:T(8,128)S(1)}, f32[256,256]{1,0:T(8,128)S(1)}, u32[]{:S(2)}, u32[]{:S(2)}) collective-permute-start(f32[256,256]{1,0:T(8,128)S(1)} %slice.64), channel_id=1, source_target_pairs={{0,9},{16,25},{17,26},{32,41},{33,42},{34,43}} | collective-permute-start | bytes 786440 | tf_op jit(solution)/shard_map/ppermute | solution.py:29
  23.3 5.1 %collective-permute-start.7 = (f32[256,256]{1,0:T(8,128)S(1)}, f32[256,256]{1,0:T(8,128)S(1)}, u32[]{:S(2)}, u32[]{:S(2)}) collective-permute-start(f32[256,256]{1,0:T(8,128)S(1)} %slice.64), channel_id=1, source_target_pairs={{0,8},{16,24},{17,25},{32,40},{33,41},{34,42}} | collective-permute-start | bytes 786440 | tf_op jit(solution)/shard_map/ppermute | solution.py:29
  24.0 5.7 %collective-permute-start.6 = (f32[256,256]{1,0:T(8,128)S(1)}, f32[256,256]{1,0:T(8,128)S(1)}, u32[]{:S(2)}, u32[]{:S(2)}) collective-permute-start(f32[256,256]{1,0:T(8,128)S(1)} %slice.64), channel_id=1, source_target_pairs={{0,7},{16,23},{17,24},{32,39},{33,40},{34,41}} | collective-permute-start | bytes 786440 | tf_op jit(solution)/shard_map/ppermute | solution.py:29
  24.6 6.3 %collective-permute-start.5 = (f32[256,256]{1,0:T(8,128)S(1)}, f32[256,256]{1,0:T(8,128)S(1)}, u32[]{:S(2)}, u32[]{:S(2)}) collective-permute-start(f32[256,256]{1,0:T(8,128)S(1)} %slice.64), channel_id=1, source_target_pairs={{0,6},{16,22},{17,23},{32,38},{33,39},{34,40}} | collective-permute-start | bytes 786440 | tf_op jit(solution)/shard_map/ppermute | solution.py:29
  26.3 6.6 %collective-permute-start.4 = (f32[256,256]{1,0:T(8,128)S(1)}, f32[256,256]{1,0:T(8,128)S(1)}, u32[]{:S(2)}, u32[]{:S(2)}) collective-permute-start(f32[256,256]{1,0:T(8,128)S(1)} %slice.64), channel_id=1, source_target_pairs={{0,5},{16,21},{17,22},{32,37},{33,38},{34,39}} | collective-permute-start | bytes 786440 | tf_op jit(solution)/shard_map/ppermute | solution.py:29
  27.0 28.8 %collective-permute-start.3 = (f32[256,256]{1,0:T(8,128)S(1)}, f32[256,256]{1,0:T(8,128)S(1)}, u32[]{:S(2)}, u32[]{:S(2)}) collective-permute-start(f32[256,256]{1,0:T(8,128)S(1)} %slice.64), channel_id=1, source_target_pairs={{0,4},{16,20},{17,21},{32,36},{33,37},{34,38}} | collective-permute-start | bytes 786440 | tf_op jit(solution)/shard_map/ppermute | solution.py:29
  28.3 31.1 %collective-permute-start.2 = (f32[256,256]{1,0:T(8,128)S(1)}, f32[256,256]{1,0:T(8,128)S(1)}, u32[]{:S(2)}, u32[]{:S(2)}) collective-permute-start(f32[256,256]{1,0:T(8,128)S(1)} %slice.64), channel_id=1, source_target_pairs={{0,3},{16,19},{17,20},{32,35},{33,36},{34,37}} | collective-permute-start | bytes 786440 | tf_op jit(solution)/shard_map/ppermute | solution.py:29
  29.6 33.2 %collective-permute-start.1 = (f32[256,256]{1,0:T(8,128)S(1)}, f32[256,256]{1,0:T(8,128)S(1)}, u32[]{:S(2)}, u32[]{:S(2)}) collective-permute-start(f32[256,256]{1,0:T(8,128)S(1)} %slice.64), channel_id=1, source_target_pairs={{0,2},{16,18},{17,19},{32,34},{33,35},{34,36}} | collective-permute-start | bytes 786440 | tf_op jit(solution)/shard_map/ppermute | solution.py:29
  30.9 31.8 %collective-permute-start = (f32[256,256]{1,0:T(8,128)S(1)}, f32[256,256]{1,0:T(8,128)S(1)}, u32[]{:S(2)}, u32[]{:S(2)}) collective-permute-start(f32[256,256]{1,0:T(8,128)S(1)} %slice.64), channel_id=1, source_target_pairs={{0,1},{16,17},{17,18},{32,33},{33,34},{34,35}} | collective-permute-start | bytes 786440 | tf_op jit(solution)/shard_map/ppermute | solution.py:29
  64.1 4.7 %collective-permute-start.21 = (f32[256,256]{1,0:T(8,128)S(1)}, f32[256,256]{1,0:T(8,128)S(1)}, u32[]{:S(2)}, u32[]{:S(2)}) collective-permute-start(f32[256,256]{1,0:T(8,128)S(1)} %get-tuple-element.16), channel_id=1, source_target_pairs={{0,112},{1,113},{2,114},{3,115},{4,116},{5,117},{6,118},{7,119},{8... | collective-permute-start | bytes 786440 | tf_op jit(solution)/shard_map/ppermute | solution.py:49
  64.7 5.3 %collective-permute-start.20 = (f32[256,256]{1,0:T(8,128)S(1)}, f32[256,256]{1,0:T(8,128)S(1)}, u32[]{:S(2)}, u32[]{:S(2)}) collective-permute-start(f32[256,256]{1,0:T(8,128)S(1)} %get-tuple-element.16), channel_id=1, source_target_pairs={{0,96},{1,97},{2,98},{3,99},{4,100},{5,101},{6,102},{7,103},{8,104... | collective-permute-start | bytes 786440 | tf_op jit(solution)/shard_map/ppermute | solution.py:49
  65.4 6.7 %collective-permute-start.19 = (f32[256,256]{1,0:T(8,128)S(1)}, f32[256,256]{1,0:T(8,128)S(1)}, u32[]{:S(2)}, u32[]{:S(2)}) collective-permute-start(f32[256,256]{1,0:T(8,128)S(1)} %get-tuple-element.16), channel_id=1, source_target_pairs={{0,80},{1,81},{2,82},{3,83},{4,84},{5,85},{6,86},{7,87},{8,88},{9,... | collective-permute-start | bytes 786440 | tf_op jit(solution)/shard_map/ppermute | solution.py:49
  66.1 19.2 %collective-permute-start.18 = (f32[256,256]{1,0:T(8,128)S(1)}, f32[256,256]{1,0:T(8,128)S(1)}, u32[]{:S(2)}, u32[]{:S(2)}) collective-permute-start(f32[256,256]{1,0:T(8,128)S(1)} %get-tuple-element.16), channel_id=1, source_target_pairs={{0,64},{1,65},{2,66},{3,67},{4,68},{5,69},{6,70},{7,71},{8,72},{9,... | collective-permute-start | bytes 786440 | tf_op jit(solution)/shard_map/ppermute | solution.py:49
  66.8 26.8 %collective-permute-start.17 = (f32[256,256]{1,0:T(8,128)S(1)}, f32[256,256]{1,0:T(8,128)S(1)}, u32[]{:S(2)}, u32[]{:S(2)}) collective-permute-start(f32[256,256]{1,0:T(8,128)S(1)} %get-tuple-element.16), channel_id=1, source_target_pairs={{0,48},{1,49},{2,50},{3,51},{4,52},{5,53},{6,54},{7,55},{8,56},{9,... | collective-permute-start | bytes 786440 | tf_op jit(solution)/shard_map/ppermute | solution.py:49
  68.8 27.0 %collective-permute-start.16 = (f32[256,256]{1,0:T(8,128)S(1)}, f32[256,256]{1,0:T(8,128)S(1)}, u32[]{:S(2)}, u32[]{:S(2)}) collective-permute-start(f32[256,256]{1,0:T(8,128)S(1)} %get-tuple-element.16), channel_id=1, source_target_pairs={{0,32},{1,33},{2,34},{3,35},{4,36},{5,37},{6,38},{7,39},{8,40},{9,... | collective-permute-start | bytes 786440 | tf_op jit(solution)/shard_map/ppermute | solution.py:49
  70.1 27.9 %collective-permute-start.15 = (f32[256,256]{1,0:T(8,128)S(1)}, f32[256,256]{1,0:T(8,128)S(1)}, u32[]{:S(2)}, u32[]{:S(2)}) collective-permute-start(f32[256,256]{1,0:T(8,128)S(1)} %get-tuple-element.16), channel_id=1, source_target_pairs={{0,16},{1,17},{2,18},{3,19},{4,20},{5,21},{6,22},{7,23},{8,24},{9,... | collective-permute-start | bytes 786440 | tf_op jit(solution)/shard_map/ppermute | solution.py:49
  72.1 75.9 %collective-permute-start.28 = (f32[256,768]{1,0:T(8,128)S(1)}, f32[256,768]{1,0:T(8,128)S(1)}, u32[]{:S(2)}, u32[]{:S(2)}) collective-permute-start(f32[256,768]{1,0:T(8,128)S(1)} %fusion.7), channel_id=1, source_target_pairs={{16,0},{17,1},{18,2},{19,3},{20,4},{21,5},{22,6},{23,7},{24,8},{25... | collective-permute-start | bytes 2359304 | tf_op jit(solution)/shard_map/ppermute | solution.py:49
  85.3 64.9 %collective-permute-start.27 = (f32[256,768]{1,0:T(8,128)S(1)}, f32[256,768]{1,0:T(8,128)S(1)}, u32[]{:S(2)}, u32[]{:S(2)}) collective-permute-start(f32[256,768]{1,0:T(8,128)S(1)} %fusion.7), channel_id=1, source_target_pairs={{16,112},{17,113},{18,114},{19,115},{20,116},{21,117},{22,118},{23... | collective-permute-start | bytes 2359304 | tf_op jit(solution)/shard_map/ppermute | solution.py:49
  93.6 61.1 %collective-permute-start.26 = (f32[256,768]{1,0:T(8,128)S(1)}, f32[256,768]{1,0:T(8,128)}, u32[]{:S(2)}, u32[]{:S(2)}) collective-permute-start(f32[256,768]{1,0:T(8,128)S(1)} %fusion.7), channel_id=1, source_target_pairs={{16,96},{17,97},{18,98},{19,99},{20,100},{21,101},{22,102},{23,103... | collective-permute-start | bytes 2359304 | tf_op jit(solution)/shard_map/ppermute | solution.py:49
  95.8 58.9 %collective-permute-start.25 = (f32[256,768]{1,0:T(8,128)S(1)}, f32[256,768]{1,0:T(8,128)}, u32[]{:S(2)}, u32[]{:S(2)}) collective-permute-start(f32[256,768]{1,0:T(8,128)S(1)} %fusion.7), channel_id=1, source_target_pairs={{16,80},{17,81},{18,82},{19,83},{20,84},{21,85},{22,86},{23,87},{2... | collective-permute-start | bytes 2359304 | tf_op jit(solution)/shard_map/ppermute | solution.py:49
  98.0 56.7 %collective-permute-start.24 = (f32[256,768]{1,0:T(8,128)S(1)}, f32[256,768]{1,0:T(8,128)}, u32[]{:S(2)}, u32[]{:S(2)}) collective-permute-start(f32[256,768]{1,0:T(8,128)S(1)} %fusion.7), channel_id=1, source_target_pairs={{16,64},{17,65},{18,66},{19,67},{20,68},{21,69},{22,70},{23,71},{2... | collective-permute-start | bytes 2359304 | tf_op jit(solution)/shard_map/ppermute | solution.py:49
  148.0 10.8 %collective-permute-start.23 = (f32[256,768]{1,0:T(8,128)S(1)}, f32[256,768]{1,0:T(8,128)}, u32[]{:S(2)}, u32[]{:S(2)}) collective-permute-start(f32[256,768]{1,0:T(8,128)S(1)} %fusion.7), channel_id=1, source_target_pairs={{16,48},{17,49},{18,50},{19,51},{20,52},{21,53},{22,54},{23,55},{2... | collective-permute-start | bytes 2359304 | tf_op jit(solution)/shard_map/ppermute | solution.py:49
  150.2 18.8 %collective-permute-start.22 = (f32[256,768]{1,0:T(8,128)S(1)}, f32[256,768]{1,0:T(8,128)}, u32[]{:S(2)}, u32[]{:S(2)}) collective-permute-start(f32[256,768]{1,0:T(8,128)S(1)} %fusion.7), channel_id=1, source_target_pairs={{16,32},{17,33},{18,34},{19,35},{20,36},{21,37},{22,38},{23,39},{2... | collective-permute-start | bytes 2359304 | tf_op jit(solution)/shard_map/ppermute | solution.py:49
  196.9 0.9 copy-start.2
  198.2 27.6 %copy-start.3 = (f32[256,768]{1,0:T(8,128)S(1)}, f32[256,768]{1,0:T(8,128)}, u32[]{:S(2)}) copy-start(f32[256,768]{1,0:T(8,128)} %copy-done.2) | copy-start | bytes 2359300
  222.6 56.6 %copy-start.7 = (f32[128,128]{1,0:T(8,128)}, f32[128,128]{1,0:T(8,128)S(1)}, u32[]{:S(2)}) copy-start(f32[128,128]{1,0:T(8,128)S(1)} %convolution_negate_fusion.4) | copy-start | bytes 196612
  222.7 4.3 %copy-start.10 = (f32[128,128]{1,0:T(8,128)}, f32[128,128]{1,0:T(8,128)S(1)}, u32[]{:S(2)}) copy-start(f32[128,128]{1,0:T(8,128)S(1)} %copy.14) | copy-start | bytes 196612
  252.6 26.6 %copy-start.13 = (f32[128,128]{1,0:T(8,128)}, f32[128,128]{1,0:T(8,128)S(1)}, u32[]{:S(2)}) copy-start(f32[128,128]{1,0:T(8,128)S(1)} %fusion.34) | copy-start | bytes 196612
  278.4 0.7 copy-start.21
  279.2 1.1 copy-start.14
  279.2 1.4 copy-start.22
  279.2 1.7 copy-start.8
  279.2 4.4 %copy-start.11 = (f32[128,128]{1,0:T(8,128)S(1)}, f32[128,128]{1,0:T(8,128)}, u32[]{:S(2)}) copy-start(f32[128,128]{1,0:T(8,128)} %copy-done.10) | copy-start | bytes 196612
  279.2 4.8 %copy-start.5 = (f32[128,256]{1,0:T(8,128)S(1)}, f32[128,256]{1,0:T(8,128)}, u32[]{:S(2)}) copy-start(f32[128,256]{1,0:T(8,128)} %concatenate.94) | copy-start | bytes 393220
  279.2 4.8 %copy-start.19 = (f32[128,128]{1,0:T(8,128)S(1)}, f32[128,128]{1,0:T(8,128)}, u32[]{:S(2)}) copy-start(f32[128,128]{1,0:T(8,128)} %copy.21) | copy-start | bytes 196612
  283.0 4.0 %copy-start.6 = (f32[128,256]{1,0:T(8,128)S(1)}, f32[128,256]{1,0:T(8,128)}, u32[]{:S(2)}) copy-start(f32[128,256]{1,0:T(8,128)} %concatenate.94) | copy-start | bytes 393220
  283.0 4.0 %copy-start.9 = (f32[128,128]{1,0:T(8,128)S(1)}, f32[128,128]{1,0:T(8,128)}, u32[]{:S(2)}) copy-start(f32[128,128]{1,0:T(8,128)} %copy-done.7) | copy-start | bytes 196612
  283.0 3.9 %copy-start.12 = (f32[128,128]{1,0:T(8,128)S(1)}, f32[128,128]{1,0:T(8,128)}, u32[]{:S(2)}) copy-start(f32[128,128]{1,0:T(8,128)} %copy-done.10) | copy-start | bytes 196612
  283.6 3.3 copy-start.20
  286.1 0.8 copy-start.28
  305.1 18.9 %copy-start.15 = (f32[256,256]{1,0:T(8,128)S(1)}, f32[256,256]{1,0:T(8,128)}, u32[]{:S(2)}) copy-start(f32[256,256]{1,0:T(8,128)} %select_maximum_fusion) | copy-start | bytes 786436
  305.1 18.9 %copy-start.23 = (f32[128,128]{1,0:T(8,128)S(1)}, f32[128,128]{1,0:T(8,128)}, u32[]{:S(2)}) copy-start(f32[128,128]{1,0:T(8,128)} %get-tuple-element.9) | copy-start | bytes 196612
  305.1 18.9 %copy-start.24 = (f32[128,128]{1,0:T(8,128)S(1)}, f32[128,128]{1,0:T(8,128)}, u32[]{:S(2)}) copy-start(f32[128,128]{1,0:T(8,128)} %get-tuple-element.7) | copy-start | bytes 196612
  305.1 18.9 %copy-start.16 = (f32[256,256]{1,0:T(8,128)S(1)}, f32[256,256]{1,0:T(8,128)}, u32[]{:S(2)}) copy-start(f32[256,256]{1,0:T(8,128)} %copy.26) | copy-start | bytes 786436
  305.1 18.9 %copy-start.17 = (f32[256,256]{1,0:T(8,128)S(1)}, f32[256,256]{1,0:T(8,128)}, u32[]{:S(2)}) copy-start(f32[256,256]{1,0:T(8,128)} %copy.28) | copy-start | bytes 786436
  305.1 18.9 %copy-start.18 = (f32[256,256]{1,0:T(8,128)S(1)}, f32[256,256]{1,0:T(8,128)}, u32[]{:S(2)}) copy-start(f32[256,256]{1,0:T(8,128)} %copy.29) | copy-start | bytes 786436
  305.2 18.9 %copy-start.25 = (f32[128,128]{1,0:T(8,128)S(1)}, f32[128,128]{1,0:T(8,128)}, u32[]{:S(2)}) copy-start(f32[128,128]{1,0:T(8,128)} %get-tuple-element.5) | copy-start | bytes 196612
  305.2 18.9 %copy-start.26 = (f32[128,128]{1,0:T(8,128)S(1)}, f32[128,128]{1,0:T(8,128)}, u32[]{:S(2)}) copy-start(f32[128,128]{1,0:T(8,128)} %copy.25) | copy-start | bytes 196612
  305.2 18.9 %copy-start.27 = (f32[128,128]{1,0:T(8,128)S(1)}, f32[128,128]{1,0:T(8,128)}, u32[]{:S(2)}) copy-start(f32[128,128]{1,0:T(8,128)} %copy.27) | copy-start | bytes 196612
  323.9 2.6 copy-start.4
  326.6 25.4 %copy-start.1 = (f32[2048,768]{1,0:T(8,128)}, f32[2048,768]{1,0:T(8,128)S(1)}, u32[]{:S(2)}) copy-start(f32[2048,768]{1,0:T(8,128)S(1)} %fusion.15) | copy-start | bytes 18874372
Sparse Core Ops, SparseCore 0:
  10.9 71.1 all-reduce.13
  86.1 148.7 all-reduce.11

commit v5 on v4

--- a/solution.py
+++ b/solution.py
@@ -127,6 +127,18 @@
     return factor, inverse
 
 
+def apply_inverse(band, inverse, axis):
+    parts = []
+    for j in range(STEPS):
+        hi = (j + 1) * BLOCK
+        piece = lax.slice_in_dim(band, 0, hi, axis=axis)
+        parts.append(lax.dot_general(
+            piece, inverse[j * BLOCK:hi, :hi], (((axis,), (1,)), ((), ())),
+            precision=lax.Precision.HIGHEST, preferred_element_type=jnp.float32,
+        ))
+    return jnp.concatenate(parts, axis=1)
+
+
 def shards(kernel):
     row_count = lax.axis_size("row")
     col_count = lax.axis_size("col")
@@ -142,14 +154,8 @@
     band_rows = gather_rows(kernel, row_index)
 
     factor, inverse = factor_corner(blocks)
-    panels = lax.dot_general(
-        band_cols, inverse, (((1,), (1,)), ((), ())),
-        precision=lax.Precision.HIGHEST, preferred_element_type=jnp.float32,
-    )
-    across = lax.dot_general(
-        band_rows, inverse, (((0,), (1,)), ((), ())),
-        precision=lax.Precision.HIGHEST, preferred_element_type=jnp.float32,
-    )
+    panels = apply_inverse(band_cols, inverse, 1)
+    across = apply_inverse(band_rows, inverse, 0)
     own = lax.dynamic_slice_in_dim(factor, jnp.minimum(row_index, STEPS - 1) * BLOCK, BLOCK, 0)
     head = jnp.where(row_index < STEPS, own, panels[:BLOCK])
     panels = lax.dynamic_update_slice(panels, head, (0, 0))

time: 365 us -> 356 us (0.975)
  matrix products: 76 us -> 66.9 us
    dot_general x2 -> x6, matrix products: 36.9 us -> 31.5 us  [apply_inverse(): lax.dot_general(piece, inverse[j * BLOCK:hi, :hi], (((axis,), (1,)), ((),...]
where the time goes in v5:
time: 356 us; the launch traced here: 350 us
  other arithmetic  160 us (45%)
  matrix products  66.9 us (19%)
  starting transfers between devices  49.4 us (14%)
  waiting for transfers between devices  45.1 us (13%)
  between operations  16 us (4%)
  local copies, waits for them, and re-layouts  12.5 us (4%)
    ppermute x14, starting transfers between devices, gather_corner(): down.append(lax.ppermute(mine, ('row', 'col'), pairs))  37.4 us
    another operation x9, other arithmetic, factor_block(): bottom = jnp.linalg.cholesky(schur[half:, half:] - mul(side, side, True))  37.4 us
    another operation x9, other arithmetic, factor_block(): top = jnp.linalg.cholesky(schur[:half, :half])  37.3 us
    another operation x6, other arithmetic, factor_block(): bottom_inv = jax.scipy.linalg.solve_triangular(bottom, eye, lower=True)  32.8 us
    another operation x6, other arithmetic, factor_block(): top_inv = jax.scipy.linalg.solve_triangular(top, eye, lower=True)  32.7 us
    dot_general x6, matrix products, apply_inverse(): lax.dot_general(piece, inverse[j * BLOCK:hi, :hi], (((axis,), (1,)), ((),...  31.5 us
    ppermute x15, waiting for transfers between devices, gather_corner(): heard.append(lax.ppermute(piece, ('row', 'col'), pairs))  29.8 us
    dot_general x1, matrix products, shards(): lax.dot_general(panels, across, (((1,), (1,)), ((), ())), precision=lax.P...  23.3 us
  transfers between devices with their start and end apart: 31, of which 5 were waited for; matrix products, arithmetic and copies ran while one was open for 55% of the time, Pallas kernels for 0%

profile of v5, /device:TPU:10, one launch (start us, length us, event | category | flops | bytes accessed | tf_op | source)
XLA Modules:
  0.0 350.1 jit_solution(18383521649298828818)
XLA Ops:
  7.6 1.3 select_dynamic-update-slice_fusion.1
  8.9 1.7 copy-done.3
  10.7 1.0 slice.80
  13.7 0.7 collective-permute-start.11
  14.4 0.7 collective-permute-start.10
  15.1 3.1 broadcast_in_dim.151
  18.2 3.0 select_dynamic-update-slice_fusion
  21.8 0.7 collective-permute-start.9
  25.3 1.0 fusion.9
  27.0 1.3 collective-permute-start.3
  28.3 1.3 collective-permute-start.2
  29.6 1.3 collective-permute-start.1
  31.6 1.3 iota_compare_fusion
  32.9 22.8 %collective-permute-done.3 = f32[256,256]{1,0:T(8,128)S(1)} collective-permute-done((f32[256,256]{1,0:T(8,128)S(1)}, f32[256,256]{1,0:T(8,128)S(1)}, u32[]{:S(2)}, u32[]{:S(2)}) %collective-permute-start.3) | collective-permute-done | bytes 262176 | tf_op jit(solution)/shard_map/ppermute | solution.py:29
  55.7 3.7 %collective-permute-done.2 = f32[256,256]{1,0:T(8,128)S(1)} collective-permute-done((f32[256,256]{1,0:T(8,128)S(1)}, f32[256,256]{1,0:T(8,128)S(1)}, u32[]{:S(2)}, u32[]{:S(2)}) %collective-permute-start.2) | collective-permute-done | bytes 262176 | tf_op jit(solution)/shard_map/ppermute | solution.py:29
  59.4 3.3 collective-permute-done.1
  62.7 1.3 broadcast_select_fusion
  67.4 1.3 select_add_fusion.3
  68.7 1.3 collective-permute-start.16
  70.7 1.3 select_add_fusion.2
  72.1 13.1 %collective-permute-start.28 = (f32[256,768]{1,0:T(8,128)S(1)}, f32[256,768]{1,0:T(8,128)S(1)}, u32[]{:S(2)}, u32[]{:S(2)}) collective-permute-start(f32[256,768]{1,0:T(8,128)S(1)} %fusion.18), channel_id=1, source_target_pairs={{16,0},{17,1},{18,2},{19,3},{20,4},{21,5},{22,6},{23,7},{24,8},{25... | collective-permute-start | bytes 2359304 | tf_op jit(solution)/shard_map/ppermute | solution.py:49
  85.2 8.1 %collective-permute-start.27 = (f32[256,768]{1,0:T(8,128)S(1)}, f32[256,768]{1,0:T(8,128)S(1)}, u32[]{:S(2)}, u32[]{:S(2)}) collective-permute-start(f32[256,768]{1,0:T(8,128)S(1)} %fusion.18), channel_id=1, source_target_pairs={{16,112},{17,113},{18,114},{19,115},{20,116},{21,117},{22,118},{23... | collective-permute-start | bytes 2359304 | tf_op jit(solution)/shard_map/ppermute | solution.py:49
  93.4 2.2 collective-permute-start.26
  95.6 2.2 collective-permute-start.25
  97.7 2.3 collective-permute-start.24
  100.4 11.7 %cholesky.104 = f32[128,128]{1,0:T(8,128)S(1)} custom-call(f32[128,128]{1,0:T(8,128)S(1)} %copy.4), custom_call_target="Cholesky" | custom-call | tf_op jit(solution)/shard_map/jit(cholesky)/cholesky | solution.py:82
  113.5 9.8 %custom-call.10 = f32[1,128,128]{1,2,0:T(8,128)S(1)} custom-call(f32[1,128,128]{2,1,0:T(8,128)S(1)} %get-tuple-element.14), custom_call_target="InvertDiagBlocksLowerTriangular" | custom-call | tf_op jit(solution)/shard_map/jit(_solve_triangular)/triangular_solve | solution.py:83
  124.5 11.7 %cholesky.115 = f32[128,128]{1,0:T(8,128)S(1)} custom-call(f32[128,128]{1,0:T(8,128)S(1)} %copy.6), custom_call_target="Cholesky" | custom-call | tf_op jit(solution)/shard_map/jit(cholesky)/cholesky | solution.py:85
  137.5 10.2 %custom-call.11 = f32[1,128,128]{1,2,0:T(8,128)S(1)} custom-call(f32[1,128,128]{2,1,0:T(8,128)S(1)} %get-tuple-element.12), custom_call_target="InvertDiagBlocksLowerTriangular" | custom-call | tf_op jit(solution)/shard_map/jit(_solve_triangular)/triangular_solve | solution.py:86
  147.7 2.2 collective-permute-start.23
  149.9 1.9 collective-permute-start.22
  152.2 0.7 select_maximum_fusion
  153.5 5.0 %collective-permute-done.23 = f32[256,768]{1,0:T(8,128)} collective-permute-done((f32[256,768]{1,0:T(8,128)S(1)}, f32[256,768]{1,0:T(8,128)}, u32[]{:S(2)}, u32[]{:S(2)}) %collective-permute-start.23) | collective-permute-done | bytes 786464 | tf_op jit(solution)/shard_map/ppermute | solution.py:49
  158.5 10.3 %collective-permute-done.22 = f32[256,768]{1,0:T(8,128)} collective-permute-done((f32[256,768]{1,0:T(8,128)S(1)}, f32[256,768]{1,0:T(8,128)}, u32[]{:S(2)}, u32[]{:S(2)}) %collective-permute-start.22) | collective-permute-done | bytes 786464 | tf_op jit(solution)/shard_map/ppermute | solution.py:49
  168.8 1.5 select_add_fusion.1
  171.6 11.7 %cholesky.126 = f32[128,128]{1,0:T(8,128)S(1)} custom-call(f32[128,128]{1,0:T(8,128)S(1)} %copy.10), custom_call_target="Cholesky" | custom-call | tf_op jit(solution)/shard_map/jit(cholesky)/cholesky | solution.py:82
  183.9 1.2 select_bitcast_fusion.3
  185.1 9.8 %custom-call.12 = f32[1,128,128]{1,2,0:T(8,128)S(1)} custom-call(f32[1,128,128]{2,1,0:T(8,128)S(1)} %get-tuple-element.10), custom_call_target="InvertDiagBlocksLowerTriangular" | custom-call | tf_op jit(solution)/shard_map/jit(_solve_triangular)/triangular_solve | solution.py:83
  196.6 0.9 copy-done.9
  198.7 11.9 %cholesky.137 = f32[128,128]{1,0:T(8,128)S(1)} custom-call(f32[128,128]{1,0:T(8,128)S(1)} %copy.12), custom_call_target="Cholesky" | custom-call | tf_op jit(solution)/shard_map/jit(cholesky)/cholesky | solution.py:85
  211.2 1.2 select_bitcast_fusion.2
  212.4 9.8 %custom-call.13 = f32[1,128,128]{1,2,0:T(8,128)S(1)} custom-call(f32[1,128,128]{2,1,0:T(8,128)S(1)} %get-tuple-element.8), custom_call_target="InvertDiagBlocksLowerTriangular" | custom-call | tf_op jit(solution)/shard_map/jit(_solve_triangular)/triangular_solve | solution.py:86
  222.9 0.8 copy.29
  223.7 0.7 copy.28
  224.5 0.8 copy.31
  225.7 0.9 copy.32
  228.0 11.7 %cholesky.148 = f32[128,128]{1,0:T(8,128)S(1)} custom-call(f32[128,128]{1,0:T(8,128)S(1)} %copy.17), custom_call_target="Cholesky" | custom-call | tf_op jit(solution)/shard_map/jit(cholesky)/cholesky | solution.py:82
  239.8 0.7 compare_reduce_fusion.1
  240.5 1.3 select_bitcast_fusion.1
  241.8 10.0 %custom-call.14 = f32[1,128,128]{1,2,0:T(8,128)S(1)} custom-call(f32[1,128,128]{2,1,0:T(8,128)S(1)} %get-tuple-element.6), custom_call_target="InvertDiagBlocksLowerTriangular" | custom-call | tf_op jit(solution)/shard_map/jit(_solve_triangular)/triangular_solve | solution.py:83
  252.3 0.7 copy.30
  253.6 11.7 %cholesky.159 = f32[128,128]{1,0:T(8,128)S(1)} custom-call(f32[128,128]{1,0:T(8,128)S(1)} %copy.19), custom_call_target="Cholesky" | custom-call | tf_op jit(solution)/shard_map/jit(cholesky)/cholesky | solution.py:85
  266.0 1.2 select_bitcast_fusion
  267.2 9.8 %custom-call.15 = f32[1,128,128]{1,2,0:T(8,128)S(1)} custom-call(f32[1,128,128]{2,1,0:T(8,128)S(1)} %get-tuple-element.4), custom_call_target="InvertDiagBlocksLowerTriangular" | custom-call | tf_op jit(solution)/shard_map/jit(_solve_triangular)/triangular_solve | solution.py:86
  277.3 1.5 pad_select_fusion
  283.1 4.6 %fusion.14 = f32[1024,256]{1,0:T(8,128)} fusion(f32[768,1024]{1,0:T(8,128)} %all-reduce.13.cloned.1.call-done, f32[128,128]{1,0:T(8,128)S(1)} %fusion.55, f32[128,128]{1,0:T(8,128)S(1)} %copy.8, f32[128,128]{1,0:T(8,128)S(1)} %convolution_negate_fusion.5), kind=kOutput, calls=%fused_computation.42 | convolution fusion | flops 805568512 | bytes 2293760 | tf_op jit(solution)/shard_map/dot_general | solution.py:135
  287.7 6.0 %fusion.10 = f32[1024,256]{1,0:T(8,128)} fusion(f32[768,1024]{1,0:T(8,128)} %all-reduce.13.cloned.1.call-done, f32[128,128]{1,0:T(8,128)S(1)} %copy.14, f32[128,128]{1,0:T(8,128)S(1)} %convolution_negate_fusion.4, f32[128,256]{1,0:T(8,128)S(1)} %concatenate.91, f32[256,256]{1,0:T(8,128)S(1)} %convolution_negate_fusion.2), kind=kOutput, calls=%fused_computation.29 | convolution fusion | flops 1611005952 | bytes 3670016 | tf_op jit(solution)/shard_map/dot_general | solution.py:135
  293.7 6.2 %fusion.37 = f32[1024,256]{1,0:T(8,128)} fusion(f32[768,1024]{1,0:T(8,128)S(1)} %copy-done.2, f32[128,128]{1,0:T(8,128)S(1)} %copy.21, f32[128,128]{1,0:T(8,128)S(1)} %convolution_negate_fusion.3, f32[128,256]{1,0:T(8,128)S(1)} %concatenate.95, f32[256,256]{1,0:T(8,128)S(1)} %convolution_negate_fusion, f32[256,256]{1,0:T(8,128)S(1)} %convolution_negate_fusion.1), kind=kOutput, calls=%fused_computation.78 | convolution fusion | flops 2416705536 | bytes 4980736 | tf_op jit(solution)/shard_map/dot_general | solution.py:135
  299.9 7.9 %fusion.38 = f32[2048,256]{1,0:T(8,128)S(1)} fusion(f32[2048,768]{1,0:T(8,128)} %all-reduce.11.cloned.1.call-done, f32[128,128]{1,0:T(8,128)S(1)} %copy.21, f32[128,128]{1,0:T(8,128)S(1)} %convolution_negate_fusion.3, f32[128,256]{1,0:T(8,128)S(1)} %concatenate.95, f32[256,256]{1,0:T(8,128)S(1)} %convolution_negate_fusion, ...), kind=kOutput, calls=%fused_computation.79 | convolution fusion | flops 4832624640 | bytes 9175040 | tf_op jit(solution)/shard_map/dot_general | solution.py:135
  307.8 3.7 %fusion = f32[2048,256]{1,0:T(8,128)S(1)} fusion(f32[2048,768]{1,0:T(8,128)S(1)} %copy-done, f32[128,128]{1,0:T(8,128)S(1)} %copy-done.14, f32[128,128]{1,0:T(8,128)S(1)} %copy-done.12, f32[128,256]{1,0:T(8,128)S(1)} %concatenate.91, f32[256,256]{1,0:T(8,128)S(1)} %convolution_negate_fusion.2), kind=kOutput, calls=%fused_computation.2 | convolution fusion | flops 3221618688 | bytes 6815744 | tf_op jit(solution)/shard_map/dot_general | solution.py:135
  311.5 3.2 fusion.12
  314.7 2.2 pad_maximum_fusion
  316.9 2.8 fusion.26
  319.8 23.3 %subtract_select_fusion = f32[2048,1024]{1,0:T(8,128)} fusion(f32[2048,1024]{1,0:T(8,128)S(1)} %bitcast.95, pred[1024]{0:T(1024)(128)(4,1)S(1)} %fusion.85, pred[2048]{0:T(1024)(128)(4,1)S(1)} %fusion.79, f32[2048,768]{1,0:T(8,128)S(1)} %fusion.26, f32[1024,256]{1,0:T(8,128)S(1)} %copy-done.5, f32[1024,256]{1,0:T(8,128)S(1)} %copy-done.4, ...), kind=kOutput, calls=%fused_computation | convolution fusion | flops 19335217152 | bytes 26217472 | tf_op jit(solution)/shard_map/dot_general | solution.py:162
  (163 shorter events, 29.9 us)
Async XLA Ops:
  7.2 275.9 %all-reduce.13.cloned.1.call-start = ((), (), s32[]{:S(2)}) async-start(), calls=%async_computation.1 | async-start | bytes 6291456 | tf_op jit(solution)/shard_map/psum | solution.py:71
  8.9 1.7 copy-start.3
  10.6 289.3 %all-reduce.11.cloned.1.call-start = ((), (), s32[]{:S(2)}) async-start(), calls=%async_computation | async-start | bytes 12582912 | tf_op jit(solution)/shard_map/psum | solution.py:62
  11.6 10.2 %collective-permute-start.14 = (f32[256,256]{1,0:T(8,128)S(1)}, f32[256,256]{1,0:T(8,128)S(1)}, u32[]{:S(2)}, u32[]{:S(2)}) collective-permute-start(f32[256,256]{1,0:T(8,128)S(1)} %slice.80), channel_id=1, source_target_pairs={{0,15},{16,31},{17,16},{32,47},{33,32},{34,33}} | collective-permute-start | bytes 786440 | tf_op jit(solution)/shard_map/ppermute | solution.py:29
  12.3 10.2 %collective-permute-start.13 = (f32[256,256]{1,0:T(8,128)S(1)}, f32[256,256]{1,0:T(8,128)S(1)}, u32[]{:S(2)}, u32[]{:S(2)}) collective-permute-start(f32[256,256]{1,0:T(8,128)S(1)} %slice.80), channel_id=1, source_target_pairs={{0,14},{16,30},{17,31},{32,46},{33,47},{34,32}} | collective-permute-start | bytes 786440 | tf_op jit(solution)/shard_map/ppermute | solution.py:29
  13.0 10.2 %collective-permute-start.12 = (f32[256,256]{1,0:T(8,128)S(1)}, f32[256,256]{1,0:T(8,128)S(1)}, u32[]{:S(2)}, u32[]{:S(2)}) collective-permute-start(f32[256,256]{1,0:T(8,128)S(1)} %slice.80), channel_id=1, source_target_pairs={{0,13},{16,29},{17,30},{32,45},{33,46},{34,47}} | collective-permute-start | bytes 786440 | tf_op jit(solution)/shard_map/ppermute | solution.py:29
  13.7 10.2 %collective-permute-start.11 = (f32[256,256]{1,0:T(8,128)S(1)}, f32[256,256]{1,0:T(8,128)S(1)}, u32[]{:S(2)}, u32[]{:S(2)}) collective-permute-start(f32[256,256]{1,0:T(8,128)S(1)} %slice.80), channel_id=1, source_target_pairs={{0,12},{16,28},{17,29},{32,44},{33,45},{34,46}} | collective-permute-start | bytes 786440 | tf_op jit(solution)/shard_map/ppermute | solution.py:29
  14.4 10.2 %collective-permute-start.10 = (f32[256,256]{1,0:T(8,128)S(1)}, f32[256,256]{1,0:T(8,128)S(1)}, u32[]{:S(2)}, u32[]{:S(2)}) collective-permute-start(f32[256,256]{1,0:T(8,128)S(1)} %slice.80), channel_id=1, source_target_pairs={{0,11},{16,27},{17,28},{32,43},{33,44},{34,45}} | collective-permute-start | bytes 786440 | tf_op jit(solution)/shard_map/ppermute | solution.py:29
  21.8 4.5 %collective-permute-start.9 = (f32[256,256]{1,0:T(8,128)S(1)}, f32[256,256]{1,0:T(8,128)S(1)}, u32[]{:S(2)}, u32[]{:S(2)}) collective-permute-start(f32[256,256]{1,0:T(8,128)S(1)} %slice.80), channel_id=1, source_target_pairs={{0,10},{16,26},{17,27},{32,42},{33,43},{34,44}} | collective-permute-start | bytes 786440 | tf_op jit(solution)/shard_map/ppermute | solution.py:29
  22.5 4.5 %collective-permute-start.8 = (f32[256,256]{1,0:T(8,128)S(1)}, f32[256,256]{1,0:T(8,128)S(1)}, u32[]{:S(2)}, u32[]{:S(2)}) collective-permute-start(f32[256,256]{1,0:T(8,128)S(1)} %slice.80), channel_id=1, source_target_pairs={{0,9},{16,25},{17,26},{32,41},{33,42},{34,43}} | collective-permute-start | bytes 786440 | tf_op jit(solution)/shard_map/ppermute | solution.py:29
  23.2 5.1 %collective-permute-start.7 = (f32[256,256]{1,0:T(8,128)S(1)}, f32[256,256]{1,0:T(8,128)S(1)}, u32[]{:S(2)}, u32[]{:S(2)}) collective-permute-start(f32[256,256]{1,0:T(8,128)S(1)} %slice.80), channel_id=1, source_target_pairs={{0,8},{16,24},{17,25},{32,40},{33,41},{34,42}} | collective-permute-start | bytes 786440 | tf_op jit(solution)/shard_map/ppermute | solution.py:29
  23.9 5.7 %collective-permute-start.6 = (f32[256,256]{1,0:T(8,128)S(1)}, f32[256,256]{1,0:T(8,128)S(1)}, u32[]{:S(2)}, u32[]{:S(2)}) collective-permute-start(f32[256,256]{1,0:T(8,128)S(1)} %slice.80), channel_id=1, source_target_pairs={{0,7},{16,23},{17,24},{32,39},{33,40},{34,41}} | collective-permute-start | bytes 786440 | tf_op jit(solution)/shard_map/ppermute | solution.py:29
  24.6 6.3 %collective-permute-start.5 = (f32[256,256]{1,0:T(8,128)S(1)}, f32[256,256]{1,0:T(8,128)S(1)}, u32[]{:S(2)}, u32[]{:S(2)}) collective-permute-start(f32[256,256]{1,0:T(8,128)S(1)} %slice.80), channel_id=1, source_target_pairs={{0,6},{16,22},{17,23},{32,38},{33,39},{34,40}} | collective-permute-start | bytes 786440 | tf_op jit(solution)/shard_map/ppermute | solution.py:29
  26.3 6.6 %collective-permute-start.4 = (f32[256,256]{1,0:T(8,128)S(1)}, f32[256,256]{1,0:T(8,128)S(1)}, u32[]{:S(2)}, u32[]{:S(2)}) collective-permute-start(f32[256,256]{1,0:T(8,128)S(1)} %slice.80), channel_id=1, source_target_pairs={{0,5},{16,21},{17,22},{32,37},{33,38},{34,39}} | collective-permute-start | bytes 786440 | tf_op jit(solution)/shard_map/ppermute | solution.py:29
  27.0 28.8 %collective-permute-start.3 = (f32[256,256]{1,0:T(8,128)S(1)}, f32[256,256]{1,0:T(8,128)S(1)}, u32[]{:S(2)}, u32[]{:S(2)}) collective-permute-start(f32[256,256]{1,0:T(8,128)S(1)} %slice.80), channel_id=1, source_target_pairs={{0,4},{16,20},{17,21},{32,36},{33,37},{34,38}} | collective-permute-start | bytes 786440 | tf_op jit(solution)/shard_map/ppermute | solution.py:29
  28.3 31.1 %collective-permute-start.2 = (f32[256,256]{1,0:T(8,128)S(1)}, f32[256,256]{1,0:T(8,128)S(1)}, u32[]{:S(2)}, u32[]{:S(2)}) collective-permute-start(f32[256,256]{1,0:T(8,128)S(1)} %slice.80), channel_id=1, source_target_pairs={{0,3},{16,19},{17,20},{32,35},{33,36},{34,37}} | collective-permute-start | bytes 786440 | tf_op jit(solution)/shard_map/ppermute | solution.py:29
  29.6 33.1 %collective-permute-start.1 = (f32[256,256]{1,0:T(8,128)S(1)}, f32[256,256]{1,0:T(8,128)S(1)}, u32[]{:S(2)}, u32[]{:S(2)}) collective-permute-start(f32[256,256]{1,0:T(8,128)S(1)} %slice.80), channel_id=1, source_target_pairs={{0,2},{16,18},{17,19},{32,34},{33,35},{34,36}} | collective-permute-start | bytes 786440 | tf_op jit(solution)/shard_map/ppermute | solution.py:29
  30.9 31.8 %collective-permute-start = (f32[256,256]{1,0:T(8,128)S(1)}, f32[256,256]{1,0:T(8,128)S(1)}, u32[]{:S(2)}, u32[]{:S(2)}) collective-permute-start(f32[256,256]{1,0:T(8,128)S(1)} %slice.80), channel_id=1, source_target_pairs={{0,1},{16,17},{17,18},{32,33},{33,34},{34,35}} | collective-permute-start | bytes 786440 | tf_op jit(solution)/shard_map/ppermute | solution.py:29
  64.0 4.7 %collective-permute-start.21 = (f32[256,256]{1,0:T(8,128)S(1)}, f32[256,256]{1,0:T(8,128)S(1)}, u32[]{:S(2)}, u32[]{:S(2)}) collective-permute-start(f32[256,256]{1,0:T(8,128)S(1)} %get-tuple-element.16), channel_id=1, source_target_pairs={{0,112},{1,113},{2,114},{3,115},{4,116},{5,117},{6,118},{7,119},{8... | collective-permute-start | bytes 786440 | tf_op jit(solution)/shard_map/ppermute | solution.py:49
  64.7 5.3 %collective-permute-start.20 = (f32[256,256]{1,0:T(8,128)S(1)}, f32[256,256]{1,0:T(8,128)S(1)}, u32[]{:S(2)}, u32[]{:S(2)}) collective-permute-start(f32[256,256]{1,0:T(8,128)S(1)} %get-tuple-element.16), channel_id=1, source_target_pairs={{0,96},{1,97},{2,98},{3,99},{4,100},{5,101},{6,102},{7,103},{8,104... | collective-permute-start | bytes 786440 | tf_op jit(solution)/shard_map/ppermute | solution.py:49
  65.4 6.7 %collective-permute-start.19 = (f32[256,256]{1,0:T(8,128)S(1)}, f32[256,256]{1,0:T(8,128)S(1)}, u32[]{:S(2)}, u32[]{:S(2)}) collective-permute-start(f32[256,256]{1,0:T(8,128)S(1)} %get-tuple-element.16), channel_id=1, source_target_pairs={{0,80},{1,81},{2,82},{3,83},{4,84},{5,85},{6,86},{7,87},{8,88},{9,... | collective-permute-start | bytes 786440 | tf_op jit(solution)/shard_map/ppermute | solution.py:49
  66.1 19.2 %collective-permute-start.18 = (f32[256,256]{1,0:T(8,128)S(1)}, f32[256,256]{1,0:T(8,128)S(1)}, u32[]{:S(2)}, u32[]{:S(2)}) collective-permute-start(f32[256,256]{1,0:T(8,128)S(1)} %get-tuple-element.16), channel_id=1, source_target_pairs={{0,64},{1,65},{2,66},{3,67},{4,68},{5,69},{6,70},{7,71},{8,72},{9,... | collective-permute-start | bytes 786440 | tf_op jit(solution)/shard_map/ppermute | solution.py:49
  66.8 26.6 %collective-permute-start.17 = (f32[256,256]{1,0:T(8,128)S(1)}, f32[256,256]{1,0:T(8,128)S(1)}, u32[]{:S(2)}, u32[]{:S(2)}) collective-permute-start(f32[256,256]{1,0:T(8,128)S(1)} %get-tuple-element.16), channel_id=1, source_target_pairs={{0,48},{1,49},{2,50},{3,51},{4,52},{5,53},{6,54},{7,55},{8,56},{9,... | collective-permute-start | bytes 786440 | tf_op jit(solution)/shard_map/ppermute | solution.py:49
  68.7 26.9 %collective-permute-start.16 = (f32[256,256]{1,0:T(8,128)S(1)}, f32[256,256]{1,0:T(8,128)S(1)}, u32[]{:S(2)}, u32[]{:S(2)}) collective-permute-start(f32[256,256]{1,0:T(8,128)S(1)} %get-tuple-element.16), channel_id=1, source_target_pairs={{0,32},{1,33},{2,34},{3,35},{4,36},{5,37},{6,38},{7,39},{8,40},{9,... | collective-permute-start | bytes 786440 | tf_op jit(solution)/shard_map/ppermute | solution.py:49
  70.0 27.7 %collective-permute-start.15 = (f32[256,256]{1,0:T(8,128)S(1)}, f32[256,256]{1,0:T(8,128)S(1)}, u32[]{:S(2)}, u32[]{:S(2)}) collective-permute-start(f32[256,256]{1,0:T(8,128)S(1)} %get-tuple-element.16), channel_id=1, source_target_pairs={{0,16},{1,17},{2,18},{3,19},{4,20},{5,21},{6,22},{7,23},{8,24},{9,... | collective-permute-start | bytes 786440 | tf_op jit(solution)/shard_map/ppermute | solution.py:49
  72.1 75.6 %collective-permute-start.28 = (f32[256,768]{1,0:T(8,128)S(1)}, f32[256,768]{1,0:T(8,128)S(1)}, u32[]{:S(2)}, u32[]{:S(2)}) collective-permute-start(f32[256,768]{1,0:T(8,128)S(1)} %fusion.18), channel_id=1, source_target_pairs={{16,0},{17,1},{18,2},{19,3},{20,4},{21,5},{22,6},{23,7},{24,8},{25... | collective-permute-start | bytes 2359304 | tf_op jit(solution)/shard_map/ppermute | solution.py:49
  85.2 64.7 %collective-permute-start.27 = (f32[256,768]{1,0:T(8,128)S(1)}, f32[256,768]{1,0:T(8,128)S(1)}, u32[]{:S(2)}, u32[]{:S(2)}) collective-permute-start(f32[256,768]{1,0:T(8,128)S(1)} %fusion.18), channel_id=1, source_target_pairs={{16,112},{17,113},{18,114},{19,115},{20,116},{21,117},{22,118},{23... | collective-permute-start | bytes 2359304 | tf_op jit(solution)/shard_map/ppermute | solution.py:49
  93.4 60.1 %collective-permute-start.26 = (f32[256,768]{1,0:T(8,128)S(1)}, f32[256,768]{1,0:T(8,128)}, u32[]{:S(2)}, u32[]{:S(2)}) collective-permute-start(f32[256,768]{1,0:T(8,128)S(1)} %fusion.18), channel_id=1, source_target_pairs={{16,96},{17,97},{18,98},{19,99},{20,100},{21,101},{22,102},{23,103... | collective-permute-start | bytes 2359304 | tf_op jit(solution)/shard_map/ppermute | solution.py:49
  95.6 58.0 %collective-permute-start.25 = (f32[256,768]{1,0:T(8,128)S(1)}, f32[256,768]{1,0:T(8,128)}, u32[]{:S(2)}, u32[]{:S(2)}) collective-permute-start(f32[256,768]{1,0:T(8,128)S(1)} %fusion.18), channel_id=1, source_target_pairs={{16,80},{17,81},{18,82},{19,83},{20,84},{21,85},{22,86},{23,87},{2... | collective-permute-start | bytes 2359304 | tf_op jit(solution)/shard_map/ppermute | solution.py:49
  97.7 55.8 %collective-permute-start.24 = (f32[256,768]{1,0:T(8,128)S(1)}, f32[256,768]{1,0:T(8,128)}, u32[]{:S(2)}, u32[]{:S(2)}) collective-permute-start(f32[256,768]{1,0:T(8,128)S(1)} %fusion.18), channel_id=1, source_target_pairs={{16,64},{17,65},{18,66},{19,67},{20,68},{21,69},{22,70},{23,71},{2... | collective-permute-start | bytes 2359304 | tf_op jit(solution)/shard_map/ppermute | solution.py:49
  147.7 10.8 %collective-permute-start.23 = (f32[256,768]{1,0:T(8,128)S(1)}, f32[256,768]{1,0:T(8,128)}, u32[]{:S(2)}, u32[]{:S(2)}) collective-permute-start(f32[256,768]{1,0:T(8,128)S(1)} %fusion.18), channel_id=1, source_target_pairs={{16,48},{17,49},{18,50},{19,51},{20,52},{21,53},{22,54},{23,55},{2... | collective-permute-start | bytes 2359304 | tf_op jit(solution)/shard_map/ppermute | solution.py:49
  149.9 18.9 %collective-permute-start.22 = (f32[256,768]{1,0:T(8,128)S(1)}, f32[256,768]{1,0:T(8,128)}, u32[]{:S(2)}, u32[]{:S(2)}) collective-permute-start(f32[256,768]{1,0:T(8,128)S(1)} %fusion.18), channel_id=1, source_target_pairs={{16,32},{17,33},{18,34},{19,35},{20,36},{21,37},{22,38},{23,39},{2... | collective-permute-start | bytes 2359304 | tf_op jit(solution)/shard_map/ppermute | solution.py:49
  153.5 129.6 %copy-start.7 = (f32[128,128]{1,0:T(8,128)}, f32[128,128]{1,0:T(8,128)S(1)}, u32[]{:S(2)}) copy-start(f32[128,128]{1,0:T(8,128)S(1)} %convolution_negate_fusion.5) | copy-start | bytes 196612
  196.5 0.9 copy-start.9
  197.8 27.5 %copy-start.10 = (f32[256,768]{1,0:T(8,128)S(1)}, f32[256,768]{1,0:T(8,128)}, u32[]{:S(2)}) copy-start(f32[256,768]{1,0:T(8,128)} %copy-done.9) | copy-start | bytes 2359300
  222.8 64.9 %copy-start.11 = (f32[128,128]{1,0:T(8,128)}, f32[128,128]{1,0:T(8,128)S(1)}, u32[]{:S(2)}) copy-start(f32[128,128]{1,0:T(8,128)S(1)} %convolution_negate_fusion.4) | copy-start | bytes 196612
  222.9 64.8 %copy-start.13 = (f32[128,128]{1,0:T(8,128)}, f32[128,128]{1,0:T(8,128)S(1)}, u32[]{:S(2)}) copy-start(f32[128,128]{1,0:T(8,128)S(1)} %copy.14) | copy-start | bytes 196612
  225.3 52.0 %copy-start.17 = (f32[128,128]{1,0:T(8,128)S(1)}, f32[128,128]{1,0:T(8,128)}, u32[]{:S(2)}) copy-start(f32[128,128]{1,0:T(8,128)} %get-tuple-element.11) | copy-start | bytes 196612
  283.1 10.6 %copy-start.2 = (f32[768,1024]{1,0:T(8,128)S(1)}, f32[768,1024]{1,0:T(8,128)}, u32[]{:S(2)}) copy-start(f32[768,1024]{1,0:T(8,128)} %all-reduce.13.cloned.1.call-done) | copy-start | bytes 9437188
  299.9 7.9 %copy-start = (f32[2048,768]{1,0:T(8,128)S(1)}, f32[2048,768]{1,0:T(8,128)}, u32[]{:S(2)}) copy-start(f32[2048,768]{1,0:T(8,128)} %all-reduce.11.cloned.1.call-done) | copy-start | bytes 18874372
  299.9 7.9 %copy-start.12 = (f32[128,128]{1,0:T(8,128)S(1)}, f32[128,128]{1,0:T(8,128)}, u32[]{:S(2)}) copy-start(f32[128,128]{1,0:T(8,128)} %copy-done.11) | copy-start | bytes 196612
  299.9 7.9 %copy-start.14 = (f32[128,128]{1,0:T(8,128)S(1)}, f32[128,128]{1,0:T(8,128)}, u32[]{:S(2)}) copy-start(f32[128,128]{1,0:T(8,128)} %copy-done.13) | copy-start | bytes 196612
  307.8 3.7 %copy-start.8 = (f32[128,128]{1,0:T(8,128)S(1)}, f32[128,128]{1,0:T(8,128)}, u32[]{:S(2)}) copy-start(f32[128,128]{1,0:T(8,128)} %copy-done.7) | copy-start | bytes 196612
  311.5 8.2 %slice-start = ((s8[8388608]{0:T(1024)(128)(4,1)}), s8[4194304]{0:T(1024)(128)(4,1)S(1)}, s32[]{:S(2)}) async-start(s8[8388608]{0:T(1024)(128)(4,1)} %bitcast.94), calls=%async_computation.2 | async-start | bytes 8388608
  314.7 2.2 copy-start.15
  314.7 2.2 copy-start.16
  314.7 5.0 %slice-start.1 = ((s8[8388608]{0:T(1024)(128)(4,1)}), s8[4194304]{0:T(1024)(128)(4,1)S(1)}, s32[]{:S(2)}) async-start(s8[8388608]{0:T(1024)(128)(4,1)} %bitcast.94), calls=%async_computation.3 | async-start | bytes 8388608
  316.8 2.9 copy-start.4
  316.9 2.9 copy-start.5
  316.9 2.9 copy-start.6
  319.7 23.3 %copy-start.1 = (f32[2048,768]{1,0:T(8,128)}, f32[2048,768]{1,0:T(8,128)S(1)}, u32[]{:S(2)}) copy-start(f32[2048,768]{1,0:T(8,128)S(1)} %fusion.26) | copy-start | bytes 18874372
Sparse Core Ops, SparseCore 0:
  10.9 70.9 all-reduce.12
  85.9 148.7 all-reduce.10
